TPU v7x, 256 devices: a whole 4x4x8 slice. The times are simulated.
256 devices in a mesh: dp: 32 (over x, y, core), shard: 8 (over z).
Axes of the slice: x: 4, y: 4, z: 8, core: 2. Of those that a mesh axis runs over, the one named last changes fastest.
Arguments:
- audio: bfloat16 [65536, 512], P(('dp', 'shard')), may hold values from -6 to 6
- cotangent: bfloat16 [65536, 512], P(('dp', 'shard')), may hold values from -6 to 6
- clip_lengths: int32 [256, 8], P(('dp', 'shard')), may hold values from 1 to 128, 256 in all within a row
- conv_weight: bfloat16 [3584, 512], P('shard'), may hold values from -0.09375 to 0.09375
- mix_weight: bfloat16 [512, 512], P('shard'), may hold values from -0.25 to 0.25
- conv_bias: float32 [512], replicated, may hold values from -3 to 3
- alpha_in: float32 [512], replicated, may hold values from 0.5 to 3
- alpha_mid: float32 [512], replicated, may hold values from 0.5 to 3
Outputs:
- in_grad: bfloat16 [65536, 512], P(('dp', 'shard'))
- conv_grad: float32 [3584, 512], P(('dp', 'shard'))
- mix_grad: float32 [512, 512], P(('dp', 'shard'))
- vector_grad: float32 [4, 512], P(None, ('dp', 'shard'))
Inputs may be any that keep to these rules, and one draw needn't show every extreme that they name: `clip_lengths`: each device's clip lengths sum to 256; the largest on each device is 128.
All inputs are finite; a program needn't handle non-finite values.
Results may differ from a plain program's by a relative error of at most 0.01.
Values may be sent and summed in bfloat16 or wider, within the bound.
No kernel may reach another device: no remote copies, remote signals or barrier semaphores. Data moves between devices by JAX's collectives and lax.ppermute only.
A program may use at most 64 MiB of HBM per device.

v0:
```python
import jax
import jax.numpy as jnp
from jax import lax
from jax.sharding import PartitionSpec as P

C = 512
TAPS = 7
DILATION_SIZE = 9


def shift_rows(block, tap_offset, fill):
    rows = block.shape[0]
    shift_amount = min(abs(tap_offset), rows)
    if shift_amount == 0:
        return block
    edge_padding = jnp.full((shift_amount,) + block.shape[1:], fill, block.dtype)
    if tap_offset > 0:
        return jnp.concatenate([block[shift_amount:], edge_padding], axis=0)
    return jnp.concatenate([edge_padding, block[: rows - shift_amount]], axis=0)


def clip_masks(lengths_row, rows):
    clip_ends = jnp.cumsum(lengths_row)
    position = jnp.arange(rows, dtype=jnp.int32)
    clip_id = jnp.sum((position[:, None] >= clip_ends[None, :]).astype(jnp.int32), axis=1)
    result = []
    for kernel_tap_index in range(TAPS):
        tap_offset = (kernel_tap_index - 3) * DILATION_SIZE
        result.append(shift_rows(clip_id, tap_offset, -1) == clip_id)
    return result


def snake_parts(value, alpha):
    sine = jnp.sin(alpha * value)
    double = jnp.sin(2.0 * alpha * value)
    return (
        value + sine * sine / alpha,
        1.0 + double,
        value * double / alpha - sine * sine / (alpha * alpha),
    )


def per_device(
    audio, cotangent, clip_lengths, conv_weight, mix_weight, conv_bias, alpha_in, alpha_mid
):
    rows = audio.shape[0]
    same_clip_flags = clip_masks(clip_lengths[0], rows)
    mix_full = lax.all_gather(mix_weight, "shard", axis=0, tiled=True)
    audio_f = audio.astype(jnp.float32)
    act_in, slope_in, dalpha_in = snake_parts(audio_f, alpha_in)
    first = act_in.astype(jnp.bfloat16)
    columns = []
    for kernel_tap_index in range(TAPS):
        tap_offset = (kernel_tap_index - 3) * DILATION_SIZE
        moved = shift_rows(first, tap_offset, 0)
        columns.append(
            jnp.where(same_clip_flags[kernel_tap_index][:, None], moved, jnp.zeros_like(moved))
        )
    unfolded = jnp.concatenate(columns, axis=1)
    product = jnp.dot(
        unfolded,
        lax.all_gather(conv_weight, "shard", axis=0, tiled=True),
        preferred_element_type=jnp.float32,
    )
    pre = product + conv_bias
    act_mid, slope_mid, dalpha_mid = snake_parts(pre, alpha_mid)
    second = act_mid.astype(jnp.bfloat16)
    mix_term = lax.dot_general(
        second, cotangent, (((0,), (0,)), ((), ())), preferred_element_type=jnp.float32
    )
    second_gradient = lax.dot_general(
        cotangent, mix_full, (((1,), (1,)), ((), ())), preferred_element_type=jnp.float32
    )
    d_pre = (second_gradient * slope_mid).astype(jnp.bfloat16)
    convolution_part = lax.dot_general(
        unfolded, d_pre, (((0,), (0,)), ((), ())), preferred_element_type=jnp.float32
    )
    d_unf = lax.dot_general(
        d_pre,
        lax.all_gather(conv_weight, "shard", axis=0, tiled=True),
        (((1,), (1,)), ((), ())),
        preferred_element_type=jnp.float32,
    ).astype(jnp.bfloat16)
    d_first = jnp.zeros((rows, C), jnp.float32)
    for kernel_tap_index in range(TAPS):
        tap_offset = (kernel_tap_index - 3) * DILATION_SIZE
        piece = d_unf[:, kernel_tap_index * C : (kernel_tap_index + 1) * C].astype(jnp.float32)
        piece = jnp.where(same_clip_flags[kernel_tap_index][:, None], piece, jnp.zeros_like(piece))
        d_first = d_first + shift_rows(piece, -tap_offset, 0.0)
    in_grad = (cotangent.astype(jnp.float32) + d_first * slope_in).astype(jnp.bfloat16)
    vectors = jnp.stack(
        [
            jnp.sum(d_pre.astype(jnp.float32), axis=0),
            jnp.sum(cotangent.astype(jnp.float32), axis=0),
            jnp.sum(d_first * dalpha_in, axis=0),
            jnp.sum(second_gradient * dalpha_mid, axis=0),
        ]
    )
    conv_grad, mix_grad, vector_grad = (
        lax.psum_scatter(convolution_part, ("dp", "shard"), scatter_dimension=0, tiled=True),
        lax.psum_scatter(mix_term, ("dp", "shard"), scatter_dimension=0, tiled=True),
        lax.psum_scatter(vectors, ("dp", "shard"), scatter_dimension=1, tiled=True),
    )
    return (in_grad, conv_grad, mix_grad, vector_grad)


def solution(mesh):
    placed = (
        P(("dp", "shard"), None),
        P(("dp", "shard"), None),
        P(("dp", "shard"), None),
        P("shard", None),
        P("shard", None),
        P(),
        P(),
        P(),
    )
    return jax.shard_map(
        per_device,
        mesh=mesh,
        in_specs=placed,
        out_specs=(
            P(("dp", "shard"), None),
            P(("dp", "shard"), None),
            P(("dp", "shard"), None),
            P(None, ("dp", "shard")),
        ),
        check_vma=False,
    )
```

profile of v0, /device:TPU:32, one launch (start us, length us, event | category | flops | bytes accessed | tf_op | source)
XLA Modules:
  0.0 1034.5 jit_solution(11425878607155914596)
XLA Ops:
  10.8 29.8 %all_gather.7 = bf16[512,512]{1,0:T(8,128)(2,1)S(1)} all-gather(bf16[64,512]{1,0:T(8,128)(2,1)} %param.12), channel_id=1, replica_groups=mesh['dp'=32,'shard'=8] {'shard'}, dimensions={0}, use_global_device_ids=true | all-gather | bytes 589824 | tf_op jit(solution)/shard_map/all_gather | solution.py:48
  46.6 16.5 %all-gather.2.cloned.1.call-done = bf16[3584,512]{1,0:T(8,128)(2,1)} async-done(((bf16[448,512]{1,0:T(8,128)(2,1)}), bf16[3584,512]{1,0:T(8,128)(2,1)}) %all-gather.2.cloned.1.call-update) | async-done | bytes 3670032 | tf_op jit(solution)/shard_map/all_gather | solution.py:62
  63.0 3.1 convolution_add_fusion
  67.0 3.0 fusion.14
  70.0 4.9 convert_reduce_fusion.1
  75.0 4.1 fusion.23
  79.0 673.7 %fusion = f32[16,512]{1,0:T(8,128)S(1)} fusion(f32[3584,512]{1,0:T(8,128)} %fusion.23), kind=kCustom, calls=%all-reduce-scatter | all-reduce-scatter fusion | flops 2097153 | bytes 7372800
  758.0 3.2 convolution_convert_fusion
  768.3 22.9 %collective-permute-start.23 = (f32[16,512]{1,0:T(8,128)S(1)}, f32[16,512]{1,0:T(8,128)S(1)}, u32[]{:S(2)}, u32[]{:S(2)}) collective-permute-start(f32[16,512]{1,0:T(8,128)S(1)} %fusion), channel_id=1, source_target_pairs={{0,24},{1,25},{2,26},{3,27},{4,28},{5,29},{6,30},{7,31},{8,32},{9,... | collective-permute-start | bytes 98312
  793.8 17.2 %collective-permute-start.20 = (f32[16,512]{1,0:T(8,128)S(1)}, f32[16,512]{1,0:T(8,128)S(1)}, u32[]{:S(2)}, u32[]{:S(2)}) collective-permute-start(f32[16,512]{1,0:T(8,128)S(1)} %fusion), channel_id=1, source_target_pairs={{0,21},{1,22},{2,23},{3,24},{4,25},{5,26},{6,27},{7,28},{8,29},{9,... | collective-permute-start | bytes 98312
  811.1 3.5 collective-permute-start.19
  817.7 3.1 collective-permute-start.17
  820.8 3.7 collective-permute-start.16
  825.8 3.9 fusion.13
  831.3 4.1 collective-permute-start.13
  835.4 3.7 collective-permute-start.12
  839.2 3.3 collective-permute-start.11
  842.5 5.8 collective-permute-start.10
  860.0 5.5 collective-permute-start.5
  865.6 73.3 %all-reduce.20 = f32[4,512]{1,0:T(4,128)S(1)} all-reduce(f32[4,512]{1,0:T(4,128)S(1)} %pad_maximum_fusion), channel_id=4, replica_groups=mesh['dp'=32,'shard'=8] {'dp','shard'}, use_global_device_ids=true, to_apply=%region_8.9.clone | all-reduce | flops 2048 | bytes 16384
  941.4 4.0 collective-permute-start.3
  945.4 5.9 collective-permute-start.2
  960.1 3.8 concatenate.76
  964.6 61.7 %all-reduce.24.cloned.1.call-done = f32[512,512]{1,0:T(8,128)} async-done(((f32[512,512]{1,0:T(8,128)}), f32[512,512]{1,0:T(8,128)}) %all-reduce.24.cloned.1.call-update) | async-done | bytes 1048592
  (103 shorter events, 55.9 us)
Async XLA Ops:
  7.2 55.9 %all-gather.2.cloned.1.call-start = ((), (), s32[]{:S(2)}) async-start(), calls=%async_computation | async-start | bytes 4128768 | tf_op jit(solution)/shard_map/all_gather | solution.py:62
  7.9 1018.4 %all-reduce.24.cloned.1.call-start = ((), (), s32[]{:S(2)}) async-start(), calls=%async_computation.1 | async-start | bytes 2097152
  756.7 34.5 %collective-permute-start.27 = (f32[16,512]{1,0:T(8,128)S(1)}, f32[16,512]{1,0:T(8,128)S(1)}, u32[]{:S(2)}, u32[]{:S(2)}) collective-permute-start(f32[16,512]{1,0:T(8,128)S(1)} %fusion), channel_id=1, source_target_pairs={{0,28},{1,29},{2,30},{3,31},{4,32},{5,33},{6,34},{7,35},{8,36},{9,... | collective-permute-start | bytes 98312
  764.2 28.3 %collective-permute-start.26 = (f32[16,512]{1,0:T(8,128)S(1)}, f32[16,512]{1,0:T(8,128)S(1)}, u32[]{:S(2)}, u32[]{:S(2)}) collective-permute-start(f32[16,512]{1,0:T(8,128)S(1)} %fusion), channel_id=1, source_target_pairs={{0,27},{1,28},{2,29},{3,30},{4,31},{5,32},{6,33},{7,34},{8,35},{9,... | collective-permute-start | bytes 98312
  765.5 28.3 %collective-permute-start.25 = (f32[16,512]{1,0:T(8,128)S(1)}, f32[16,512]{1,0:T(8,128)S(1)}, u32[]{:S(2)}, u32[]{:S(2)}) collective-permute-start(f32[16,512]{1,0:T(8,128)S(1)} %fusion), channel_id=1, source_target_pairs={{0,26},{1,27},{2,28},{3,29},{4,30},{5,31},{6,32},{7,33},{8,34},{9,... | collective-permute-start | bytes 98312
  766.9 44.2 %collective-permute-start.24 = (f32[16,512]{1,0:T(8,128)S(1)}, f32[16,512]{1,0:T(8,128)S(1)}, u32[]{:S(2)}, u32[]{:S(2)}) collective-permute-start(f32[16,512]{1,0:T(8,128)S(1)} %fusion), channel_id=1, source_target_pairs={{0,25},{1,26},{2,27},{3,28},{4,29},{5,30},{6,31},{7,32},{8,33},{9,... | collective-permute-start | bytes 98312
  768.3 46.4 %collective-permute-start.23 = (f32[16,512]{1,0:T(8,128)S(1)}, f32[16,512]{1,0:T(8,128)S(1)}, u32[]{:S(2)}, u32[]{:S(2)}) collective-permute-start(f32[16,512]{1,0:T(8,128)S(1)} %fusion), channel_id=1, source_target_pairs={{0,24},{1,25},{2,26},{3,27},{4,28},{5,29},{6,30},{7,31},{8,32},{9,... | collective-permute-start | bytes 98312
  791.2 26.5 %collective-permute-start.22 = (f32[16,512]{1,0:T(8,128)S(1)}, f32[16,512]{1,0:T(8,128)S(1)}, u32[]{:S(2)}, u32[]{:S(2)}) collective-permute-start(f32[16,512]{1,0:T(8,128)S(1)} %fusion), channel_id=1, source_target_pairs={{0,23},{1,24},{2,25},{3,26},{4,27},{5,28},{6,29},{7,30},{8,31},{9,... | collective-permute-start | bytes 98312
  792.5 28.3 %collective-permute-start.21 = (f32[16,512]{1,0:T(8,128)S(1)}, f32[16,512]{1,0:T(8,128)S(1)}, u32[]{:S(2)}, u32[]{:S(2)}) collective-permute-start(f32[16,512]{1,0:T(8,128)S(1)} %fusion), channel_id=1, source_target_pairs={{0,22},{1,23},{2,24},{3,25},{4,26},{5,27},{6,28},{7,29},{8,30},{9,... | collective-permute-start | bytes 98312
  793.8 30.7 %collective-permute-start.20 = (f32[16,512]{1,0:T(8,128)S(1)}, f32[16,512]{1,0:T(8,128)S(1)}, u32[]{:S(2)}, u32[]{:S(2)}) collective-permute-start(f32[16,512]{1,0:T(8,128)S(1)} %fusion), channel_id=1, source_target_pairs={{0,21},{1,22},{2,23},{3,24},{4,25},{5,26},{6,27},{7,28},{8,29},{9,... | collective-permute-start | bytes 98312
  811.1 18.5 %collective-permute-start.19 = (f32[16,512]{1,0:T(8,128)S(1)}, f32[16,512]{1,0:T(8,128)S(1)}, u32[]{:S(2)}, u32[]{:S(2)}) collective-permute-start(f32[16,512]{1,0:T(8,128)S(1)} %fusion), channel_id=1, source_target_pairs={{0,20},{1,21},{2,22},{3,23},{4,24},{5,25},{6,26},{7,27},{8,28},{9,... | collective-permute-start | bytes 98312
  817.7 17.7 %collective-permute-start.17 = (f32[16,512]{1,0:T(8,128)S(1)}, f32[16,512]{1,0:T(8,128)S(1)}, u32[]{:S(2)}, u32[]{:S(2)}) collective-permute-start(f32[16,512]{1,0:T(8,128)S(1)} %fusion), channel_id=1, source_target_pairs={{0,18},{1,19},{2,20},{3,21},{4,22},{5,23},{6,24},{7,25},{8,26},{9,... | collective-permute-start | bytes 98312
  820.8 18.4 %collective-permute-start.16 = (f32[16,512]{1,0:T(8,128)S(1)}, f32[16,512]{1,0:T(8,128)S(1)}, u32[]{:S(2)}, u32[]{:S(2)}) collective-permute-start(f32[16,512]{1,0:T(8,128)S(1)} %fusion), channel_id=1, source_target_pairs={{0,17},{1,18},{2,19},{3,20},{4,21},{5,22},{6,23},{7,24},{8,25},{9,... | collective-permute-start | bytes 98312
  824.5 18.0 %collective-permute-start.15 = (f32[16,512]{1,0:T(8,128)S(1)}, f32[16,512]{1,0:T(8,128)S(1)}, u32[]{:S(2)}, u32[]{:S(2)}) collective-permute-start(f32[16,512]{1,0:T(8,128)S(1)} %fusion), channel_id=1, source_target_pairs={{0,16},{1,17},{2,18},{3,19},{4,20},{5,21},{6,22},{7,23},{8,24},{9,... | collective-permute-start | bytes 98312
  829.7 21.2 %collective-permute-start.14 = (f32[16,512]{1,0:T(8,128)S(1)}, f32[16,512]{1,0:T(8,128)S(1)}, u32[]{:S(2)}, u32[]{:S(2)}) collective-permute-start(f32[16,512]{1,0:T(8,128)S(1)} %fusion), channel_id=1, source_target_pairs={{0,15},{1,16},{2,17},{3,18},{4,19},{5,20},{6,21},{7,22},{8,23},{9,... | collective-permute-start | bytes 98312
  831.3 20.9 %collective-permute-start.13 = (f32[16,512]{1,0:T(8,128)S(1)}, f32[16,512]{1,0:T(8,128)S(1)}, u32[]{:S(2)}, u32[]{:S(2)}) collective-permute-start(f32[16,512]{1,0:T(8,128)S(1)} %fusion), channel_id=1, source_target_pairs={{0,14},{1,15},{2,16},{3,17},{4,18},{5,19},{6,20},{7,21},{8,22},{9,... | collective-permute-start | bytes 98312
  835.4 18.8 %collective-permute-start.12 = (f32[16,512]{1,0:T(8,128)S(1)}, f32[16,512]{1,0:T(8,128)S(1)}, u32[]{:S(2)}, u32[]{:S(2)}) collective-permute-start(f32[16,512]{1,0:T(8,128)S(1)} %fusion), channel_id=1, source_target_pairs={{0,13},{1,14},{2,15},{3,16},{4,17},{5,18},{6,19},{7,20},{8,21},{9,... | collective-permute-start | bytes 98312
  839.2 17.8 %collective-permute-start.11 = (f32[16,512]{1,0:T(8,128)S(1)}, f32[16,512]{1,0:T(8,128)S(1)}, u32[]{:S(2)}, u32[]{:S(2)}) collective-permute-start(f32[16,512]{1,0:T(8,128)S(1)} %fusion), channel_id=1, source_target_pairs={{0,12},{1,13},{2,14},{3,15},{4,16},{5,17},{6,18},{7,19},{8,20},{9,... | collective-permute-start | bytes 98312
  850.9 87.9 %collective-permute-start.9 = (f32[16,512]{1,0:T(8,128)S(1)}, f32[16,512]{1,0:T(8,128)S(1)}, u32[]{:S(2)}, u32[]{:S(2)}) collective-permute-start(f32[16,512]{1,0:T(8,128)S(1)} %fusion), channel_id=1, source_target_pairs={{0,10},{1,11},{2,12},{3,13},{4,14},{5,15},{6,16},{7,17},{8,18},{9,... | collective-permute-start | bytes 98312
  852.2 89.2 %collective-permute-start.8 = (f32[16,512]{1,0:T(8,128)S(1)}, f32[16,512]{1,0:T(8,128)S(1)}, u32[]{:S(2)}, u32[]{:S(2)}) collective-permute-start(f32[16,512]{1,0:T(8,128)S(1)} %fusion), channel_id=1, source_target_pairs={{0,9},{1,10},{2,11},{3,12},{4,13},{5,14},{6,15},{7,16},{8,17},{9,1... | collective-permute-start | bytes 98312
  854.2 91.2 %collective-permute-start.7 = (f32[16,512]{1,0:T(8,128)S(1)}, f32[16,512]{1,0:T(8,128)S(1)}, u32[]{:S(2)}, u32[]{:S(2)}) collective-permute-start(f32[16,512]{1,0:T(8,128)S(1)} %fusion), channel_id=1, source_target_pairs={{0,8},{1,9},{2,10},{3,11},{4,12},{5,13},{6,14},{7,15},{8,16},{9,17... | collective-permute-start | bytes 98312
  857.0 94.2 %collective-permute-start.6 = (f32[16,512]{1,0:T(8,128)S(1)}, f32[16,512]{1,0:T(8,128)S(1)}, u32[]{:S(2)}, u32[]{:S(2)}) collective-permute-start(f32[16,512]{1,0:T(8,128)S(1)} %fusion), channel_id=1, source_target_pairs={{0,7},{1,8},{2,9},{3,10},{4,11},{5,12},{6,13},{7,14},{8,15},{9,16}... | collective-permute-start | bytes 98312
  860.0 94.3 %collective-permute-start.5 = (f32[16,512]{1,0:T(8,128)S(1)}, f32[16,512]{1,0:T(8,128)S(1)}, u32[]{:S(2)}, u32[]{:S(2)}) collective-permute-start(f32[16,512]{1,0:T(8,128)S(1)} %fusion), channel_id=1, source_target_pairs={{0,6},{1,7},{2,8},{3,9},{4,10},{5,11},{6,12},{7,13},{8,14},{9,15},... | collective-permute-start | bytes 98312
  938.8 18.7 %collective-permute-start.4 = (f32[16,512]{1,0:T(8,128)S(1)}, f32[16,512]{1,0:T(8,128)S(1)}, u32[]{:S(2)}, u32[]{:S(2)}) collective-permute-start(f32[16,512]{1,0:T(8,128)S(1)} %fusion), channel_id=1, source_target_pairs={{0,5},{1,6},{2,7},{3,8},{4,9},{5,10},{6,11},{7,12},{8,13},{9,14},{... | collective-permute-start | bytes 98312
  (16 other events, 178.5 us)
Sparse Core Ops, SparseCore 0:
  9.8 53.2 all-gather.1
  758.1 268.1 all-reduce.23
where the time goes:
time: 1040 us; the launch traced here: 1030 us
  blocking collectives  777 us (75%)
  starting transfers between devices  119 us (11%)
  waiting for transfers between devices  82.7 us (8%)
  matrix products  18.3 us (2%)
  between operations  14.8 us (1%)
  other arithmetic  14.6 us (1%)
    unnamed x2, blocking collectives  747 us
    unnamed x33, starting transfers between devices  119 us
    unnamed x35, waiting for transfers between devices  66.3 us
    all_gather x1, blocking collectives, per_device(): mix_full = lax.all_gather(mix_weight, 'shard', axis=0, tiled=True)  29.8 us
  transfers between devices with their start and end apart: 34, of which 4 were waited for; matrix products, arithmetic and copies ran while one was open for 2% of the time, Pallas kernels for 0%

commit v1 on v0

--- a/solution.py
+++ b/solution.py
@@ -45,7 +45,13 @@
 ):
     rows = audio.shape[0]
     same_clip_flags = clip_masks(clip_lengths[0], rows)
-    mix_full = lax.all_gather(mix_weight, "shard", axis=0, tiled=True)
+    conv_rows = conv_weight.shape[0]
+    mix_rows = mix_weight.shape[0]
+    both = jnp.concatenate([conv_weight, mix_weight], axis=0)
+    gathered = lax.all_gather(both, "shard", axis=0, tiled=True)
+    gathered = gathered.reshape(-1, conv_rows + mix_rows, C)
+    conv_full = gathered[:, :conv_rows].reshape(-1, C)
+    mix_full = gathered[:, conv_rows:].reshape(-1, C)
     audio_f = audio.astype(jnp.float32)
     act_in, slope_in, dalpha_in = snake_parts(audio_f, alpha_in)
     first = act_in.astype(jnp.bfloat16)
@@ -59,7 +65,7 @@
     unfolded = jnp.concatenate(columns, axis=1)
     product = jnp.dot(
         unfolded,
-        lax.all_gather(conv_weight, "shard", axis=0, tiled=True),
+        conv_full,
         preferred_element_type=jnp.float32,
     )
     pre = product + conv_bias
@@ -77,7 +83,7 @@
     )
     d_unf = lax.dot_general(
         d_pre,
-        lax.all_gather(conv_weight, "shard", axis=0, tiled=True),
+        conv_full,
         (((1,), (1,)), ((), ())),
         preferred_element_type=jnp.float32,
     ).astype(jnp.bfloat16)
@@ -96,11 +102,20 @@
             jnp.sum(second_gradient * dalpha_mid, axis=0),
         ]
     )
-    conv_grad, mix_grad, vector_grad = (
-        lax.psum_scatter(convolution_part, ("dp", "shard"), scatter_dimension=0, tiled=True),
-        lax.psum_scatter(mix_term, ("dp", "shard"), scatter_dimension=0, tiled=True),
-        lax.psum_scatter(vectors, ("dp", "shard"), scatter_dimension=1, tiled=True),
-    )
+    devices = lax.axis_size(("dp", "shard"))
+    conv_each = convolution_part.shape[0] // devices
+    mix_each = mix_term.shape[0] // devices
+    packed = jnp.concatenate(
+        [
+            convolution_part.reshape(devices, conv_each, C),
+            mix_term.reshape(devices, mix_each, C),
+        ],
+        axis=1,
+    ).reshape(-1, C)
+    summed = lax.psum_scatter(packed, ("dp", "shard"), scatter_dimension=0, tiled=True)
+    conv_grad = summed[:conv_each]
+    mix_grad = summed[conv_each:]
+    vector_grad = lax.psum_scatter(vectors, ("dp", "shard"), scatter_dimension=1, tiled=True)
     return (in_grad, conv_grad, mix_grad, vector_grad)
 
 

time: 1040 us -> 1410 us (1.36)
  waiting for transfers between devices: 82.7 us -> 1250 us
  blocking collectives: 777 us -> 78.9 us
  starting transfers between devices: 119 us -> 0.08 us
    reduce_scatter x0 -> x1, waiting for transfers between devices: none -> 1200 us  [per_device(): lax.psum_scatter(packed, ('dp', 'shard'), scatter_dimension=0, tiled=True)]
    unnamed x2 -> x1, blocking collectives: 747 us -> 78.9 us
    unnamed x33 -> x0, starting transfers between devices: 119 us -> none
    unnamed x35 -> x2, waiting for transfers between devices: 66.3 us -> 0.03 us
    all_gather x1, waiting for transfers between devices: 16.5 us -> 48.3 us  [per_device(): gathered = lax.all_gather(both, 'shard', axis=0, tiled=True)]
    all_gather x1 -> x0, blocking collectives: 29.8 us -> none  [per_device(): mix_full = lax.all_gather(mix_weight, 'shard', axis=0, tiled=True)]
  transfers between devices with their start and end apart: 34 -> 2, of which waited for: 4 -> 2; matrix products, arithmetic and copies ran while one was open for 2% -> 1% of each run, Pallas kernels for 0% -> 0%
where the time goes in v1:
time: 1410 us
  waiting for transfers between devices  1250 us (89%)
  blocking collectives  78.9 us (6%)
  other arithmetic  24.4 us (2%)
  local copies, waits for them, and re-layouts  19.7 us (1%)
  matrix products  16.5 us (1%)
  between operations  14.3 us (1%)
    reduce_scatter x1, waiting for transfers between devices, per_device(): lax.psum_scatter(packed, ('dp', 'shard'), scatter_dimension=0, tiled=True)  1200 us
    unnamed x1, blocking collectives  78.9 us
    all_gather x1, waiting for transfers between devices, per_device(): gathered = lax.all_gather(both, 'shard', axis=0, tiled=True)  48.3 us
  transfers between devices with their start and end apart: 2, of which 2 were waited for; matrix products, arithmetic and copies ran while one was open for 1% of the time, Pallas kernels for 0%

profile of v1, /device:TPU:32, one launch (start us, length us, event | category | flops | bytes accessed | tf_op | source)
XLA Modules:
  0.0 1406.0 jit_solution(2043270761040086073)
XLA Ops:
  7.2 1.9 pad_maximum_fusion.1
  9.2 0.8 reduce-window.8
  10.4 0.7 broadcast_multiply_fusion.1
  11.1 2.8 fusion.7
  14.9 1.8 constant_dynamic-update-slice_fusion
  17.1 48.3 %all-gather.2.cloned.1.call-done = bf16[4096,512]{1,0:T(8,128)(2,1)} async-done(((bf16[512,512]{1,0:T(8,128)(2,1)}), bf16[4096,512]{1,0:T(8,128)(2,1)}) %all-gather.2.cloned.1.call-update) | async-done | bytes 4194320 | tf_op jit(solution)/shard_map/all_gather | solution.py:51
  65.4 1.9 slice.116
  67.2 2.3 slice.123
  69.6 1.1 convolution_add_fusion
  70.7 0.6 copy-done
  71.3 0.8 copy-done.7
  72.1 3.0 fusion.13
  75.1 1.8 reshape.69
  77.0 5.0 convert_reduce_fusion.1
  82.0 4.1 fusion.22
  86.2 9.0 reshape.68
  95.2 8.5 pad_maximum_fusion
  103.9 3.2 convolution_convert_fusion
  107.8 4.0 fusion.12
  111.9 2.5 convert_reduce_fusion
  114.4 78.9 %all-reduce.18 = f32[4,512]{1,0:T(4,128)S(1)} all-reduce(f32[4,512]{1,0:T(4,128)S(1)} %pad_maximum_fusion.2), channel_id=3, replica_groups=mesh['dp'=32,'shard'=8] {'dp','shard'}, use_global_device_ids=true, to_apply=%region_7.8.clone | all-reduce | flops 2048 | bytes 16384
  193.4 0.7 copy.14
  194.1 1203.7 %reduce-scatter.3.cloned.1.call-done = f32[16,512]{1,0:T(8,128)} async-done(((f32[4096,512]{1,0:T(8,128)}), f32[16,512]{1,0:T(8,128)}) %reduce-scatter.3.cloned.1.call-update) | async-done | bytes 32784 | tf_op jit(solution)/shard_map/reduce_scatter | solution.py:115
  1397.8 1.3 slice.144
  (42 shorter events, 2.8 us)
Async XLA Ops:
  7.2 58.2 %all-gather.2.cloned.1.call-start = ((), (), s32[]{:S(2)}) async-start(), calls=%async_computation.1 | async-start | bytes 4718592 | tf_op jit(solution)/shard_map/all_gather | solution.py:51
  9.1 1388.7 %reduce-scatter.3.cloned.1.call-start = ((), (), s32[]{:S(2)}) async-start(), calls=%async_computation.2 | async-start | bytes 8421376 | tf_op jit(solution)/shard_map/reduce_scatter | solution.py:115
  13.9 1.0 copy-start.1
  13.9 0.9 copy-start.4
  67.2 2.3 copy-start.6
  69.5 1.8 copy-start
  69.6 2.6 copy-start.2
  69.6 2.6 copy-start.5
  71.3 0.8 copy-start.7
  107.8 4.1 copy-start.3
Sparse Core Ops, SparseCore 0:
  9.8 55.5 all-gather.1
  103.8 1293.9 reduce-scatter.2

commit v2 on v1

--- a/solution.py
+++ b/solution.py
@@ -1,11 +1,13 @@
 import jax
 import jax.numpy as jnp
 from jax import lax
-from jax.sharding import PartitionSpec as P
+from jax.sharding import Mesh, PartitionSpec as P
 
 C = 512
 TAPS = 7
 DILATION_SIZE = 9
+FRAME_AXES = ("x", "y", "c", "z")
+SCATTER_ORDER = ("c", "z", "y", "x")
 
 
 def shift_rows(block, tap_offset, fill):
@@ -48,7 +50,7 @@
     conv_rows = conv_weight.shape[0]
     mix_rows = mix_weight.shape[0]
     both = jnp.concatenate([conv_weight, mix_weight], axis=0)
-    gathered = lax.all_gather(both, "shard", axis=0, tiled=True)
+    gathered = lax.all_gather(both, "z", axis=0, tiled=True)
     gathered = gathered.reshape(-1, conv_rows + mix_rows, C)
     conv_full = gathered[:, :conv_rows].reshape(-1, C)
     mix_full = gathered[:, conv_rows:].reshape(-1, C)
@@ -102,7 +104,10 @@
             jnp.sum(second_gradient * dalpha_mid, axis=0),
         ]
     )
-    devices = lax.axis_size(("dp", "shard"))
+    sizes = [lax.axis_size(a) for a in FRAME_AXES]
+    devices = 1
+    for s in sizes:
+        devices *= s
     conv_each = convolution_part.shape[0] // devices
     mix_each = mix_term.shape[0] // devices
     packed = jnp.concatenate(
@@ -111,34 +116,30 @@
             mix_term.reshape(devices, mix_each, C),
         ],
         axis=1,
-    ).reshape(-1, C)
-    summed = lax.psum_scatter(packed, ("dp", "shard"), scatter_dimension=0, tiled=True)
-    conv_grad = summed[:conv_each]
-    mix_grad = summed[conv_each:]
-    vector_grad = lax.psum_scatter(vectors, ("dp", "shard"), scatter_dimension=1, tiled=True)
+    )
+    packed = packed.reshape(*sizes, conv_each + mix_each, C)
+    order = [FRAME_AXES.index(a) for a in SCATTER_ORDER]
+    packed = packed.transpose(*order, 4, 5).reshape(-1, C)
+    for axis in SCATTER_ORDER:
+        packed = lax.psum_scatter(packed, axis, scatter_dimension=0, tiled=True)
+    conv_grad = packed[:conv_each]
+    mix_grad = packed[conv_each:]
+    vector_grad = lax.psum_scatter(vectors, FRAME_AXES, scatter_dimension=1, tiled=True)
     return (in_grad, conv_grad, mix_grad, vector_grad)
 
 
 def solution(mesh):
-    placed = (
-        P(("dp", "shard"), None),
-        P(("dp", "shard"), None),
-        P(("dp", "shard"), None),
-        P("shard", None),
-        P("shard", None),
-        P(),
-        P(),
-        P(),
-    )
+    devices = mesh.devices
+    xs = len({d.coords[0] for d in devices.flat})
+    ys = len({d.coords[1] for d in devices.flat})
+    dp, shard = devices.shape
+    split = Mesh(devices.reshape(xs, ys, dp // (xs * ys), shard), FRAME_AXES)
+    frames = P(FRAME_AXES, None)
+    placed = (frames, frames, frames, P("z", None), P("z", None), P(), P(), P())
     return jax.shard_map(
         per_device,
-        mesh=mesh,
+        mesh=split,
         in_specs=placed,
-        out_specs=(
-            P(("dp", "shard"), None),
-            P(("dp", "shard"), None),
-            P(("dp", "shard"), None),
-            P(None, ("dp", "shard")),
-        ),
+        out_specs=(frames, frames, frames, P(None, FRAME_AXES)),
         check_vma=False,
     )

time: 1410 us -> 298 us (0.21)
  waiting for transfers between devices: 1250 us -> 145 us
    reduce_scatter x1 -> x4, waiting for transfers between devices: 1200 us -> 96.8 us  [per_device(): packed = lax.psum_scatter(packed, axis, scatter_dimension=0, tiled=True)]
  transfers between devices with their start and end apart: 2 -> 5, of which waited for: 2 -> 4; matrix products, arithmetic and copies ran while one was open for 1% -> 7% of each run, Pallas kernels for 0% -> 0%
where the time goes in v2:
time: 298 us; the launch traced here: 296 us
  waiting for transfers between devices  145 us (49%)
  blocking collectives  76.1 us (26%)
  local copies, waits for them, and re-layouts  23.5 us (8%)
  other arithmetic  21.3 us (7%)
  matrix products  15.5 us (5%)
  between operations  14.1 us (5%)
    reduce_scatter x4, waiting for transfers between devices, per_device(): packed = lax.psum_scatter(packed, axis, scatter_dimension=0, tiled=True)  96.8 us
    unnamed x1, blocking collectives  76.1 us
    all_gather x1, waiting for transfers between devices, per_device(): gathered = lax.all_gather(both, 'z', axis=0, tiled=True)  48.3 us
    concatenate x2, local copies, waits for them, and re-layouts, per_device(): jnp.concatenate([convolution_part.reshape(devices, conv_each, C), mix_ter...  9.66 us
  transfers between devices with their start and end apart: 5, of which 4 were waited for; matrix products, arithmetic and copies ran while one was open for 7% of the time, Pallas kernels for 0%

profile of v2, /device:TPU:32, one launch (start us, length us, event | category | flops | bytes accessed | tf_op | source)
XLA Modules:
  0.0 296.0 jit_solution(16943515620186127932)
XLA Ops:
  7.2 1.9 pad_maximum_fusion
  9.2 0.8 reduce-window.8
  11.1 2.8 fusion.7
  14.9 1.8 constant_dynamic-update-slice_fusion
  17.1 48.3 %all-gather.2.cloned.1.call-done = bf16[4096,512]{1,0:T(8,128)(2,1)} async-done(((bf16[512,512]{1,0:T(8,128)(2,1)}), bf16[4096,512]{1,0:T(8,128)(2,1)}) %all-gather.2.cloned.1.call-update) | async-done | bytes 4194320 | tf_op jit(solution)/shard_map/all_gather | solution.py:53
  65.4 1.9 slice.116
  67.2 2.3 slice.123
  69.6 1.1 convolution_add_fusion
  72.2 2.0 fusion.13
  74.8 5.1 %convert_reduce_fusion.1 = (f32[512]{0:T(512)S(1)}, bf16[256,512]{1,0:T(8,128)(2,1)S(1)}, f32[512]{0:T(512)S(1)}) fusion(f32[256,512]{1,0:T(8,128)} %copy-done.10, f32[512]{0:T(512)S(1)} %get-tuple-element.39, f32[512]{0:T(512)S(1)} %get-tuple-element.40, f32[512]{0:T(512)S(1)} %copy-done.8, bf16[512,512]{1,0:T(8,128)(2,1)S(1)} %bitcast.34, ...), kind=kOutput, calls=%fused_computation.24 | convolution fusion | flops 136051712 | bytes 1583104 | tf_op jit(solution)/shard_map/dot_general | solution.py:79
  79.9 4.1 %fusion.22 = f32[3584,512]{1,0:T(8,128)} fusion(bf16[256,3584]{1,0:T(8,128)(2,1)S(1)} %copy-done.3, bf16[256,512]{1,0:T(8,128)(2,1)S(1)} %get-tuple-element.21), kind=kOutput, calls=%fused_computation.65 | convolution fusion | flops 939524096 | bytes 9437184 | tf_op jit(solution)/shard_map/dot_general | solution.py:83
  84.0 9.0 %concatenate.88 = f32[4,4,2,8,14,512]{5,4,3,2,1,0:T(8,128)} reshape(f32[3584,512]{1,0:T(8,128)} %fusion.22) | data formatting | bytes 14680064 | tf_op jit(solution)/shard_map/concatenate | solution.py:113
  93.1 4.6 %maximum_bitcast_fusion = f32[2,8,4,4,16,512]{5,4,1,0,2,3:T(8,128)S(1)} fusion(f32[4,4,2,8,2,512]{5,4,3,2,1,0:T(2,128)S(1)} %concatenate.89, f32[4,4,2,8,14,512]{5,4,3,2,1,0:T(8,128)} %concatenate.88), kind=kLoop, calls=%fused_computation | loop fusion | flops 2097152 | bytes 16777216 | tf_op jit(solution)/shard_map/transpose | solution.py:122
  97.6 4.2 %copy.18 = f32[2,8,4,4,16,512]{5,4,3,2,1,0:T(8,128)} copy(f32[2,8,4,4,16,512]{5,4,1,0,2,3:T(8,128)S(1)} %maximum_bitcast_fusion) | data formatting | bytes 16777216 | tf_op jit(solution)/shard_map/transpose | solution.py:122
  101.9 22.3 %reduce-scatter.6.cloned.1.call-done = f32[2048,512]{1,0:T(8,128)} async-done(((f32[4096,512]{1,0:T(8,128)}), f32[2048,512]{1,0:T(8,128)}) %reduce-scatter.6.cloned.1.call-update) | async-done | bytes 4194320 | tf_op jit(solution)/shard_map/reduce_scatter | solution.py:124
  124.7 3.2 %convolution_convert_fusion = bf16[256,3584]{1,0:T(8,128)(2,1)S(1)} fusion(bf16[256,512]{1,0:T(8,128)(2,1)S(1)} %get-tuple-element.21, bf16[3584,512]{1,0:T(8,128)(2,1)} %bitcast.31), kind=kOutput, calls=%fused_computation.1 | convolution fusion | flops 940441600 | bytes 5767168 | tf_op jit(solution)/shard_map/dot_general | solution.py:86
  127.9 0.9 fusion.15
  128.8 52.9 %reduce-scatter.8.cloned.1.call-done = f32[256,512]{1,0:T(8,128)} async-done(((f32[2048,512]{1,0:T(8,128)}), f32[256,512]{1,0:T(8,128)}) %reduce-scatter.8.cloned.1.call-update) | async-done | bytes 524304 | tf_op jit(solution)/shard_map/reduce_scatter | solution.py:124
  181.8 1.1 convert_select_fusion.4
  183.3 3.9 %fusion.12 = (f32[512]{0:T(512)S(1)}, f32[256,512]{1,0:T(8,128)S(1)}) fusion(bf16[256,512]{1,0:T(8,128)(2,1)S(1)} %copy-done.1, f32[512]{0:T(512)S(1)} %get-tuple-element.42, f32[512]{0:T(512)S(1)} %get-tuple-element.41, f32[512]{0:T(512)S(1)} %copy-done.7, f32[229,512]{1,0:T(8,128)S(1)} %get-tuple-element.59, f32[238,512]{1,0:T(8,128)S(1)} %get-tuple-element.57, ...), kind=kLoop, calls=%fused_computation.30 | loop fusion | flops 2227712 | bytes 3981312 | tf_op jit(solution)/shard_map/reduce_sum | solution.py:103
  187.1 21.6 %reduce-scatter.10.cloned.1.call-done = f32[64,512]{1,0:T(8,128)} async-done(((f32[256,512]{1,0:T(8,128)}), f32[64,512]{1,0:T(8,128)}) %reduce-scatter.10.cloned.1.call-update) | async-done | bytes 131088 | tf_op jit(solution)/shard_map/reduce_scatter | solution.py:124
  208.7 2.5 convert_reduce_fusion
  211.3 76.1 %all-reduce.18 = f32[4,512]{1,0:T(4,128)S(1)} all-reduce(f32[4,512]{1,0:T(4,128)S(1)} %pad_maximum_fusion.1), channel_id=6, replica_groups=mesh['x'=4,'y'=4,'c'=2,'z'=8] {'x','y','c','z'}, use_global_device_ids=true, to_apply=%region_10.11.clone | all-reduce | flops 2048 | bytes 16384
  288.1 1.3 slice.144
  (58 shorter events, 6.2 us)
Async XLA Ops:
  7.2 58.2 %all-gather.2.cloned.1.call-start = ((), (), s32[]{:S(2)}) async-start(), calls=%async_computation.4 | async-start | bytes 4718592 | tf_op jit(solution)/shard_map/all_gather | solution.py:53
  9.1 115.1 %reduce-scatter.6.cloned.1.call-start = ((), (), s32[]{:S(2)}) async-start(), calls=%async_computation.5 | async-start | bytes 12582912 | tf_op jit(solution)/shard_map/reduce_scatter | solution.py:124
  13.9 1.0 copy-start.1
  13.9 0.9 copy-start.7
  17.1 52.5 %copy-start.2 = (bf16[256,3584]{1,0:T(8,128)(2,1)}, bf16[256,3584]{1,0:T(8,128)(2,1)S(1)}, u32[]{:S(2)}) copy-start(bf16[256,3584]{1,0:T(8,128)(2,1)S(1)} %select_dynamic-update-slice_fusion) | copy-start | bytes 5505028
  67.2 2.3 copy-start.9
  69.5 1.8 copy-start
  69.6 2.6 copy-start.5
  69.6 2.6 copy-start.8
  71.4 0.8 copy-start.10
  72.2 2.6 copy-start.4
  74.8 5.1 %copy-start.3 = (bf16[256,3584]{1,0:T(8,128)(2,1)S(1)}, bf16[256,3584]{1,0:T(8,128)(2,1)}, u32[]{:S(2)}) copy-start(bf16[256,3584]{1,0:T(8,128)(2,1)} %copy-done.2) | copy-start | bytes 5505028
  101.9 79.8 %reduce-scatter.8.cloned.1.call-start = ((), (), s32[]{:S(2)}) async-start(), calls=%async_computation.6 | async-start | bytes 4718592 | tf_op jit(solution)/shard_map/reduce_scatter | solution.py:124
  124.3 84.4 %reduce-scatter.10.cloned.1.call-start = ((), (), s32[]{:S(2)}) async-start(), calls=%async_computation.7 | async-start | bytes 655360 | tf_op jit(solution)/shard_map/reduce_scatter | solution.py:124
  181.7 106.4 %reduce-scatter.12.cloned.1.call-start = ((), (), s32[]{:S(2)}) async-start(), calls=%async_computation.8 | async-start | bytes 163840 | tf_op jit(solution)/shard_map/reduce_scatter | solution.py:124
  183.2 25.5 %copy-start.6 = (bf16[256,512]{1,0:T(8,128)(2,1)S(1)}, bf16[256,512]{1,0:T(8,128)(2,1)}, u32[]{:S(2)}) copy-start(bf16[256,512]{1,0:T(8,128)(2,1)} %param.9) | copy-start | bytes 786436
Sparse Core Ops, SparseCore 0:
  9.8 55.5 all-gather.1
  102.0 22.2 reduce-scatter.5
  126.8 54.8 reduce-scatter.7
  184.1 24.5 reduce-scatter.9
  211.6 22.9 reduce-scatter.11

commit v3 on v2

--- a/solution.py
+++ b/solution.py
@@ -8,6 +8,7 @@
 DILATION_SIZE = 9
 FRAME_AXES = ("x", "y", "c", "z")
 SCATTER_ORDER = ("c", "z", "y", "x")
+EXTRA_COLUMNS = 128
 
 
 def shift_rows(block, tap_offset, fill):
@@ -120,11 +121,30 @@
     packed = packed.reshape(*sizes, conv_each + mix_each, C)
     order = [FRAME_AXES.index(a) for a in SCATTER_ORDER]
     packed = packed.transpose(*order, 4, 5).reshape(-1, C)
-    for axis in SCATTER_ORDER:
+    first_axis, *rest = SCATTER_ORDER
+    packed = lax.psum_scatter(packed, first_axis, scatter_dimension=0, tiled=True)
+    vectors = lax.psum(vectors, first_axis)
+    block = conv_each + mix_each
+    held = packed.shape[0] // block
+    share = vectors.shape[1] // devices
+    vec_blocks = vectors.reshape(4, devices, share).transpose(1, 0, 2).reshape(*sizes, 4 * share)
+    order_rest = [FRAME_AXES.index(a) for a in rest]
+    mine = lax.axis_index(first_axis)
+    vec_blocks = jnp.take(vec_blocks, mine, axis=FRAME_AXES.index(first_axis))
+    kept = [FRAME_AXES.index(a) for a in FRAME_AXES if a != first_axis]
+    vec_blocks = vec_blocks.transpose(*[kept.index(o) for o in order_rest], len(kept))
+    vec_blocks = vec_blocks.reshape(held, 4 * share)
+    extra = jnp.zeros((held, block, EXTRA_COLUMNS), jnp.float32)
+    extra = extra.at[:, 0, : 4 * share].set(vec_blocks)
+    packed = jnp.concatenate([packed.reshape(held, block, C), extra], axis=2)
+    packed = packed.reshape(held * block, C + EXTRA_COLUMNS).astype(jnp.bfloat16)
+    for i, axis in enumerate(rest):
         packed = lax.psum_scatter(packed, axis, scatter_dimension=0, tiled=True)
-    conv_grad = packed[:conv_each]
-    mix_grad = packed[conv_each:]
-    vector_grad = lax.psum_scatter(vectors, FRAME_AXES, scatter_dimension=1, tiled=True)
+        if i == 0:
+            packed = packed.astype(jnp.float32)
+    conv_grad = packed[:conv_each, :C]
+    mix_grad = packed[conv_each:, :C]
+    vector_grad = packed[0, C : C + 4 * share].reshape(4, share)
     return (in_grad, conv_grad, mix_grad, vector_grad)
 
 

time: 298 us -> 240 us (0.81)
  blocking collectives: 76.1 us -> 3.9 us
  waiting for transfers between devices: 145 us -> 151 us
  other arithmetic: 21.3 us -> 26.4 us
  local copies, waits for them, and re-layouts: 23.5 us -> 26.9 us
    unnamed x1 -> x0, blocking collectives: 76.1 us -> none
    reduce_scatter x0 -> x1, waiting for transfers between devices: none -> 6.71 us  [per_device(): lax.psum_scatter(packed, first_axis, scatter_dimension=0, tiled=True)]
    psum x0 -> x1, blocking collectives: none -> 3.9 us  [per_device(): vectors = lax.psum(vectors, first_axis)]
    reduce_scatter x4 -> x3, waiting for transfers between devices: 96.8 us -> 95.5 us  [per_device(): packed = lax.psum_scatter(packed, axis, scatter_dimension=0, tiled=True)]
  transfers between devices with their start and end apart: 5 -> 5, of which waited for: 4 -> 5; matrix products, arithmetic and copies ran while one was open for 7% -> 8% of each run, Pallas kernels for 0% -> 0%
where the time goes in v3:
time: 240 us; the launch traced here: 239 us
  waiting for transfers between devices  151 us (63%)
  local copies, waits for them, and re-layouts  26.9 us (11%)
  other arithmetic  26.4 us (11%)
  matrix products  16.5 us (7%)
  between operations  14.1 us (6%)
  blocking collectives  3.9 us (2%)
    reduce_scatter x3, waiting for transfers between devices, per_device(): packed = lax.psum_scatter(packed, axis, scatter_dimension=0, tiled=True)  95.5 us
    all_gather x1, waiting for transfers between devices, per_device(): gathered = lax.all_gather(both, 'z', axis=0, tiled=True)  48.3 us
    concatenate x2, local copies, waits for them, and re-layouts, per_device(): jnp.concatenate([convolution_part.reshape(devices, conv_each, C), mix_ter...  10.9 us
    reduce_scatter x1, waiting for transfers between devices, per_device(): lax.psum_scatter(packed, first_axis, scatter_dimension=0, tiled=True)  6.71 us
    dot_general x1, matrix products, per_device(): lax.dot_general(cotangent, mix_full, (((1,), (1,)), ((), ())), preferred_...  5.03 us
  transfers between devices with their start and end apart: 5, of which 5 were waited for; matrix products, arithmetic and copies ran while one was open for 8% of the time, Pallas kernels for 0%

profile of v3, /device:TPU:32, one launch (start us, length us, event | category | flops | bytes accessed | tf_op | source)
XLA Modules:
  0.0 238.7 jit_solution(9269736031557551234)
XLA Ops:
  7.2 1.9 pad_maximum_fusion.1
  11.1 2.8 %fusion.7 = bf16[256,512]{1,0:T(8,128)(2,1)S(1)} fusion(bf16[256,512]{1,0:T(8,128)(2,1)} %param.10, f32[512]{0:T(512)} %param.16), kind=kLoop, calls=%fused_computation.18 | loop fusion | flops 786432 | bytes 526336 | tf_op jit(solution)/shard_map/convert_element_type | solution.py:60
  14.9 1.8 constant_dynamic-update-slice_fusion
  17.1 48.3 %all-gather.2.cloned.1.call-done = bf16[4096,512]{1,0:T(8,128)(2,1)} async-done(((bf16[512,512]{1,0:T(8,128)(2,1)}), bf16[4096,512]{1,0:T(8,128)(2,1)}) %all-gather.2.cloned.1.call-update) | async-done | bytes 4194320 | tf_op jit(solution)/shard_map/all_gather | solution.py:54
  65.4 1.9 slice.156
  67.2 2.3 slice.163
  72.2 3.0 %fusion.13 = f32[512,512]{1,0:T(8,128)} fusion(bf16[256,512]{1,0:T(8,128)(2,1)S(1)} %copy-done.2, f32[256,512]{1,0:T(8,128)S(1)} %convolution_add_fusion, f32[512]{0:T(512)S(1)} %copy-done.5), kind=kOutput, calls=%fused_computation.38 | convolution fusion | flops 134873088 | bytes 1837056 | tf_op jit(solution)/shard_map/dot_general | solution.py:77
  75.2 1.8 concatenate.98
  77.0 5.0 %convert_reduce_fusion.1 = (f32[512]{0:T(512)S(1)}, bf16[256,512]{1,0:T(8,128)(2,1)S(1)}, f32[512]{0:T(512)S(1)}) fusion(f32[256,512]{1,0:T(8,128)} %copy-done.7, f32[512]{0:T(512)S(1)} %get-tuple-element.62, f32[512]{0:T(512)S(1)} %get-tuple-element.63, f32[512]{0:T(512)S(1)} %copy-done.5, bf16[512,512]{1,0:T(8,128)(2,1)} %bitcast.43, ...), kind=kOutput, calls=%fused_computation.25 | convolution fusion | flops 136051712 | bytes 1583104 | tf_op jit(solution)/shard_map/dot_general | solution.py:80
  82.0 4.2 %fusion.23 = f32[3584,512]{1,0:T(8,128)} fusion(bf16[256,3584]{1,0:T(8,128)(2,1)S(1)} %select_dynamic-update-slice_fusion, bf16[256,512]{1,0:T(8,128)(2,1)S(1)} %get-tuple-element.44), kind=kOutput, calls=%fused_computation.68 | convolution fusion | flops 939524096 | bytes 9437184 | tf_op jit(solution)/shard_map/dot_general | solution.py:84
  86.2 9.0 %concatenate.97 = f32[4,4,2,8,14,512]{5,4,3,2,1,0:T(8,128)} reshape(f32[3584,512]{1,0:T(8,128)} %fusion.23) | data formatting | bytes 14680064 | tf_op jit(solution)/shard_map/concatenate | solution.py:114
  95.2 4.6 %maximum_bitcast_fusion = f32[2,8,4,4,16,512]{5,4,1,0,2,3:T(8,128)S(1)} fusion(f32[4,4,2,8,2,512]{5,4,3,2,1,0:T(2,128)S(1)} %concatenate.98, f32[4,4,2,8,14,512]{5,4,3,2,1,0:T(8,128)} %concatenate.97), kind=kLoop, calls=%fused_computation | loop fusion | flops 2097152 | bytes 16777216 | tf_op jit(solution)/shard_map/transpose | solution.py:123
  99.8 4.2 %copy.24 = f32[2,8,4,4,16,512]{5,4,3,2,1,0:T(8,128)} copy(f32[2,8,4,4,16,512]{5,4,1,0,2,3:T(8,128)S(1)} %maximum_bitcast_fusion) | data formatting | bytes 16777216 | tf_op jit(solution)/shard_map/transpose | solution.py:123
  104.5 3.2 %convolution_convert_fusion = bf16[256,3584]{1,0:T(8,128)(2,1)S(1)} fusion(bf16[256,512]{1,0:T(8,128)(2,1)S(1)} %get-tuple-element.44, bf16[3584,512]{1,0:T(8,128)(2,1)} %bitcast.38), kind=kOutput, calls=%fused_computation.1 | convolution fusion | flops 940441600 | bytes 5767168 | tf_op jit(solution)/shard_map/dot_general | solution.py:87
  108.4 3.9 %fusion.12 = (f32[512]{0:T(512)S(1)}, f32[256,512]{1,0:T(8,128)S(1)}) fusion(bf16[256,512]{1,0:T(8,128)(2,1)S(1)} %copy-done.1, f32[512]{0:T(512)S(1)} %get-tuple-element.65, f32[512]{0:T(512)S(1)} %get-tuple-element.64, f32[512]{0:T(512)S(1)} %copy-done.4, f32[229,512]{1,0:T(8,128)S(1)} %get-tuple-element.82, f32[238,512]{1,0:T(8,128)S(1)} %get-tuple-element.80, ...), kind=kLoop, calls=%fused_computation.31 | loop fusion | flops 2227712 | bytes 3981312 | tf_op jit(solution)/shard_map/reduce_sum | solution.py:104
  112.3 2.5 %convert_reduce_fusion = (f32[512]{0:T(512)S(1)}, bf16[256,512]{1,0:T(8,128)(2,1)}) fusion(bf16[256,512]{1,0:T(8,128)(2,1)S(1)} %copy-done.3, f32[256,512]{1,0:T(8,128)S(1)} %get-tuple-element.46, bf16[256,512]{1,0:T(8,128)(2,1)S(1)} %copy-done.1, f32[512]{0:T(512)S(1)} %get-tuple-element.64), kind=kLoop, calls=%fused_computation.9 | loop fusion | flops 1048064 | bytes 1314816 | tf_op jit(solution)/shard_map/reduce_sum | solution.py:103
  115.4 3.9 %psum.7 = bf16[4,4,2,8,8]{3,2,1,0,4:T(2,128)(2,1)S(1)} all-reduce(f32[4,4,2,8,8]{3,2,1,0,4:T(2,128)S(1)} %reshape.126), channel_id=1, replica_groups=mesh['x'=4,'y'=4,'c'=2,'z'=8] {'c'}, use_global_device_ids=true, to_apply=%region_7.8 | all-reduce | flops 2048 | bytes 12288 | tf_op jit(solution)/shard_map/psum | solution.py:126
  119.7 6.7 %reduce-scatter.5.cloned.1.call-done = f32[2048,512]{1,0:T(8,128)} async-done(((f32[4096,512]{1,0:T(8,128)}), f32[2048,512]{1,0:T(8,128)}) %reduce-scatter.5.cloned.1.call-update) | async-done | bytes 4194320 | tf_op jit(solution)/shard_map/reduce_scatter | solution.py:125
  126.4 2.5 %convert.11 = bf16[2048,512]{1,0:T(8,128)(2,1)S(1)} convert(f32[2048,512]{1,0:T(8,128)} %reduce-scatter.5.cloned.1.call-done) | non-fusion elementwise | flops 1048576 | bytes 6291456 | tf_op jit(solution)/shard_map/convert
  128.8 1.7 pad_maximum_fusion
  130.6 44.5 %reduce-scatter.7.cloned.1.call-done = bf16[256,640]{1,0:T(8,128)(2,1)} async-done(((bf16[2048,640]{1,0:T(8,128)(2,1)}), bf16[256,640]{1,0:T(8,128)(2,1)}) %reduce-scatter.7.cloned.1.call-update) | async-done | bytes 327696 | tf_op jit(solution)/shard_map/reduce_scatter | solution.py:142
  175.2 1.9 convert_element_type.69
  177.1 25.6 %reduce-scatter.9.cloned.1.call-done = f32[64,640]{1,0:T(8,128)} async-done(((f32[256,640]{1,0:T(8,128)}), f32[64,640]{1,0:T(8,128)}) %reduce-scatter.9.cloned.1.call-update) | async-done | bytes 163856 | tf_op jit(solution)/shard_map/reduce_scatter | solution.py:142
  202.7 25.3 %reduce-scatter.11.cloned.1.call-done = f32[16,640]{1,0:T(8,128)} async-done(((f32[64,640]{1,0:T(8,128)}), f32[16,640]{1,0:T(8,128)}) %reduce-scatter.11.cloned.1.call-update) | async-done | bytes 40976 | tf_op jit(solution)/shard_map/reduce_scatter | solution.py:142
  (65 shorter events, 12.2 us)
Async XLA Ops:
  7.2 58.2 %all-gather.2.cloned.1.call-start = ((), (), s32[]{:S(2)}) async-start(), calls=%async_computation.4 | async-start | bytes 4718592 | tf_op jit(solution)/shard_map/all_gather | solution.py:54
  9.1 117.3 %reduce-scatter.5.cloned.1.call-start = ((), (), s32[]{:S(2)}) async-start(), calls=%async_computation.5 | async-start | bytes 12582912 | tf_op jit(solution)/shard_map/reduce_scatter | solution.py:125
  13.9 1.0 copy-start.1
  13.9 0.9 copy-start.4
  67.2 2.3 copy-start.6
  69.5 1.8 copy-start
  69.6 2.6 %copy-start.2 = (bf16[256,512]{1,0:T(8,128)(2,1)S(1)}, bf16[256,512]{1,0:T(8,128)(2,1)}, u32[]{:S(2)}) copy-start(bf16[256,512]{1,0:T(8,128)(2,1)} %param.11) | copy-start | bytes 786436
  69.6 2.6 %copy-start.5 = (f32[512]{0:T(512)S(1)}, f32[512]{0:T(512)}, u32[]{:S(2)}) copy-start(f32[512]{0:T(512)} %param.17) | copy-start | bytes 6148
  71.4 0.8 copy-start.7
  104.0 71.2 %reduce-scatter.7.cloned.1.call-start = ((), (), s32[]{:S(2)}) async-start(), calls=%async_computation.6 | async-start | bytes 2949120 | tf_op jit(solution)/shard_map/reduce_scatter | solution.py:142
  108.4 3.9 %copy-start.3 = (bf16[256,512]{1,0:T(8,128)(2,1)S(1)}, bf16[256,512]{1,0:T(8,128)(2,1)}, u32[]{:S(2)}) copy-start(bf16[256,512]{1,0:T(8,128)(2,1)} %param.11) | copy-start | bytes 786436
  130.6 72.1 %reduce-scatter.9.cloned.1.call-start = ((), (), s32[]{:S(2)}) async-start(), calls=%async_computation.7 | async-start | bytes 819200 | tf_op jit(solution)/shard_map/reduce_scatter | solution.py:142
  177.1 51.0 %reduce-scatter.11.cloned.1.call-start = ((), (), s32[]{:S(2)}) async-start(), calls=%async_computation.8 | async-start | bytes 204800 | tf_op jit(solution)/shard_map/reduce_scatter | solution.py:142
Sparse Core Ops, SparseCore 0:
  9.8 55.5 all-gather.1
  104.1 22.2 reduce-scatter.4
  130.7 44.4 reduce-scatter.6
  177.6 25.0 reduce-scatter.8
  205.0 22.9 reduce-scatter.10

commit v4 on v3

--- a/solution.py
+++ b/solution.py
@@ -41,6 +41,17 @@
         1.0 + double,
         value * double / alpha - sine * sine / (alpha * alpha),
     )
+
+
+def permute_scatter(value, axis):
+    n = lax.axis_size(axis)
+    me = lax.axis_index(axis)
+    each = value.shape[0] // n
+    total = lax.dynamic_slice_in_dim(value, me * each, each)
+    for step in range(1, n):
+        chunk = lax.dynamic_slice_in_dim(value, ((me + step) % n) * each, each)
+        total = total + lax.ppermute(chunk, axis, [(j, (j + step) % n) for j in range(n)])
+    return total
 
 
 def per_device(
@@ -138,10 +149,10 @@
     extra = extra.at[:, 0, : 4 * share].set(vec_blocks)
     packed = jnp.concatenate([packed.reshape(held, block, C), extra], axis=2)
     packed = packed.reshape(held * block, C + EXTRA_COLUMNS).astype(jnp.bfloat16)
-    for i, axis in enumerate(rest):
-        packed = lax.psum_scatter(packed, axis, scatter_dimension=0, tiled=True)
-        if i == 0:
-            packed = packed.astype(jnp.float32)
+    packed = lax.psum_scatter(packed, rest[0], scatter_dimension=0, tiled=True)
+    packed = packed.astype(jnp.float32)
+    for axis in rest[1:]:
+        packed = permute_scatter(packed, axis)
     conv_grad = packed[:conv_each, :C]
     mix_grad = packed[conv_each:, :C]
     vector_grad = packed[0, C : C + 4 * share].reshape(4, share)

time: 240 us -> 205 us (0.85)
  waiting for transfers between devices: 151 us -> 111 us
  starting transfers between devices: 0.39 us -> 9.35 us
    reduce_scatter x3 -> x1, waiting for transfers between devices: 95.5 us -> 44.6 us  [per_device(): packed = lax.psum_scatter(packed, rest[0], scatter_dimension=0, tiled=True)]
    ppermute x0 -> x6, waiting for transfers between devices: none -> 11.1 us  [permute_scatter(): lax.ppermute(chunk, axis, [(j, (j + step) % n) for j in range(n)])]
    ppermute x0 -> x6, starting transfers between devices: none -> 9.04 us  [permute_scatter(): lax.ppermute(chunk, axis, [(j, (j + step) % n) for j in range(n)])]
  transfers between devices with their start and end apart: 5 -> 9, of which waited for: 5 -> 8; matrix products, arithmetic and copies ran while one was open for 8% -> 9% of each run, Pallas kernels for 0% -> 0%
where the time goes in v4:
time: 205 us
  waiting for transfers between devices  111 us (54%)
  other arithmetic  25.7 us (13%)
  local copies, waits for them, and re-layouts  24.5 us (12%)
  matrix products  16.5 us (8%)
  between operations  14.1 us (7%)
  starting transfers between devices  9.35 us (5%)
  blocking collectives  3.88 us (2%)
    all_gather x1, waiting for transfers between devices, per_device(): gathered = lax.all_gather(both, 'z', axis=0, tiled=True)  48.3 us
    reduce_scatter x1, waiting for transfers between devices, per_device(): packed = lax.psum_scatter(packed, rest[0], scatter_dimension=0, tiled=True)  44.6 us
    ppermute x6, waiting for transfers between devices, permute_scatter(): lax.ppermute(chunk, axis, [(j, (j + step) % n) for j in range(n)])  11.1 us
    concatenate x2, local copies, waits for them, and re-layouts, per_device(): jnp.concatenate([convolution_part.reshape(devices, conv_each, C), mix_ter...  10.9 us
    ppermute x6, starting transfers between devices, permute_scatter(): lax.ppermute(chunk, axis, [(j, (j + step) % n) for j in range(n)])  9.04 us
    reduce_scatter x1, waiting for transfers between devices, per_device(): lax.psum_scatter(packed, first_axis, scatter_dimension=0, tiled=True)  6.74 us
    dot_general x1, matrix products, per_device(): lax.dot_general(cotangent, mix_full, (((1,), (1,)), ((), ())), preferred_...  5.03 us
    transpose x1, other arithmetic, per_device(): packed = packed.transpose(*order, 4, 5).reshape(-1, C)  4.56 us
  transfers between devices with their start and end apart: 9, of which 8 were waited for; matrix products, arithmetic and copies ran while one was open for 9% of the time, Pallas kernels for 0%

profile of v4, /device:TPU:32, one launch (start us, length us, event | category | flops | bytes accessed | tf_op | source)
XLA Modules:
  0.0 204.8 jit_solution(13807871902257210792)
XLA Ops:
  7.2 1.9 pad_maximum_fusion.1
  11.1 2.8 %fusion.7 = bf16[256,512]{1,0:T(8,128)(2,1)S(1)} fusion(bf16[256,512]{1,0:T(8,128)(2,1)} %param.10, f32[512]{0:T(512)} %param.16), kind=kLoop, calls=%fused_computation.18 | loop fusion | flops 786432 | bytes 526336 | tf_op jit(solution)/shard_map/convert_element_type | solution.py:71
  17.0 48.3 %all-gather.2.cloned.1.call-done = bf16[4096,512]{1,0:T(8,128)(2,1)} async-done(((bf16[512,512]{1,0:T(8,128)(2,1)}), bf16[4096,512]{1,0:T(8,128)(2,1)}) %all-gather.2.cloned.1.call-update) | async-done | bytes 4194320 | tf_op jit(solution)/shard_map/all_gather | solution.py:65
  65.4 2.3 %slice.163 = bf16[8,448,512]{2,1,0:T(8,128)(2,1)S(1)} slice(bf16[8,512,512]{2,1,0:T(8,128)(2,1)} %bitcast.39), slice={[0:8], [0:448], [0:512]} | slice | bytes 7340032 | tf_op jit(solution)/shard_map/slice | solution.py:67
  67.7 2.3 %slice.156 = bf16[8,64,512]{2,1,0:T(8,128)(2,1)} slice(bf16[8,512,512]{2,1,0:T(8,128)(2,1)} %bitcast.40), slice={[0:8], [448:512], [0:512]} | slice | bytes 1048576 | tf_op jit(solution)/shard_map/slice | solution.py:68
  71.9 3.0 %fusion.13 = f32[512,512]{1,0:T(8,128)} fusion(bf16[256,512]{1,0:T(8,128)(2,1)S(1)} %copy-done.2, f32[256,512]{1,0:T(8,128)S(1)} %convolution_add_fusion, f32[512]{0:T(512)S(1)} %copy-done.5), kind=kOutput, calls=%fused_computation.38 | convolution fusion | flops 134873088 | bytes 1837056 | tf_op jit(solution)/shard_map/dot_general | solution.py:88
  74.9 1.8 concatenate.98
  76.7 5.0 %convert_reduce_fusion.1 = (f32[512]{0:T(512)S(1)}, bf16[256,512]{1,0:T(8,128)(2,1)S(1)}, f32[512]{0:T(512)S(1)}) fusion(f32[256,512]{1,0:T(8,128)} %copy-done.7, f32[512]{0:T(512)S(1)} %get-tuple-element.68, f32[512]{0:T(512)S(1)} %get-tuple-element.69, f32[512]{0:T(512)S(1)} %copy-done.5, bf16[512,512]{1,0:T(8,128)(2,1)} %bitcast.43, ...), kind=kOutput, calls=%fused_computation.25 | convolution fusion | flops 136051712 | bytes 1583104 | tf_op jit(solution)/shard_map/dot_general | solution.py:91
  81.8 4.1 %fusion.23 = f32[3584,512]{1,0:T(8,128)} fusion(bf16[256,3584]{1,0:T(8,128)(2,1)S(1)} %select_dynamic-update-slice_fusion, bf16[256,512]{1,0:T(8,128)(2,1)S(1)} %get-tuple-element.44), kind=kOutput, calls=%fused_computation.76 | convolution fusion | flops 939524096 | bytes 9437184 | tf_op jit(solution)/shard_map/dot_general | solution.py:95
  85.9 9.0 %concatenate.97 = f32[4,4,2,8,14,512]{5,4,3,2,1,0:T(8,128)} reshape(f32[3584,512]{1,0:T(8,128)} %fusion.23) | data formatting | bytes 14680064 | tf_op jit(solution)/shard_map/concatenate | solution.py:125
  94.9 4.6 %maximum_bitcast_fusion = f32[2,8,4,4,16,512]{5,4,1,0,2,3:T(8,128)S(1)} fusion(f32[4,4,2,8,2,512]{5,4,3,2,1,0:T(2,128)S(1)} %concatenate.98, f32[4,4,2,8,14,512]{5,4,3,2,1,0:T(8,128)} %concatenate.97), kind=kLoop, calls=%fused_computation | loop fusion | flops 2097152 | bytes 16777216 | tf_op jit(solution)/shard_map/transpose | solution.py:134
  99.5 4.2 %copy.24 = f32[2,8,4,4,16,512]{5,4,3,2,1,0:T(8,128)} copy(f32[2,8,4,4,16,512]{5,4,1,0,2,3:T(8,128)S(1)} %maximum_bitcast_fusion) | data formatting | bytes 16777216 | tf_op jit(solution)/shard_map/transpose | solution.py:134
  104.2 3.2 %convolution_convert_fusion = bf16[256,3584]{1,0:T(8,128)(2,1)S(1)} fusion(bf16[256,512]{1,0:T(8,128)(2,1)S(1)} %get-tuple-element.44, bf16[3584,512]{1,0:T(8,128)(2,1)} %bitcast.38), kind=kOutput, calls=%fused_computation.1 | convolution fusion | flops 940441600 | bytes 5767168 | tf_op jit(solution)/shard_map/dot_general | solution.py:98
  108.1 3.9 %fusion.12 = (f32[512]{0:T(512)S(1)}, f32[256,512]{1,0:T(8,128)S(1)}) fusion(bf16[256,512]{1,0:T(8,128)(2,1)S(1)} %copy-done.1, f32[512]{0:T(512)S(1)} %get-tuple-element.71, f32[512]{0:T(512)S(1)} %get-tuple-element.70, f32[512]{0:T(512)S(1)} %copy-done.4, f32[229,512]{1,0:T(8,128)S(1)} %get-tuple-element.88, f32[238,512]{1,0:T(8,128)S(1)} %get-tuple-element.86, ...), kind=kLoop, calls=%fused_computation.31 | loop fusion | flops 2227712 | bytes 3981312 | tf_op jit(solution)/shard_map/reduce_sum | solution.py:115
  112.0 2.5 %convert_reduce_fusion = (f32[512]{0:T(512)S(1)}, bf16[256,512]{1,0:T(8,128)(2,1)}) fusion(bf16[256,512]{1,0:T(8,128)(2,1)S(1)} %copy-done.3, f32[256,512]{1,0:T(8,128)S(1)} %get-tuple-element.46, bf16[256,512]{1,0:T(8,128)(2,1)S(1)} %copy-done.1, f32[512]{0:T(512)S(1)} %get-tuple-element.70), kind=kLoop, calls=%fused_computation.9 | loop fusion | flops 1048064 | bytes 1314816 | tf_op jit(solution)/shard_map/reduce_sum | solution.py:114
  115.1 3.9 %psum.7 = bf16[4,4,2,8,8]{3,2,1,0,4:T(2,128)(2,1)S(1)} all-reduce(f32[4,4,2,8,8]{3,2,1,0,4:T(2,128)S(1)} %reshape.126), channel_id=1, replica_groups=mesh['x'=4,'y'=4,'c'=2,'z'=8] {'c'}, use_global_device_ids=true, to_apply=%region_7.8 | all-reduce | flops 2048 | bytes 12288 | tf_op jit(solution)/shard_map/psum | solution.py:137
  119.4 6.7 %reduce-scatter.3.cloned.1.call-done = f32[2048,512]{1,0:T(8,128)} async-done(((f32[4096,512]{1,0:T(8,128)}), f32[2048,512]{1,0:T(8,128)}) %reduce-scatter.3.cloned.1.call-update) | async-done | bytes 4194320 | tf_op jit(solution)/shard_map/reduce_scatter | solution.py:136
  126.1 2.5 %convert.11 = bf16[2048,512]{1,0:T(8,128)(2,1)S(1)} convert(f32[2048,512]{1,0:T(8,128)} %reduce-scatter.3.cloned.1.call-done) | non-fusion elementwise | flops 1048576 | bytes 6291456 | tf_op jit(solution)/shard_map/convert
  130.4 44.6 %reduce-scatter.5.cloned.1.call-done = bf16[256,640]{1,0:T(8,128)(2,1)} async-done(((bf16[2048,640]{1,0:T(8,128)(2,1)}), bf16[256,640]{1,0:T(8,128)(2,1)}) %reduce-scatter.5.cloned.1.call-update) | async-done | bytes 327696 | tf_op jit(solution)/shard_map/reduce_scatter | solution.py:152
  176.0 2.8 %collective-permute-start.2 = (f32[64,640]{1,0:T(8,128)S(1)}, f32[64,640]{1,0:T(8,128)S(1)}, u32[]{:S(2)}, u32[]{:S(2)}) collective-permute-start(f32[64,640]{1,0:T(8,128)S(1)} %get-tuple-element.55), channel_id=1, source_target_pairs={{0,48},{16,0},{32,16},{48,32},{1,49},{17,1},{33,17},{49,33},{2,50}... | collective-permute-start | bytes 491528 | tf_op jit(solution)/shard_map/ppermute | solution.py:53
  180.5 2.9 %collective-permute-done.2 = f32[64,640]{1,0:T(8,128)S(1)} collective-permute-done((f32[64,640]{1,0:T(8,128)S(1)}, f32[64,640]{1,0:T(8,128)S(1)}, u32[]{:S(2)}, u32[]{:S(2)}) %collective-permute-start.2) | collective-permute-done | bytes 163872 | tf_op jit(solution)/shard_map/ppermute | solution.py:53
  183.5 2.3 %collective-permute-done.1 = f32[64,640]{1,0:T(8,128)S(1)} collective-permute-done((f32[64,640]{1,0:T(8,128)S(1)}, f32[64,640]{1,0:T(8,128)S(1)}, u32[]{:S(2)}, u32[]{:S(2)}) %collective-permute-start.1) | collective-permute-done | bytes 163872 | tf_op jit(solution)/shard_map/ppermute | solution.py:53
  187.5 2.8 %collective-permute-start.5 = (f32[16,640]{1,0:T(8,128)S(1)}, f32[16,640]{1,0:T(8,128)S(1)}, u32[]{:S(2)}, u32[]{:S(2)}) collective-permute-start(f32[16,640]{1,0:T(8,128)S(1)} %get-tuple-element.66), channel_id=1, source_target_pairs={{0,192},{64,0},{128,64},{192,128},{1,193},{65,1},{129,65},{193,129... | collective-permute-start | bytes 122888 | tf_op jit(solution)/shard_map/ppermute | solution.py:53
  192.0 3.7 %collective-permute-done.4 = f32[16,640]{1,0:T(8,128)S(1)} collective-permute-done((f32[16,640]{1,0:T(8,128)S(1)}, f32[16,640]{1,0:T(8,128)S(1)}, u32[]{:S(2)}, u32[]{:S(2)}) %collective-permute-start.4) | collective-permute-done | bytes 40992 | tf_op jit(solution)/shard_map/ppermute | solution.py:53
  (75 shorter events, 19.6 us)
Async XLA Ops:
  7.2 58.2 %all-gather.2.cloned.1.call-start = ((), (), s32[]{:S(2)}) async-start(), calls=%async_computation.2 | async-start | bytes 4718592 | tf_op jit(solution)/shard_map/all_gather | solution.py:65
  9.1 117.0 %reduce-scatter.3.cloned.1.call-start = ((), (), s32[]{:S(2)}) async-start(), calls=%async_computation.3 | async-start | bytes 12582912 | tf_op jit(solution)/shard_map/reduce_scatter | solution.py:136
  13.9 1.0 copy-start.1
  13.9 0.9 copy-start.4
  65.4 4.6 %copy-start.6 = (f32[512]{0:T(512)S(1)}, f32[512]{0:T(512)}, u32[]{:S(2)}) copy-start(f32[512]{0:T(512)} %param.15) | copy-start | bytes 6148
  67.7 3.4 %copy-start = (bf16[8,448,512]{2,1,0:T(8,128)(2,1)}, bf16[8,448,512]{2,1,0:T(8,128)(2,1)S(1)}, u32[]{:S(2)}) copy-start(bf16[8,448,512]{2,1,0:T(8,128)(2,1)S(1)} %slice.163) | copy-start | bytes 11010052
  69.9 2.0 copy-start.2
  69.9 2.0 copy-start.5
  71.1 0.8 copy-start.7
  103.7 71.2 %reduce-scatter.5.cloned.1.call-start = ((), (), s32[]{:S(2)}) async-start(), calls=%async_computation.4 | async-start | bytes 2949120 | tf_op jit(solution)/shard_map/reduce_scatter | solution.py:152
  108.1 3.9 %copy-start.3 = (bf16[256,512]{1,0:T(8,128)(2,1)S(1)}, bf16[256,512]{1,0:T(8,128)(2,1)}, u32[]{:S(2)}) copy-start(bf16[256,512]{1,0:T(8,128)(2,1)} %param.11) | copy-start | bytes 786436
  176.0 7.4 %collective-permute-start.2 = (f32[64,640]{1,0:T(8,128)S(1)}, f32[64,640]{1,0:T(8,128)S(1)}, u32[]{:S(2)}, u32[]{:S(2)}) collective-permute-start(f32[64,640]{1,0:T(8,128)S(1)} %get-tuple-element.55), channel_id=1, source_target_pairs={{0,48},{16,0},{32,16},{48,32},{1,49},{17,1},{33,17},{49,33},{2,50}... | collective-permute-start | bytes 491528 | tf_op jit(solution)/shard_map/ppermute | solution.py:53
  178.8 6.9 %collective-permute-start.1 = (f32[64,640]{1,0:T(8,128)S(1)}, f32[64,640]{1,0:T(8,128)S(1)}, u32[]{:S(2)}, u32[]{:S(2)}) collective-permute-start(f32[64,640]{1,0:T(8,128)S(1)} %get-tuple-element.56), channel_id=1, source_target_pairs={{0,32},{16,48},{32,0},{48,16},{1,33},{17,49},{33,1},{49,17},{2,34}... | collective-permute-start | bytes 491528 | tf_op jit(solution)/shard_map/ppermute | solution.py:53
  179.7 7.7 %collective-permute-start = (f32[64,640]{1,0:T(8,128)S(1)}, f32[64,640]{1,0:T(8,128)S(1)}, u32[]{:S(2)}, u32[]{:S(2)}) collective-permute-start(f32[64,640]{1,0:T(8,128)S(1)} %get-tuple-element.54), channel_id=1, source_target_pairs={{0,16},{16,32},{32,48},{48,0},{1,17},{17,33},{33,49},{49,1},{2,18}... | collective-permute-start | bytes 491528 | tf_op jit(solution)/shard_map/ppermute | solution.py:53
  187.5 4.6 %collective-permute-start.5 = (f32[16,640]{1,0:T(8,128)S(1)}, f32[16,640]{1,0:T(8,128)S(1)}, u32[]{:S(2)}, u32[]{:S(2)}) collective-permute-start(f32[16,640]{1,0:T(8,128)S(1)} %get-tuple-element.66), channel_id=1, source_target_pairs={{0,192},{64,0},{128,64},{192,128},{1,193},{65,1},{129,65},{193,129... | collective-permute-start | bytes 122888 | tf_op jit(solution)/shard_map/ppermute | solution.py:53
  190.3 5.5 %collective-permute-start.4 = (f32[16,640]{1,0:T(8,128)S(1)}, f32[16,640]{1,0:T(8,128)S(1)}, u32[]{:S(2)}, u32[]{:S(2)}) collective-permute-start(f32[16,640]{1,0:T(8,128)S(1)} %get-tuple-element.67), channel_id=1, source_target_pairs={{0,128},{64,192},{128,0},{192,64},{1,129},{65,193},{129,1},{193,65... | collective-permute-start | bytes 122888 | tf_op jit(solution)/shard_map/ppermute | solution.py:53
  191.1 5.2 %collective-permute-start.3 = (f32[16,640]{1,0:T(8,128)S(1)}, f32[16,640]{1,0:T(8,128)S(1)}, u32[]{:S(2)}, u32[]{:S(2)}) collective-permute-start(f32[16,640]{1,0:T(8,128)S(1)} %get-tuple-element.65), channel_id=1, source_target_pairs={{0,64},{64,128},{128,192},{192,0},{1,65},{65,129},{129,193},{193,1... | collective-permute-start | bytes 122888 | tf_op jit(solution)/shard_map/ppermute | solution.py:53
Sparse Core Ops, SparseCore 0:
  9.8 55.5 all-gather.1
  103.9 22.2 reduce-scatter.2
  130.5 44.4 reduce-scatter.4

commit v5 on v4

--- a/solution.py
+++ b/solution.py
@@ -85,16 +85,10 @@
     pre = product + conv_bias
     act_mid, slope_mid, dalpha_mid = snake_parts(pre, alpha_mid)
     second = act_mid.astype(jnp.bfloat16)
-    mix_term = lax.dot_general(
-        second, cotangent, (((0,), (0,)), ((), ())), preferred_element_type=jnp.float32
-    )
     second_gradient = lax.dot_general(
         cotangent, mix_full, (((1,), (1,)), ((), ())), preferred_element_type=jnp.float32
     )
     d_pre = (second_gradient * slope_mid).astype(jnp.bfloat16)
-    convolution_part = lax.dot_general(
-        unfolded, d_pre, (((0,), (0,)), ((), ())), preferred_element_type=jnp.float32
-    )
     d_unf = lax.dot_general(
         d_pre,
         conv_full,
@@ -120,18 +114,22 @@
     devices = 1
     for s in sizes:
         devices *= s
-    conv_each = convolution_part.shape[0] // devices
-    mix_each = mix_term.shape[0] // devices
-    packed = jnp.concatenate(
-        [
-            convolution_part.reshape(devices, conv_each, C),
-            mix_term.reshape(devices, mix_each, C),
-        ],
-        axis=1,
+    conv_each = unfolded.shape[1] // devices
+    mix_each = second.shape[1] // devices
+    order = [FRAME_AXES.index(a) for a in SCATTER_ORDER]
+
+    def lay_out(left):
+        left = jnp.concatenate(left, axis=2).reshape(rows, *sizes, conv_each + mix_each)
+        return left.transpose(0, *[o + 1 for o in order], 5).reshape(rows, -1)
+
+    conv_lhs = lay_out([unfolded.reshape(rows, devices, conv_each), jnp.zeros((rows, devices, mix_each), unfolded.dtype)])
+    mix_lhs = lay_out([jnp.zeros((rows, devices, conv_each), second.dtype), second.reshape(rows, devices, mix_each)])
+    packed = lax.dot_general(
+        jnp.concatenate([conv_lhs, mix_lhs], axis=0),
+        jnp.concatenate([d_pre, cotangent], axis=0),
+        (((0,), (0,)), ((), ())),
+        preferred_element_type=jnp.float32,
     )
-    packed = packed.reshape(*sizes, conv_each + mix_each, C)
-    order = [FRAME_AXES.index(a) for a in SCATTER_ORDER]
-    packed = packed.transpose(*order, 4, 5).reshape(-1, C)
     first_axis, *rest = SCATTER_ORDER
     packed = lax.psum_scatter(packed, first_axis, scatter_dimension=0, tiled=True)
     vectors = lax.psum(vectors, first_axis)
@@ -165,7 +163,7 @@
     ys = len({d.coords[1] for d in devices.flat})
     dp, shard = devices.shape
     split = Mesh(devices.reshape(xs, ys, dp // (xs * ys), shard), FRAME_AXES)
-    frames = P(FRAME_AXES, None)
+    frames = P(FRAME_AXES)
     placed = (frames, frames, frames, P("z", None), P("z", None), P(), P(), P())
     return jax.shard_map(
         per_device,

time: 205 us -> 183 us (0.89)
  local copies, waits for them, and re-layouts: 24.5 us -> 15.7 us
  waiting for transfers between devices: 111 us -> 105 us
  other arithmetic: 25.7 us -> 20.5 us
  matrix products: 16.5 us -> 13.9 us
    concatenate x2 -> x3, local copies, waits for them, and re-layouts: 10.9 us -> 2.94 us  [the longest x1 2.25 us: per_device(): unfolded = jnp.concatenate(columns, axis=1)]
    all_gather x1, waiting for transfers between devices: 48.3 us -> 42 us  [per_device(): gathered = lax.all_gather(both, 'z', axis=0, tiled=True)]
    transpose x1 -> x0, other arithmetic: 4.56 us -> none  [per_device(): packed = packed.transpose(*order, 4, 5).reshape(-1, C)]
    transpose x1 -> x0, local copies, waits for them, and re-layouts: 4.2 us -> none  [per_device(): packed = packed.transpose(*order, 4, 5).reshape(-1, C)]
    reshape x0 -> x4, local copies, waits for them, and re-layouts: none -> 3.16 us  [the longest x1 2.52 us: per_device(): unfolded.reshape(rows, devices, conv_each)]
    dot_general x2 -> x1, matrix products: 7.14 us -> 5.56 us  [per_device(): lax.dot_general(jnp.concatenate([conv_lhs, mix_lhs], axis=0), jnp.concate...]
  transfers between devices with their start and end apart: 9 -> 9, of which waited for: 8 -> 8; matrix products, arithmetic and copies ran while one was open for 9% -> 13% of each run, Pallas kernels for 0% -> 0%
where the time goes in v5:
time: 183 us; the launch traced here: 182 us
  waiting for transfers between devices  105 us (57%)
  other arithmetic  20.5 us (11%)
  local copies, waits for them, and re-layouts  15.7 us (9%)
  between operations  14.2 us (8%)
  matrix products  13.9 us (8%)
  starting transfers between devices  9.35 us (5%)
  blocking collectives  3.85 us (2%)
    reduce_scatter x1, waiting for transfers between devices, per_device(): packed = lax.psum_scatter(packed, rest[0], scatter_dimension=0, tiled=True)  44.6 us
    all_gather x1, waiting for transfers between devices, per_device(): gathered = lax.all_gather(both, 'z', axis=0, tiled=True)  42 us
    ppermute x6, waiting for transfers between devices, permute_scatter(): lax.ppermute(chunk, axis, [(j, (j + step) % n) for j in range(n)])  11.1 us
    ppermute x6, starting transfers between devices, permute_scatter(): lax.ppermute(chunk, axis, [(j, (j + step) % n) for j in range(n)])  9.05 us
    reduce_scatter x1, waiting for transfers between devices, per_device(): lax.psum_scatter(packed, first_axis, scatter_dimension=0, tiled=True)  6.8 us
    dot_general x1, matrix products, per_device(): lax.dot_general(jnp.concatenate([conv_lhs, mix_lhs], axis=0), jnp.concate...  5.56 us
    dot_general x1, matrix products, per_device(): lax.dot_general(cotangent, mix_full, (((1,), (1,)), ((), ())), preferred_...  4.07 us
    reduce_sum x1, other arithmetic, per_device(): jnp.sum(d_first * dalpha_in, axis=0)  3.87 us
  transfers between devices with their start and end apart: 9, of which 8 were waited for; matrix products, arithmetic and copies ran while one was open for 13% of the time, Pallas kernels for 0%

profile of v5, /device:TPU:32, one launch (start us, length us, event | category | flops | bytes accessed | tf_op | source)
XLA Modules:
  0.0 182.1 jit_solution(11097324945408559576)
XLA Ops:
  7.2 1.9 %pad_maximum_fusion.1 = bf16[512,512]{1,0:T(8,128)(2,1)} fusion(bf16[64,512]{1,0:T(8,128)(2,1)} %param.14, bf16[448,512]{1,0:T(8,128)(2,1)} %param.13), kind=kLoop, calls=%fused_computation.26 | loop fusion | flops 1048576 | bytes 1048576 | tf_op jit(solution)/shard_map/concatenate | solution.py:64
  10.4 2.8 %fusion.11 = bf16[256,512]{1,0:T(8,128)(2,1)S(1)} fusion(bf16[256,512]{1,0:T(8,128)(2,1)} %param.10, f32[512]{0:T(512)} %param.16), kind=kLoop, calls=%fused_computation.21 | loop fusion | flops 786432 | bytes 526336 | tf_op jit(solution)/shard_map/convert_element_type | solution.py:71
  14.2 1.8 %constant_dynamic-update-slice_fusion = bf16[256,3584]{1,0:T(8,128)(2,1)S(1)} fusion(bf16[256,3584]{1,0:T(8,128)(2,1)S(1)} %select_dynamic-update-slice_fusion.3, f32[512]{0:T(512)S(1)} %copy-done.5, bf16[256,512]{1,0:T(8,128)(2,1)S(1)} %copy-done.1), kind=kLoop, calls=%fused_computation.54 | loop fusion | flops 786432 | bytes 526336
  17.6 2.2 %copy.31 = bf16[256,3584]{0,1:T(8,128)(2,1)} copy(bf16[256,3584]{1,0:T(8,128)(2,1)S(1)} %select_dynamic-update-slice_fusion) | data formatting | bytes 3670016 | tf_op jit(solution)/shard_map/concatenate | solution.py:79
  19.9 2.5 %reshape.132 = bf16[256,256,14]{0,2,1:T(8,128)(2,1)S(1)} reshape(bf16[256,3584]{0,1:T(8,128)(2,1)} %copy.31) | data formatting | bytes 3670016 | tf_op jit(solution)/shard_map/reshape | solution.py:125
  23.3 42.0 %all-gather.2.cloned.1.call-done = bf16[4096,512]{1,0:T(8,128)(2,1)} async-done(((bf16[512,512]{1,0:T(8,128)(2,1)}), bf16[4096,512]{1,0:T(8,128)(2,1)}) %all-gather.2.cloned.1.call-update) | async-done | bytes 4194320 | tf_op jit(solution)/shard_map/all_gather | solution.py:65
  65.4 2.4 %slice.163 = bf16[8,448,512]{2,1,0:T(8,128)(2,1)S(1)} slice(bf16[8,512,512]{2,1,0:T(8,128)(2,1)} %bitcast.46), slice={[0:8], [0:448], [0:512]} | slice | bytes 7340032 | tf_op jit(solution)/shard_map/slice | solution.py:67
  67.8 1.5 slice.156
  70.4 4.1 %convert_reduce_fusion.1 = (f32[512]{0:T(512)S(1)}, bf16[256,512]{1,0:T(8,128)(2,1)S(1)}, f32[512]{0:T(512)S(1)}, bf16[256,512]{1,0:T(8,128)(2,1)S(1)}) fusion(f32[256,512]{1,0:T(8,128)S(1)} %convolution_add_fusion, f32[512]{0:T(512)S(1)} %get-tuple-element.69, f32[512]{0:T(512)S(1)} %get-tuple-element.70, f32[512]{0:T(512)S(1)} %copy-done.6, ...), kind=kOutput, calls=%fused_computation.31 | convolution fusion | flops 136444928 | bytes 1845248 | tf_op jit(solution)/shard_map/dot_general | solution.py:88
  75.5 5.6 %fusion = f32[4096,512]{1,0:T(8,128)} fusion(bf16[256,4096]{0,1:T(8,128)(2,1)S(1)} %bitcast.50, bf16[256,4096]{0,1:T(8,128)(2,1)S(1)} %bitcast.49, bf16[256,512]{1,0:T(8,128)(2,1)S(1)} %copy-done.4, bf16[256,512]{1,0:T(8,128)(2,1)S(1)} %get-tuple-element.44), kind=kOutput, calls=%fused_computation.1 | convolution fusion | flops 2156920832 | bytes 13107200 | tf_op jit(solution)/shard_map/dot_general | solution.py:127
  81.5 3.2 %convolution_convert_fusion = bf16[256,3584]{1,0:T(8,128)(2,1)S(1)} fusion(bf16[256,512]{1,0:T(8,128)(2,1)S(1)} %get-tuple-element.44, bf16[3584,512]{1,0:T(8,128)(2,1)} %bitcast.43), kind=kOutput, calls=%fused_computation | convolution fusion | flops 940441600 | bytes 5767168 | tf_op jit(solution)/shard_map/dot_general | solution.py:92
  85.4 3.9 %fusion.19 = (f32[512]{0:T(512)S(1)}, f32[256,512]{1,0:T(8,128)S(1)}) fusion(bf16[256,512]{1,0:T(8,128)(2,1)S(1)} %copy-done.1, f32[512]{0:T(512)S(1)} %get-tuple-element.72, f32[512]{0:T(512)S(1)} %get-tuple-element.71, f32[512]{0:T(512)S(1)} %copy-done.5, f32[229,512]{1,0:T(8,128)S(1)} %get-tuple-element.89, f32[238,512]{1,0:T(8,128)S(1)} %get-tuple-element.87, ...), kind=kLoop, calls=%fused_computation.37 | loop fusion | flops 2227712 | bytes 3981312 | tf_op jit(solution)/shard_map/reduce_sum | solution.py:109
  89.3 2.5 %convert_reduce_fusion = (f32[512]{0:T(512)S(1)}, bf16[256,512]{1,0:T(8,128)(2,1)}) fusion(bf16[256,512]{1,0:T(8,128)(2,1)S(1)} %copy-done.4, f32[256,512]{1,0:T(8,128)S(1)} %get-tuple-element.46, bf16[256,512]{1,0:T(8,128)(2,1)S(1)} %copy-done.1, f32[512]{0:T(512)S(1)} %get-tuple-element.71), kind=kLoop, calls=%fused_computation.12 | loop fusion | flops 1048064 | bytes 1314816 | tf_op jit(solution)/shard_map/reduce_sum | solution.py:108
  92.3 3.8 %psum.7 = bf16[4,4,2,8,8]{3,2,1,0,4:T(2,128)(2,1)S(1)} all-reduce(f32[4,4,2,8,8]{3,2,1,0,4:T(2,128)S(1)} %reshape.139), channel_id=1, replica_groups=mesh['x'=4,'y'=4,'c'=2,'z'=8] {'c'}, use_global_device_ids=true, to_apply=%region_7.8 | all-reduce | flops 2048 | bytes 12288 | tf_op jit(solution)/shard_map/psum | solution.py:135
  96.6 6.8 %reduce-scatter.3.cloned.1.call-done = f32[2048,512]{1,0:T(8,128)} async-done(((f32[4096,512]{1,0:T(8,128)}), f32[2048,512]{1,0:T(8,128)}) %reduce-scatter.3.cloned.1.call-update) | async-done | bytes 4194320 | tf_op jit(solution)/shard_map/reduce_scatter | solution.py:134
  103.4 2.5 %convert.11 = bf16[2048,512]{1,0:T(8,128)(2,1)S(1)} convert(f32[2048,512]{1,0:T(8,128)} %reduce-scatter.3.cloned.1.call-done) | non-fusion elementwise | flops 1048576 | bytes 6291456 | tf_op jit(solution)/shard_map/convert
  105.9 1.7 pad_maximum_fusion
  107.7 44.6 %reduce-scatter.5.cloned.1.call-done = bf16[256,640]{1,0:T(8,128)(2,1)} async-done(((bf16[2048,640]{1,0:T(8,128)(2,1)}), bf16[256,640]{1,0:T(8,128)(2,1)}) %reduce-scatter.5.cloned.1.call-update) | async-done | bytes 327696 | tf_op jit(solution)/shard_map/reduce_scatter | solution.py:150
  153.4 2.8 %collective-permute-start.2 = (f32[64,640]{1,0:T(8,128)S(1)}, f32[64,640]{1,0:T(8,128)S(1)}, u32[]{:S(2)}, u32[]{:S(2)}) collective-permute-start(f32[64,640]{1,0:T(8,128)S(1)} %get-tuple-element.55), channel_id=1, source_target_pairs={{0,48},{16,0},{32,16},{48,32},{1,49},{17,1},{33,17},{49,33},{2,50}... | collective-permute-start | bytes 491528 | tf_op jit(solution)/shard_map/ppermute | solution.py:53
  157.9 2.8 %collective-permute-done.2 = f32[64,640]{1,0:T(8,128)S(1)} collective-permute-done((f32[64,640]{1,0:T(8,128)S(1)}, f32[64,640]{1,0:T(8,128)S(1)}, u32[]{:S(2)}, u32[]{:S(2)}) %collective-permute-start.2) | collective-permute-done | bytes 163872 | tf_op jit(solution)/shard_map/ppermute | solution.py:53
  160.8 2.3 %collective-permute-done.1 = f32[64,640]{1,0:T(8,128)S(1)} collective-permute-done((f32[64,640]{1,0:T(8,128)S(1)}, f32[64,640]{1,0:T(8,128)S(1)}, u32[]{:S(2)}, u32[]{:S(2)}) %collective-permute-start.1) | collective-permute-done | bytes 163872 | tf_op jit(solution)/shard_map/ppermute | solution.py:53
  163.1 1.7 collective-permute-done
  164.8 2.8 %collective-permute-start.5 = (f32[16,640]{1,0:T(8,128)S(1)}, f32[16,640]{1,0:T(8,128)S(1)}, u32[]{:S(2)}, u32[]{:S(2)}) collective-permute-start(f32[16,640]{1,0:T(8,128)S(1)} %get-tuple-element.67), channel_id=1, source_target_pairs={{0,192},{64,0},{128,64},{192,128},{1,193},{65,1},{129,65},{193,129... | collective-permute-start | bytes 122888 | tf_op jit(solution)/shard_map/ppermute | solution.py:53
  169.3 3.8 %collective-permute-done.4 = f32[16,640]{1,0:T(8,128)S(1)} collective-permute-done((f32[16,640]{1,0:T(8,128)S(1)}, f32[16,640]{1,0:T(8,128)S(1)}, u32[]{:S(2)}, u32[]{:S(2)}) %collective-permute-start.4) | collective-permute-done | bytes 40992 | tf_op jit(solution)/shard_map/ppermute | solution.py:53
  (78 shorter events, 15.9 us)
Async XLA Ops:
  7.2 58.2 %all-gather.2.cloned.1.call-start = ((), (), s32[]{:S(2)}) async-start(), calls=%async_computation.2 | async-start | bytes 4718592 | tf_op jit(solution)/shard_map/all_gather | solution.py:65
  9.2 94.2 %reduce-scatter.3.cloned.1.call-start = ((), (), s32[]{:S(2)}) async-start(), calls=%async_computation.3 | async-start | bytes 12582912 | tf_op jit(solution)/shard_map/reduce_scatter | solution.py:134
  13.2 1.0 copy-start.1
  13.2 0.9 copy-start.5
  16.3 1.3 copy-start.2
  22.6 0.7 copy-start.6
  65.4 3.9 %copy-start.3 = (bf16[256,3584]{1,0:T(8,128)(2,1)S(1)}, bf16[256,3584]{1,0:T(8,128)(2,1)}, u32[]{:S(2)}) copy-start(bf16[256,3584]{1,0:T(8,128)(2,1)} %copy-done.2) | copy-start | bytes 5505028
  65.4 3.9 %copy-start.7 = (f32[512]{0:T(512)S(1)}, f32[512]{0:T(512)}, u32[]{:S(2)}) copy-start(f32[512]{0:T(512)} %param.15) | copy-start | bytes 6148
  67.8 2.6 %copy-start = (bf16[8,448,512]{2,1,0:T(8,128)(2,1)}, bf16[8,448,512]{2,1,0:T(8,128)(2,1)S(1)}, u32[]{:S(2)}) copy-start(bf16[8,448,512]{2,1,0:T(8,128)(2,1)S(1)} %slice.163) | copy-start | bytes 11010052
  69.3 1.1 copy-start.4
  81.0 71.3 %reduce-scatter.5.cloned.1.call-start = ((), (), s32[]{:S(2)}) async-start(), calls=%async_computation.4 | async-start | bytes 2949120 | tf_op jit(solution)/shard_map/reduce_scatter | solution.py:150
  153.4 7.4 %collective-permute-start.2 = (f32[64,640]{1,0:T(8,128)S(1)}, f32[64,640]{1,0:T(8,128)S(1)}, u32[]{:S(2)}, u32[]{:S(2)}) collective-permute-start(f32[64,640]{1,0:T(8,128)S(1)} %get-tuple-element.55), channel_id=1, source_target_pairs={{0,48},{16,0},{32,16},{48,32},{1,49},{17,1},{33,17},{49,33},{2,50}... | collective-permute-start | bytes 491528 | tf_op jit(solution)/shard_map/ppermute | solution.py:53
  156.2 6.9 %collective-permute-start.1 = (f32[64,640]{1,0:T(8,128)S(1)}, f32[64,640]{1,0:T(8,128)S(1)}, u32[]{:S(2)}, u32[]{:S(2)}) collective-permute-start(f32[64,640]{1,0:T(8,128)S(1)} %get-tuple-element.56), channel_id=1, source_target_pairs={{0,32},{16,48},{32,0},{48,16},{1,33},{17,49},{33,1},{49,17},{2,34}... | collective-permute-start | bytes 491528 | tf_op jit(solution)/shard_map/ppermute | solution.py:53
  157.0 7.8 %collective-permute-start = (f32[64,640]{1,0:T(8,128)S(1)}, f32[64,640]{1,0:T(8,128)S(1)}, u32[]{:S(2)}, u32[]{:S(2)}) collective-permute-start(f32[64,640]{1,0:T(8,128)S(1)} %get-tuple-element.54), channel_id=1, source_target_pairs={{0,16},{16,32},{32,48},{48,0},{1,17},{17,33},{33,49},{49,1},{2,18}... | collective-permute-start | bytes 491528 | tf_op jit(solution)/shard_map/ppermute | solution.py:53
  164.8 4.5 %collective-permute-start.5 = (f32[16,640]{1,0:T(8,128)S(1)}, f32[16,640]{1,0:T(8,128)S(1)}, u32[]{:S(2)}, u32[]{:S(2)}) collective-permute-start(f32[16,640]{1,0:T(8,128)S(1)} %get-tuple-element.67), channel_id=1, source_target_pairs={{0,192},{64,0},{128,64},{192,128},{1,193},{65,1},{129,65},{193,129... | collective-permute-start | bytes 122888 | tf_op jit(solution)/shard_map/ppermute | solution.py:53
  167.6 5.5 %collective-permute-start.4 = (f32[16,640]{1,0:T(8,128)S(1)}, f32[16,640]{1,0:T(8,128)S(1)}, u32[]{:S(2)}, u32[]{:S(2)}) collective-permute-start(f32[16,640]{1,0:T(8,128)S(1)} %get-tuple-element.68), channel_id=1, source_target_pairs={{0,128},{64,192},{128,0},{192,64},{1,129},{65,193},{129,1},{193,65... | collective-permute-start | bytes 122888 | tf_op jit(solution)/shard_map/ppermute | solution.py:53
  168.4 5.2 %collective-permute-start.3 = (f32[16,640]{1,0:T(8,128)S(1)}, f32[16,640]{1,0:T(8,128)S(1)}, u32[]{:S(2)}, u32[]{:S(2)}) collective-permute-start(f32[16,640]{1,0:T(8,128)S(1)} %get-tuple-element.66), channel_id=1, source_target_pairs={{0,64},{64,128},{128,192},{192,0},{1,65},{65,129},{129,193},{193,1... | collective-permute-start | bytes 122888 | tf_op jit(solution)/shard_map/ppermute | solution.py:53
Sparse Core Ops, SparseCore 0:
  9.8 55.5 all-gather.1
  81.2 22.2 reduce-scatter.2
  107.8 44.5 reduce-scatter.4

commit v6 on v5

--- a/solution.py
+++ b/solution.py
@@ -7,7 +7,7 @@
 TAPS = 7
 DILATION_SIZE = 9
 FRAME_AXES = ("x", "y", "c", "z")
-SCATTER_ORDER = ("c", "z", "y", "x")
+SCATTER_ORDER = ("c", "z", "x", "y")
 EXTRA_COLUMNS = 128
 
 
@@ -149,8 +149,7 @@
     packed = packed.reshape(held * block, C + EXTRA_COLUMNS).astype(jnp.bfloat16)
     packed = lax.psum_scatter(packed, rest[0], scatter_dimension=0, tiled=True)
     packed = packed.astype(jnp.float32)
-    for axis in rest[1:]:
-        packed = permute_scatter(packed, axis)
+    packed = permute_scatter(packed, tuple(rest[1:]))
     conv_grad = packed[:conv_each, :C]
     mix_grad = packed[conv_each:, :C]
     vector_grad = packed[0, C : C + 4 * share].reshape(4, share)

time: 183 us -> 199 us (1.087)
  starting transfers between devices: 9.35 us -> 28.7 us
  waiting for transfers between devices: 105 us -> 101 us
    ppermute x6 -> x15, starting transfers between devices: 9.05 us -> 28.4 us  [permute_scatter(): lax.ppermute(chunk, axis, [(j, (j + step) % n) for j in range(n)])]
    ppermute x6 -> x15, waiting for transfers between devices: 11.1 us -> 7.34 us  [permute_scatter(): lax.ppermute(chunk, axis, [(j, (j + step) % n) for j in range(n)])]
  transfers between devices with their start and end apart: 9 -> 18, of which waited for: 8 -> 7; matrix products, arithmetic and copies ran while one was open for 13% -> 12% of each run, Pallas kernels for 0% -> 0%
where the time goes in v6:
time: 199 us; the launch traced here: 198 us
  waiting for transfers between devices  101 us (51%)
  starting transfers between devices  28.7 us (14%)
  other arithmetic  20.5 us (10%)
  local copies, waits for them, and re-layouts  15.7 us (8%)
  between operations  14.4 us (7%)
  matrix products  13.9 us (7%)
  blocking collectives  3.85 us (2%)
    reduce_scatter x1, waiting for transfers between devices, per_device(): packed = lax.psum_scatter(packed, rest[0], scatter_dimension=0, tiled=True)  44.4 us
    all_gather x1, waiting for transfers between devices, per_device(): gathered = lax.all_gather(both, 'z', axis=0, tiled=True)  42.1 us
    ppermute x15, starting transfers between devices, permute_scatter(): lax.ppermute(chunk, axis, [(j, (j + step) % n) for j in range(n)])  28.4 us
    ppermute x15, waiting for transfers between devices, permute_scatter(): lax.ppermute(chunk, axis, [(j, (j + step) % n) for j in range(n)])  7.34 us
    reduce_scatter x1, waiting for transfers between devices, per_device(): lax.psum_scatter(packed, first_axis, scatter_dimension=0, tiled=True)  6.81 us
    dot_general x1, matrix products, per_device(): lax.dot_general(jnp.concatenate([conv_lhs, mix_lhs], axis=0), jnp.concate...  5.58 us
    dot_general x1, matrix products, per_device(): lax.dot_general(cotangent, mix_full, (((1,), (1,)), ((), ())), preferred_...  4.07 us
  transfers between devices with their start and end apart: 18, of which 7 were waited for; matrix products, arithmetic and copies ran while one was open for 12% of the time, Pallas kernels for 0%

profile of v6, /device:TPU:32, one launch (start us, length us, event | category | flops | bytes accessed | tf_op | source)
XLA Modules:
  0.0 197.8 jit_solution(6938051590928278961)
XLA Ops:
  7.2 1.9 pad_maximum_fusion.1
  10.4 2.8 %fusion.11 = bf16[256,512]{1,0:T(8,128)(2,1)S(1)} fusion(bf16[256,512]{1,0:T(8,128)(2,1)} %param.10, f32[512]{0:T(512)} %param.16), kind=kLoop, calls=%fused_computation.21 | loop fusion | flops 786432 | bytes 526336 | tf_op jit(solution)/shard_map/convert_element_type | solution.py:71
  14.1 1.8 constant_dynamic-update-slice_fusion
  17.6 2.3 %copy.31 = bf16[256,3584]{0,1:T(8,128)(2,1)} copy(bf16[256,3584]{1,0:T(8,128)(2,1)S(1)} %select_dynamic-update-slice_fusion) | data formatting | bytes 3670016 | tf_op jit(solution)/shard_map/concatenate | solution.py:79
  19.8 2.5 %reshape.132 = bf16[256,256,14]{0,2,1:T(8,128)(2,1)S(1)} reshape(bf16[256,3584]{0,1:T(8,128)(2,1)} %copy.31) | data formatting | bytes 3670016 | tf_op jit(solution)/shard_map/reshape | solution.py:125
  23.3 42.1 %all-gather.2.cloned.1.call-done = bf16[4096,512]{1,0:T(8,128)(2,1)} async-done(((bf16[512,512]{1,0:T(8,128)(2,1)}), bf16[4096,512]{1,0:T(8,128)(2,1)}) %all-gather.2.cloned.1.call-update) | async-done | bytes 4194320 | tf_op jit(solution)/shard_map/all_gather | solution.py:65
  65.4 2.4 %slice.163 = bf16[8,448,512]{2,1,0:T(8,128)(2,1)S(1)} slice(bf16[8,512,512]{2,1,0:T(8,128)(2,1)} %bitcast.46), slice={[0:8], [0:448], [0:512]} | slice | bytes 7340032 | tf_op jit(solution)/shard_map/slice | solution.py:67
  70.4 4.1 %convert_reduce_fusion.1 = (f32[512]{0:T(512)S(1)}, bf16[256,512]{1,0:T(8,128)(2,1)S(1)}, f32[512]{0:T(512)S(1)}, bf16[256,512]{1,0:T(8,128)(2,1)S(1)}) fusion(f32[256,512]{1,0:T(8,128)S(1)} %convolution_add_fusion, f32[512]{0:T(512)S(1)} %get-tuple-element.78, f32[512]{0:T(512)S(1)} %get-tuple-element.79, f32[512]{0:T(512)S(1)} %copy-done.6, ...), kind=kOutput, calls=%fused_computation.31 | convolution fusion | flops 136444928 | bytes 1845248 | tf_op jit(solution)/shard_map/dot_general | solution.py:88
  75.5 5.6 %fusion = f32[4096,512]{1,0:T(8,128)} fusion(bf16[256,4096]{0,1:T(8,128)(2,1)S(1)} %bitcast.50, bf16[256,4096]{0,1:T(8,128)(2,1)S(1)} %bitcast.49, bf16[256,512]{1,0:T(8,128)(2,1)S(1)} %copy-done.4, bf16[256,512]{1,0:T(8,128)(2,1)S(1)} %get-tuple-element.44), kind=kOutput, calls=%fused_computation.1 | convolution fusion | flops 2156920832 | bytes 13107200 | tf_op jit(solution)/shard_map/dot_general | solution.py:127
  81.5 3.2 %convolution_convert_fusion = bf16[256,3584]{1,0:T(8,128)(2,1)S(1)} fusion(bf16[256,512]{1,0:T(8,128)(2,1)S(1)} %get-tuple-element.44, bf16[3584,512]{1,0:T(8,128)(2,1)} %bitcast.43), kind=kOutput, calls=%fused_computation | convolution fusion | flops 940441600 | bytes 5767168 | tf_op jit(solution)/shard_map/dot_general | solution.py:92
  85.4 3.9 %fusion.19 = (f32[512]{0:T(512)S(1)}, f32[256,512]{1,0:T(8,128)S(1)}) fusion(bf16[256,512]{1,0:T(8,128)(2,1)S(1)} %copy-done.1, f32[512]{0:T(512)S(1)} %get-tuple-element.81, f32[512]{0:T(512)S(1)} %get-tuple-element.80, f32[512]{0:T(512)S(1)} %copy-done.5, f32[229,512]{1,0:T(8,128)S(1)} %get-tuple-element.98, f32[238,512]{1,0:T(8,128)S(1)} %get-tuple-element.96, ...), kind=kLoop, calls=%fused_computation.37 | loop fusion | flops 2227712 | bytes 3981312 | tf_op jit(solution)/shard_map/reduce_sum | solution.py:109
  89.3 2.5 %convert_reduce_fusion = (f32[512]{0:T(512)S(1)}, bf16[256,512]{1,0:T(8,128)(2,1)}) fusion(bf16[256,512]{1,0:T(8,128)(2,1)S(1)} %copy-done.4, f32[256,512]{1,0:T(8,128)S(1)} %get-tuple-element.46, bf16[256,512]{1,0:T(8,128)(2,1)S(1)} %copy-done.1, f32[512]{0:T(512)S(1)} %get-tuple-element.80), kind=kLoop, calls=%fused_computation.12 | loop fusion | flops 1048064 | bytes 1314816 | tf_op jit(solution)/shard_map/reduce_sum | solution.py:108
  92.4 3.8 %psum.7 = bf16[4,4,2,8,8]{3,2,1,0,4:T(2,128)(2,1)S(1)} all-reduce(f32[4,4,2,8,8]{3,2,1,0,4:T(2,128)S(1)} %reshape.139), channel_id=1, replica_groups=mesh['x'=4,'y'=4,'c'=2,'z'=8] {'c'}, use_global_device_ids=true, to_apply=%region_7.8 | all-reduce | flops 2048 | bytes 12288 | tf_op jit(solution)/shard_map/psum | solution.py:135
  96.6 6.8 %reduce-scatter.3.cloned.1.call-done = f32[2048,512]{1,0:T(8,128)} async-done(((f32[4096,512]{1,0:T(8,128)}), f32[2048,512]{1,0:T(8,128)}) %reduce-scatter.3.cloned.1.call-update) | async-done | bytes 4194320 | tf_op jit(solution)/shard_map/reduce_scatter | solution.py:134
  103.4 2.5 %convert.11 = bf16[2048,512]{1,0:T(8,128)(2,1)S(1)} convert(f32[2048,512]{1,0:T(8,128)} %reduce-scatter.3.cloned.1.call-done) | non-fusion elementwise | flops 1048576 | bytes 6291456 | tf_op jit(solution)/shard_map/convert
  107.9 44.4 %reduce-scatter.5.cloned.1.call-done = bf16[256,640]{1,0:T(8,128)(2,1)} async-done(((bf16[2048,640]{1,0:T(8,128)(2,1)}), bf16[256,640]{1,0:T(8,128)(2,1)}) %reduce-scatter.5.cloned.1.call-update) | async-done | bytes 327696 | tf_op jit(solution)/shard_map/reduce_scatter | solution.py:150
  153.4 5.0 %collective-permute-start.14 = (f32[16,640]{1,0:T(8,128)S(1)}, f32[16,640]{1,0:T(8,128)S(1)}, u32[]{:S(2)}, u32[]{:S(2)}) collective-permute-start(f32[16,640]{1,0:T(8,128)S(1)} %get-tuple-element.55), channel_id=1, source_target_pairs={{0,240},{16,0},{32,16},{48,32},{64,48},{80,64},{96,80},{112,96},{1... | collective-permute-start | bytes 122888 | tf_op jit(solution)/shard_map/ppermute | solution.py:53
  160.9 2.4 %collective-permute-start.10 = (f32[16,640]{1,0:T(8,128)S(1)}, f32[16,640]{1,0:T(8,128)S(1)}, u32[]{:S(2)}, u32[]{:S(2)}) collective-permute-start(f32[16,640]{1,0:T(8,128)S(1)} %get-tuple-element.59), channel_id=1, source_target_pairs={{0,176},{16,192},{32,208},{48,224},{64,240},{80,0},{96,16},{112,32... | collective-permute-start | bytes 122888 | tf_op jit(solution)/shard_map/ppermute | solution.py:53
  163.2 3.9 %collective-permute-start.9 = (f32[16,640]{1,0:T(8,128)S(1)}, f32[16,640]{1,0:T(8,128)S(1)}, u32[]{:S(2)}, u32[]{:S(2)}) collective-permute-start(f32[16,640]{1,0:T(8,128)S(1)} %get-tuple-element.60), channel_id=1, source_target_pairs={{0,160},{16,176},{32,192},{48,208},{64,224},{80,240},{96,0},{112,1... | collective-permute-start | bytes 122888 | tf_op jit(solution)/shard_map/ppermute | solution.py:53
  167.2 2.1 %collective-permute-start.7 = (f32[16,640]{1,0:T(8,128)S(1)}, f32[16,640]{1,0:T(8,128)S(1)}, u32[]{:S(2)}, u32[]{:S(2)}) collective-permute-start(f32[16,640]{1,0:T(8,128)S(1)} %get-tuple-element.62), channel_id=1, source_target_pairs={{0,128},{16,144},{32,160},{48,176},{64,192},{80,208},{96,224},{112... | collective-permute-start | bytes 122888 | tf_op jit(solution)/shard_map/ppermute | solution.py:53
  169.3 2.1 %collective-permute-start.6 = (f32[16,640]{1,0:T(8,128)S(1)}, f32[16,640]{1,0:T(8,128)S(1)}, u32[]{:S(2)}, u32[]{:S(2)}) collective-permute-start(f32[16,640]{1,0:T(8,128)S(1)} %get-tuple-element.63), channel_id=1, source_target_pairs={{0,112},{16,128},{32,144},{48,160},{64,176},{80,192},{96,208},{112... | collective-permute-start | bytes 122888 | tf_op jit(solution)/shard_map/ppermute | solution.py:53
  171.4 3.0 %collective-permute-start.5 = (f32[16,640]{1,0:T(8,128)S(1)}, f32[16,640]{1,0:T(8,128)S(1)}, u32[]{:S(2)}, u32[]{:S(2)}) collective-permute-start(f32[16,640]{1,0:T(8,128)S(1)} %get-tuple-element.64), channel_id=1, source_target_pairs={{0,96},{16,112},{32,128},{48,144},{64,160},{80,176},{96,192},{112,... | collective-permute-start | bytes 122888 | tf_op jit(solution)/shard_map/ppermute | solution.py:53
  176.9 3.3 %collective-permute-start.2 = (f32[16,640]{1,0:T(8,128)S(1)}, f32[16,640]{1,0:T(8,128)S(1)}, u32[]{:S(2)}, u32[]{:S(2)}) collective-permute-start(f32[16,640]{1,0:T(8,128)S(1)} %get-tuple-element.67), channel_id=1, source_target_pairs={{0,48},{16,64},{32,80},{48,96},{64,112},{80,128},{96,144},{112,160... | collective-permute-start | bytes 122888 | tf_op jit(solution)/shard_map/ppermute | solution.py:53
  183.6 4.3 %collective-permute-done.1 = f32[16,640]{1,0:T(8,128)S(1)} collective-permute-done((f32[16,640]{1,0:T(8,128)S(1)}, f32[16,640]{1,0:T(8,128)S(1)}, u32[]{:S(2)}, u32[]{:S(2)}) %collective-permute-start.1) | collective-permute-done | bytes 40992 | tf_op jit(solution)/shard_map/ppermute | solution.py:53
  (94 shorter events, 24.8 us)
Async XLA Ops:
  7.2 58.2 %all-gather.2.cloned.1.call-start = ((), (), s32[]{:S(2)}) async-start(), calls=%async_computation.2 | async-start | bytes 4718592 | tf_op jit(solution)/shard_map/all_gather | solution.py:65
  9.2 94.3 %reduce-scatter.3.cloned.1.call-start = ((), (), s32[]{:S(2)}) async-start(), calls=%async_computation.3 | async-start | bytes 12582912 | tf_op jit(solution)/shard_map/reduce_scatter | solution.py:134
  13.2 1.0 copy-start.1
  16.3 1.2 copy-start.2
  65.4 3.9 %copy-start.3 = (bf16[256,3584]{1,0:T(8,128)(2,1)S(1)}, bf16[256,3584]{1,0:T(8,128)(2,1)}, u32[]{:S(2)}) copy-start(bf16[256,3584]{1,0:T(8,128)(2,1)} %copy-done.2) | copy-start | bytes 5505028
  65.4 3.9 %copy-start.7 = (f32[512]{0:T(512)S(1)}, f32[512]{0:T(512)}, u32[]{:S(2)}) copy-start(f32[512]{0:T(512)} %param.15) | copy-start | bytes 6148
  67.8 2.6 %copy-start = (bf16[8,448,512]{2,1,0:T(8,128)(2,1)}, bf16[8,448,512]{2,1,0:T(8,128)(2,1)S(1)}, u32[]{:S(2)}) copy-start(bf16[8,448,512]{2,1,0:T(8,128)(2,1)S(1)} %slice.163) | copy-start | bytes 11010052
  69.3 1.1 copy-start.4
  81.1 71.3 %reduce-scatter.5.cloned.1.call-start = ((), (), s32[]{:S(2)}) async-start(), calls=%async_computation.4 | async-start | bytes 2949120 | tf_op jit(solution)/shard_map/reduce_scatter | solution.py:150
  153.4 9.8 %collective-permute-start.14 = (f32[16,640]{1,0:T(8,128)S(1)}, f32[16,640]{1,0:T(8,128)S(1)}, u32[]{:S(2)}, u32[]{:S(2)}) collective-permute-start(f32[16,640]{1,0:T(8,128)S(1)} %get-tuple-element.55), channel_id=1, source_target_pairs={{0,240},{16,0},{32,16},{48,32},{64,48},{80,64},{96,80},{112,96},{1... | collective-permute-start | bytes 122888 | tf_op jit(solution)/shard_map/ppermute | solution.py:53
  158.4 8.8 %collective-permute-start.13 = (f32[16,640]{1,0:T(8,128)S(1)}, f32[16,640]{1,0:T(8,128)S(1)}, u32[]{:S(2)}, u32[]{:S(2)}) collective-permute-start(f32[16,640]{1,0:T(8,128)S(1)} %get-tuple-element.56), channel_id=1, source_target_pairs={{0,224},{16,240},{32,0},{48,16},{64,32},{80,48},{96,64},{112,80},{... | collective-permute-start | bytes 122888 | tf_op jit(solution)/shard_map/ppermute | solution.py:53
  159.1 8.1 %collective-permute-start.12 = (f32[16,640]{1,0:T(8,128)S(1)}, f32[16,640]{1,0:T(8,128)S(1)}, u32[]{:S(2)}, u32[]{:S(2)}) collective-permute-start(f32[16,640]{1,0:T(8,128)S(1)} %get-tuple-element.57), channel_id=1, source_target_pairs={{0,208},{16,224},{32,240},{48,0},{64,16},{80,32},{96,48},{112,64},... | collective-permute-start | bytes 122888 | tf_op jit(solution)/shard_map/ppermute | solution.py:53
  160.3 9.0 %collective-permute-start.11 = (f32[16,640]{1,0:T(8,128)S(1)}, f32[16,640]{1,0:T(8,128)S(1)}, u32[]{:S(2)}, u32[]{:S(2)}) collective-permute-start(f32[16,640]{1,0:T(8,128)S(1)} %get-tuple-element.58), channel_id=1, source_target_pairs={{0,192},{16,208},{32,224},{48,240},{64,0},{80,16},{96,32},{112,48}... | collective-permute-start | bytes 122888 | tf_op jit(solution)/shard_map/ppermute | solution.py:53
  160.9 10.6 %collective-permute-start.10 = (f32[16,640]{1,0:T(8,128)S(1)}, f32[16,640]{1,0:T(8,128)S(1)}, u32[]{:S(2)}, u32[]{:S(2)}) collective-permute-start(f32[16,640]{1,0:T(8,128)S(1)} %get-tuple-element.59), channel_id=1, source_target_pairs={{0,176},{16,192},{32,208},{48,224},{64,240},{80,0},{96,16},{112,32... | collective-permute-start | bytes 122888 | tf_op jit(solution)/shard_map/ppermute | solution.py:53
  163.2 11.2 %collective-permute-start.9 = (f32[16,640]{1,0:T(8,128)S(1)}, f32[16,640]{1,0:T(8,128)S(1)}, u32[]{:S(2)}, u32[]{:S(2)}) collective-permute-start(f32[16,640]{1,0:T(8,128)S(1)} %get-tuple-element.60), channel_id=1, source_target_pairs={{0,160},{16,176},{32,192},{48,208},{64,224},{80,240},{96,0},{112,1... | collective-permute-start | bytes 122888 | tf_op jit(solution)/shard_map/ppermute | solution.py:53
  167.2 8.2 %collective-permute-start.8 = (f32[16,640]{1,0:T(8,128)S(1)}, f32[16,640]{1,0:T(8,128)S(1)}, u32[]{:S(2)}, u32[]{:S(2)}) collective-permute-start(f32[16,640]{1,0:T(8,128)S(1)} %get-tuple-element.61), channel_id=1, source_target_pairs={{0,144},{16,160},{32,176},{48,192},{64,208},{80,224},{96,240},{112... | collective-permute-start | bytes 122888 | tf_op jit(solution)/shard_map/ppermute | solution.py:53
  167.2 9.7 %collective-permute-start.7 = (f32[16,640]{1,0:T(8,128)S(1)}, f32[16,640]{1,0:T(8,128)S(1)}, u32[]{:S(2)}, u32[]{:S(2)}) collective-permute-start(f32[16,640]{1,0:T(8,128)S(1)} %get-tuple-element.62), channel_id=1, source_target_pairs={{0,128},{16,144},{32,160},{48,176},{64,192},{80,208},{96,224},{112... | collective-permute-start | bytes 122888 | tf_op jit(solution)/shard_map/ppermute | solution.py:53
  169.3 10.9 %collective-permute-start.6 = (f32[16,640]{1,0:T(8,128)S(1)}, f32[16,640]{1,0:T(8,128)S(1)}, u32[]{:S(2)}, u32[]{:S(2)}) collective-permute-start(f32[16,640]{1,0:T(8,128)S(1)} %get-tuple-element.63), channel_id=1, source_target_pairs={{0,112},{16,128},{32,144},{48,160},{64,176},{80,192},{96,208},{112... | collective-permute-start | bytes 122888 | tf_op jit(solution)/shard_map/ppermute | solution.py:53
  171.4 10.5 %collective-permute-start.5 = (f32[16,640]{1,0:T(8,128)S(1)}, f32[16,640]{1,0:T(8,128)S(1)}, u32[]{:S(2)}, u32[]{:S(2)}) collective-permute-start(f32[16,640]{1,0:T(8,128)S(1)} %get-tuple-element.64), channel_id=1, source_target_pairs={{0,96},{16,112},{32,128},{48,144},{64,160},{80,176},{96,192},{112,... | collective-permute-start | bytes 122888 | tf_op jit(solution)/shard_map/ppermute | solution.py:53
  174.4 7.6 %collective-permute-start.4 = (f32[16,640]{1,0:T(8,128)S(1)}, f32[16,640]{1,0:T(8,128)S(1)}, u32[]{:S(2)}, u32[]{:S(2)}) collective-permute-start(f32[16,640]{1,0:T(8,128)S(1)} %get-tuple-element.65), channel_id=1, source_target_pairs={{0,80},{16,96},{32,112},{48,128},{64,144},{80,160},{96,176},{112,1... | collective-permute-start | bytes 122888 | tf_op jit(solution)/shard_map/ppermute | solution.py:53
  175.4 6.7 %collective-permute-start.3 = (f32[16,640]{1,0:T(8,128)S(1)}, f32[16,640]{1,0:T(8,128)S(1)}, u32[]{:S(2)}, u32[]{:S(2)}) collective-permute-start(f32[16,640]{1,0:T(8,128)S(1)} %get-tuple-element.66), channel_id=1, source_target_pairs={{0,64},{16,80},{32,96},{48,112},{64,128},{80,144},{96,160},{112,17... | collective-permute-start | bytes 122888 | tf_op jit(solution)/shard_map/ppermute | solution.py:53
  176.9 6.6 %collective-permute-start.2 = (f32[16,640]{1,0:T(8,128)S(1)}, f32[16,640]{1,0:T(8,128)S(1)}, u32[]{:S(2)}, u32[]{:S(2)}) collective-permute-start(f32[16,640]{1,0:T(8,128)S(1)} %get-tuple-element.67), channel_id=1, source_target_pairs={{0,48},{16,64},{32,80},{48,96},{64,112},{80,128},{96,144},{112,160... | collective-permute-start | bytes 122888 | tf_op jit(solution)/shard_map/ppermute | solution.py:53
  180.2 7.6 %collective-permute-start.1 = (f32[16,640]{1,0:T(8,128)S(1)}, f32[16,640]{1,0:T(8,128)S(1)}, u32[]{:S(2)}, u32[]{:S(2)}) collective-permute-start(f32[16,640]{1,0:T(8,128)S(1)} %get-tuple-element.68), channel_id=1, source_target_pairs={{0,32},{16,48},{32,64},{48,80},{64,96},{80,112},{96,128},{112,144}... | collective-permute-start | bytes 122888 | tf_op jit(solution)/shard_map/ppermute | solution.py:53
  181.9 7.3 %collective-permute-start = (f32[16,640]{1,0:T(8,128)S(1)}, f32[16,640]{1,0:T(8,128)S(1)}, u32[]{:S(2)}, u32[]{:S(2)}) collective-permute-start(f32[16,640]{1,0:T(8,128)S(1)} %get-tuple-element.54), channel_id=1, source_target_pairs={{0,16},{16,32},{32,48},{48,64},{64,80},{80,96},{96,112},{112,128},... | collective-permute-start | bytes 122888 | tf_op jit(solution)/shard_map/ppermute | solution.py:53
  (2 other events, 1.6 us)
Sparse Core Ops, SparseCore 0:
  9.8 55.5 all-gather.1
  81.2 22.2 reduce-scatter.2
  107.8 44.5 reduce-scatter.4

commit v7 on v5

--- a/solution.py
+++ b/solution.py
@@ -130,26 +130,28 @@
         (((0,), (0,)), ((), ())),
         preferred_element_type=jnp.float32,
     )
-    first_axis, *rest = SCATTER_ORDER
+    first_axis, second_axis, *rest = SCATTER_ORDER
     packed = lax.psum_scatter(packed, first_axis, scatter_dimension=0, tiled=True)
+    packed = lax.psum_scatter(packed.astype(jnp.bfloat16), second_axis, scatter_dimension=0, tiled=True)
+    packed = packed.astype(jnp.float32)
     vectors = lax.psum(vectors, first_axis)
+    vectors = lax.psum(vectors, second_axis)
     block = conv_each + mix_each
     held = packed.shape[0] // block
     share = vectors.shape[1] // devices
     vec_blocks = vectors.reshape(4, devices, share).transpose(1, 0, 2).reshape(*sizes, 4 * share)
-    order_rest = [FRAME_AXES.index(a) for a in rest]
-    mine = lax.axis_index(first_axis)
-    vec_blocks = jnp.take(vec_blocks, mine, axis=FRAME_AXES.index(first_axis))
-    kept = [FRAME_AXES.index(a) for a in FRAME_AXES if a != first_axis]
-    vec_blocks = vec_blocks.transpose(*[kept.index(o) for o in order_rest], len(kept))
+    kept_names = list(FRAME_AXES)
+    for axis in (first_axis, second_axis):
+        position = kept_names.index(axis)
+        vec_blocks = jnp.take(vec_blocks, lax.axis_index(axis), axis=position)
+        kept_names.pop(position)
+    vec_blocks = vec_blocks.transpose(*[kept_names.index(a) for a in rest], len(kept_names))
     vec_blocks = vec_blocks.reshape(held, 4 * share)
     extra = jnp.zeros((held, block, EXTRA_COLUMNS), jnp.float32)
     extra = extra.at[:, 0, : 4 * share].set(vec_blocks)
     packed = jnp.concatenate([packed.reshape(held, block, C), extra], axis=2)
-    packed = packed.reshape(held * block, C + EXTRA_COLUMNS).astype(jnp.bfloat16)
-    packed = lax.psum_scatter(packed, rest[0], scatter_dimension=0, tiled=True)
-    packed = packed.astype(jnp.float32)
-    for axis in rest[1:]:
+    packed = packed.reshape(held * block, C + EXTRA_COLUMNS)
+    for axis in rest:
         packed = permute_scatter(packed, axis)
     conv_grad = packed[:conv_each, :C]
     mix_grad = packed[conv_each:, :C]

time: 183 us -> 183 us (level)
  blocking collectives: 3.85 us -> 33.7 us
  waiting for transfers between devices: 105 us -> 75.7 us
    reduce_scatter x1, waiting for transfers between devices: 44.6 us -> 0.02 us  [per_device(): lax.psum_scatter(packed.astype(jnp.bfloat16), second_axis, scatter_dimens...]
    psum x0 -> x1, blocking collectives: none -> 31.2 us  [per_device(): vectors = lax.psum(vectors, second_axis)]
    reduce_scatter x1, waiting for transfers between devices: 6.8 us -> 22.1 us  [per_device(): lax.psum_scatter(packed, first_axis, scatter_dimension=0, tiled=True)]
    convert_element_type x0 -> x1, other arithmetic: none -> 3.8 us  [per_device(): packed.astype(jnp.bfloat16)]
    another operation x3 -> x1, other arithmetic: 3.38 us -> 0.83 us
  transfers between devices with their start and end apart: 9 -> 9, of which waited for: 8 -> 7; matrix products, arithmetic and copies ran while one was open for 13% -> 13% of each run, Pallas kernels for 0% -> 0%
where the time goes in v7:
time: 183 us; the launch traced here: 182 us
  waiting for transfers between devices  75.7 us (41%)
  blocking collectives  33.7 us (18%)
  other arithmetic  20.2 us (11%)
  local copies, waits for them, and re-layouts  15.6 us (9%)
  between operations  14.1 us (8%)
  matrix products  13.9 us (8%)
  starting transfers between devices  8.86 us (5%)
    all_gather x1, waiting for transfers between devices, per_device(): gathered = lax.all_gather(both, 'z', axis=0, tiled=True)  42 us
    psum x1, blocking collectives, per_device(): vectors = lax.psum(vectors, second_axis)  31.2 us
    reduce_scatter x1, waiting for transfers between devices, per_device(): lax.psum_scatter(packed, first_axis, scatter_dimension=0, tiled=True)  22.1 us
    ppermute x6, waiting for transfers between devices, permute_scatter(): lax.ppermute(chunk, axis, [(j, (j + step) % n) for j in range(n)])  11.5 us
    ppermute x6, starting transfers between devices, permute_scatter(): lax.ppermute(chunk, axis, [(j, (j + step) % n) for j in range(n)])  8.56 us
    dot_general x1, matrix products, per_device(): lax.dot_general(jnp.concatenate([conv_lhs, mix_lhs], axis=0), jnp.concate...  5.59 us
    dot_general x1, matrix products, per_device(): lax.dot_general(cotangent, mix_full, (((1,), (1,)), ((), ())), preferred_...  4.06 us
    reduce_sum x1, other arithmetic, per_device(): jnp.sum(d_first * dalpha_in, axis=0)  3.87 us
  transfers between devices with their start and end apart: 9, of which 7 were waited for; matrix products, arithmetic and copies ran while one was open for 13% of the time, Pallas kernels for 0%

profile of v7, /device:TPU:32, one launch (start us, length us, event | category | flops | bytes accessed | tf_op | source)
XLA Modules:
  0.0 182.2 jit_solution(12821313407173074665)
XLA Ops:
  7.2 1.9 %pad_maximum_fusion = bf16[512,512]{1,0:T(8,128)(2,1)} fusion(bf16[64,512]{1,0:T(8,128)(2,1)} %param.14, bf16[448,512]{1,0:T(8,128)(2,1)} %param.13), kind=kLoop, calls=%fused_computation.33 | loop fusion | flops 1048576 | bytes 1048576 | tf_op jit(solution)/shard_map/concatenate | solution.py:64
  10.4 2.8 %fusion.11 = bf16[256,512]{1,0:T(8,128)(2,1)S(1)} fusion(bf16[256,512]{1,0:T(8,128)(2,1)} %param.10, f32[512]{0:T(512)} %param.16), kind=kLoop, calls=%fused_computation.28 | loop fusion | flops 786432 | bytes 526336 | tf_op jit(solution)/shard_map/convert_element_type | solution.py:71
  14.2 1.8 %constant_dynamic-update-slice_fusion = bf16[256,3584]{1,0:T(8,128)(2,1)S(1)} fusion(bf16[256,3584]{1,0:T(8,128)(2,1)S(1)} %select_dynamic-update-slice_fusion.3, f32[512]{0:T(512)S(1)} %copy-done.5, bf16[256,512]{1,0:T(8,128)(2,1)S(1)} %copy-done.1), kind=kLoop, calls=%fused_computation.67 | loop fusion | flops 786432 | bytes 526336
  16.4 1.2 copy-done.2
  17.6 2.3 %copy.34 = bf16[256,3584]{0,1:T(8,128)(2,1)} copy(bf16[256,3584]{1,0:T(8,128)(2,1)S(1)} %select_dynamic-update-slice_fusion) | data formatting | bytes 3670016 | tf_op jit(solution)/shard_map/concatenate | solution.py:79
  19.9 2.5 %reshape.131 = bf16[256,256,14]{0,2,1:T(8,128)(2,1)S(1)} reshape(bf16[256,3584]{0,1:T(8,128)(2,1)} %copy.34) | data formatting | bytes 3670016 | tf_op jit(solution)/shard_map/reshape | solution.py:125
  23.3 42.0 %all-gather.2.cloned.1.call-done = bf16[4096,512]{1,0:T(8,128)(2,1)} async-done(((bf16[512,512]{1,0:T(8,128)(2,1)}), bf16[4096,512]{1,0:T(8,128)(2,1)}) %all-gather.2.cloned.1.call-update) | async-done | bytes 4194320 | tf_op jit(solution)/shard_map/all_gather | solution.py:65
  65.4 2.4 %slice.174 = bf16[8,448,512]{2,1,0:T(8,128)(2,1)S(1)} slice(bf16[8,512,512]{2,1,0:T(8,128)(2,1)} %bitcast.49), slice={[0:8], [0:448], [0:512]} | slice | bytes 7340032 | tf_op jit(solution)/shard_map/slice | solution.py:67
  67.8 1.5 slice.167
  70.4 4.1 %convert_reduce_fusion.1 = (f32[512]{0:T(512)S(1)}, bf16[256,512]{1,0:T(8,128)(2,1)S(1)}, f32[512]{0:T(512)S(1)}, bf16[256,512]{1,0:T(8,128)(2,1)S(1)}) fusion(f32[256,512]{1,0:T(8,128)S(1)} %convolution_add_fusion, f32[512]{0:T(512)S(1)} %get-tuple-element.80, f32[512]{0:T(512)S(1)} %get-tuple-element.81, f32[512]{0:T(512)S(1)} %copy-done.6, ...), kind=kOutput, calls=%fused_computation.38 | convolution fusion | flops 136444928 | bytes 1845248 | tf_op jit(solution)/shard_map/dot_general | solution.py:88
  75.5 5.6 %fusion = f32[4096,512]{1,0:T(8,128)} fusion(bf16[256,4096]{0,1:T(8,128)(2,1)S(1)} %bitcast.52, bf16[256,4096]{0,1:T(8,128)(2,1)S(1)} %bitcast.51, bf16[256,512]{1,0:T(8,128)(2,1)S(1)} %copy-done.4, bf16[256,512]{1,0:T(8,128)(2,1)S(1)} %get-tuple-element.55), kind=kOutput, calls=%fused_computation.1 | convolution fusion | flops 2156920832 | bytes 13107200 | tf_op jit(solution)/shard_map/dot_general | solution.py:127
  81.3 22.1 %reduce-scatter.3.cloned.1.call-done = f32[2048,512]{1,0:T(8,128)} async-done(((f32[4096,512]{1,0:T(8,128)}), f32[2048,512]{1,0:T(8,128)}) %reduce-scatter.3.cloned.1.call-update) | async-done | bytes 4194320 | tf_op jit(solution)/shard_map/reduce_scatter | solution.py:134
  103.4 3.8 %convert_element_type.70 = bf16[2048,512]{1,0:T(8,128)(2,1)} convert(f32[2048,512]{1,0:T(8,128)} %reduce-scatter.3.cloned.1.call-done) | non-fusion elementwise | flops 1048576 | bytes 6291456 | tf_op jit(solution)/shard_map/convert_element_type | solution.py:135
  107.5 3.2 %convolution_convert_fusion = bf16[256,3584]{1,0:T(8,128)(2,1)S(1)} fusion(bf16[256,512]{1,0:T(8,128)(2,1)S(1)} %get-tuple-element.55, bf16[3584,512]{1,0:T(8,128)(2,1)} %bitcast.46), kind=kOutput, calls=%fused_computation | convolution fusion | flops 940441600 | bytes 5767168 | tf_op jit(solution)/shard_map/dot_general | solution.py:92
  111.4 3.9 %fusion.19 = (f32[512]{0:T(512)S(1)}, f32[256,512]{1,0:T(8,128)S(1)}) fusion(bf16[256,512]{1,0:T(8,128)(2,1)S(1)} %copy-done.1, f32[512]{0:T(512)S(1)} %get-tuple-element.83, f32[512]{0:T(512)S(1)} %get-tuple-element.82, f32[512]{0:T(512)S(1)} %copy-done.5, f32[229,512]{1,0:T(8,128)S(1)} %get-tuple-element.100, f32[238,512]{1,0:T(8,128)S(1)} %get-tuple-element.98, ...), kind=kLoop, calls=%fused_computation.44 | loop fusion | flops 2227712 | bytes 3981312 | tf_op jit(solution)/shard_map/reduce_sum | solution.py:109
  115.2 2.5 %convert_reduce_fusion = (f32[512]{0:T(512)S(1)}, bf16[256,512]{1,0:T(8,128)(2,1)}) fusion(bf16[256,512]{1,0:T(8,128)(2,1)S(1)} %copy-done.4, f32[256,512]{1,0:T(8,128)S(1)} %get-tuple-element.57, bf16[256,512]{1,0:T(8,128)(2,1)S(1)} %copy-done.1, f32[512]{0:T(512)S(1)} %get-tuple-element.82), kind=kLoop, calls=%fused_computation.19 | loop fusion | flops 1048064 | bytes 1314816 | tf_op jit(solution)/shard_map/reduce_sum | solution.py:108
  117.8 2.5 %psum.14 = f32[4,512]{1,0:T(4,128)S(1)} all-reduce(f32[4,512]{1,0:T(4,128)S(1)} %pad_maximum_fusion.1), channel_id=1, replica_groups=mesh['x'=4,'y'=4,'c'=2,'z'=8] {'c'}, use_global_device_ids=true, to_apply=%region_8.9 | all-reduce | flops 2048 | bytes 16384 | tf_op jit(solution)/shard_map/psum | solution.py:137
  120.8 31.2 %psum.15 = f32[4,4,2,8,8]{3,2,1,0,4:T(2,128)S(1)} all-reduce(f32[4,4,2,8,8]{3,2,1,0,4:T(2,128)S(1)} %reshape.138), channel_id=1, replica_groups=mesh['x'=4,'y'=4,'c'=2,'z'=8] {'z'}, use_global_device_ids=true, to_apply=%region_9.10 | all-reduce | flops 2048 | bytes 16384 | tf_op jit(solution)/shard_map/psum | solution.py:138
  153.5 3.0 %collective-permute-start.2 = (f32[64,640]{1,0:T(8,128)S(1)}, f32[64,640]{1,0:T(8,128)S(1)}, u32[]{:S(2)}, u32[]{:S(2)}) collective-permute-start(f32[64,640]{1,0:T(8,128)S(1)} %get-tuple-element.67), channel_id=1, source_target_pairs={{0,48},{16,0},{32,16},{48,32},{1,49},{17,1},{33,17},{49,33},{2,50}... | collective-permute-start | bytes 491528 | tf_op jit(solution)/shard_map/ppermute | solution.py:53
  157.9 3.3 %collective-permute-done.2 = f32[64,640]{1,0:T(8,128)S(1)} collective-permute-done((f32[64,640]{1,0:T(8,128)S(1)}, f32[64,640]{1,0:T(8,128)S(1)}, u32[]{:S(2)}, u32[]{:S(2)}) %collective-permute-start.2) | collective-permute-done | bytes 163872 | tf_op jit(solution)/shard_map/ppermute | solution.py:53
  161.2 2.3 %collective-permute-done.1 = f32[64,640]{1,0:T(8,128)S(1)} collective-permute-done((f32[64,640]{1,0:T(8,128)S(1)}, f32[64,640]{1,0:T(8,128)S(1)}, u32[]{:S(2)}, u32[]{:S(2)}) %collective-permute-start.1) | collective-permute-done | bytes 163872 | tf_op jit(solution)/shard_map/ppermute | solution.py:53
  163.5 1.7 collective-permute-done
  165.2 2.4 %collective-permute-start.5 = (f32[16,640]{1,0:T(8,128)S(1)}, f32[16,640]{1,0:T(8,128)S(1)}, u32[]{:S(2)}, u32[]{:S(2)}) collective-permute-start(f32[16,640]{1,0:T(8,128)S(1)} %get-tuple-element.78), channel_id=1, source_target_pairs={{0,192},{64,0},{128,64},{192,128},{1,193},{65,1},{129,65},{193,129... | collective-permute-start | bytes 122888 | tf_op jit(solution)/shard_map/ppermute | solution.py:53
  169.4 3.7 %collective-permute-done.4 = f32[16,640]{1,0:T(8,128)S(1)} collective-permute-done((f32[16,640]{1,0:T(8,128)S(1)}, f32[16,640]{1,0:T(8,128)S(1)}, u32[]{:S(2)}, u32[]{:S(2)}) %collective-permute-start.4) | collective-permute-done | bytes 40992 | tf_op jit(solution)/shard_map/ppermute | solution.py:53
  (76 shorter events, 14.3 us)
Async XLA Ops:
  7.2 58.2 %all-gather.2.cloned.1.call-start = ((), (), s32[]{:S(2)}) async-start(), calls=%async_computation.2 | async-start | bytes 4718592 | tf_op jit(solution)/shard_map/all_gather | solution.py:65
  9.2 94.3 %reduce-scatter.3.cloned.1.call-start = ((), (), s32[]{:S(2)}) async-start(), calls=%async_computation.3 | async-start | bytes 12582912 | tf_op jit(solution)/shard_map/reduce_scatter | solution.py:134
  13.2 1.0 copy-start.1
  13.2 0.9 copy-start.5
  16.4 1.3 copy-start.2
  22.6 0.7 copy-start.6
  65.4 3.9 %copy-start.3 = (bf16[256,3584]{1,0:T(8,128)(2,1)S(1)}, bf16[256,3584]{1,0:T(8,128)(2,1)}, u32[]{:S(2)}) copy-start(bf16[256,3584]{1,0:T(8,128)(2,1)} %copy-done.2) | copy-start | bytes 5505028
  65.4 3.9 %copy-start.7 = (f32[512]{0:T(512)S(1)}, f32[512]{0:T(512)}, u32[]{:S(2)}) copy-start(f32[512]{0:T(512)} %param.15) | copy-start | bytes 6148
  67.8 2.6 %copy-start = (bf16[8,448,512]{2,1,0:T(8,128)(2,1)}, bf16[8,448,512]{2,1,0:T(8,128)(2,1)S(1)}, u32[]{:S(2)}) copy-start(bf16[8,448,512]{2,1,0:T(8,128)(2,1)S(1)} %slice.174) | copy-start | bytes 11010052
  69.3 1.1 copy-start.4
  81.1 71.4 %reduce-scatter.5.cloned.1.call-start = ((), (), s32[]{:S(2)}) async-start(), calls=%async_computation.4 | async-start | bytes 2359296 | tf_op jit(solution)/shard_map/reduce_scatter | solution.py:135
  153.5 7.7 %collective-permute-start.2 = (f32[64,640]{1,0:T(8,128)S(1)}, f32[64,640]{1,0:T(8,128)S(1)}, u32[]{:S(2)}, u32[]{:S(2)}) collective-permute-start(f32[64,640]{1,0:T(8,128)S(1)} %get-tuple-element.67), channel_id=1, source_target_pairs={{0,48},{16,0},{32,16},{48,32},{1,49},{17,1},{33,17},{49,33},{2,50}... | collective-permute-start | bytes 491528 | tf_op jit(solution)/shard_map/ppermute | solution.py:53
  156.6 6.9 %collective-permute-start.1 = (f32[64,640]{1,0:T(8,128)S(1)}, f32[64,640]{1,0:T(8,128)S(1)}, u32[]{:S(2)}, u32[]{:S(2)}) collective-permute-start(f32[64,640]{1,0:T(8,128)S(1)} %get-tuple-element.66), channel_id=1, source_target_pairs={{0,32},{16,48},{32,0},{48,16},{1,33},{17,49},{33,1},{49,17},{2,34}... | collective-permute-start | bytes 491528 | tf_op jit(solution)/shard_map/ppermute | solution.py:53
  157.2 7.9 %collective-permute-start = (f32[64,640]{1,0:T(8,128)S(1)}, f32[64,640]{1,0:T(8,128)S(1)}, u32[]{:S(2)}, u32[]{:S(2)}) collective-permute-start(f32[64,640]{1,0:T(8,128)S(1)} %get-tuple-element.65), channel_id=1, source_target_pairs={{0,16},{16,32},{32,48},{48,0},{1,17},{17,33},{33,49},{49,1},{2,18}... | collective-permute-start | bytes 491528 | tf_op jit(solution)/shard_map/ppermute | solution.py:53
  165.2 4.2 %collective-permute-start.5 = (f32[16,640]{1,0:T(8,128)S(1)}, f32[16,640]{1,0:T(8,128)S(1)}, u32[]{:S(2)}, u32[]{:S(2)}) collective-permute-start(f32[16,640]{1,0:T(8,128)S(1)} %get-tuple-element.78), channel_id=1, source_target_pairs={{0,192},{64,0},{128,64},{192,128},{1,193},{65,1},{129,65},{193,129... | collective-permute-start | bytes 122888 | tf_op jit(solution)/shard_map/ppermute | solution.py:53
  167.6 5.5 %collective-permute-start.4 = (f32[16,640]{1,0:T(8,128)S(1)}, f32[16,640]{1,0:T(8,128)S(1)}, u32[]{:S(2)}, u32[]{:S(2)}) collective-permute-start(f32[16,640]{1,0:T(8,128)S(1)} %get-tuple-element.79), channel_id=1, source_target_pairs={{0,128},{64,192},{128,0},{192,64},{1,129},{65,193},{129,1},{193,65... | collective-permute-start | bytes 122888 | tf_op jit(solution)/shard_map/ppermute | solution.py:53
  168.4 5.2 %collective-permute-start.3 = (f32[16,640]{1,0:T(8,128)S(1)}, f32[16,640]{1,0:T(8,128)S(1)}, u32[]{:S(2)}, u32[]{:S(2)}) collective-permute-start(f32[16,640]{1,0:T(8,128)S(1)} %get-tuple-element.77), channel_id=1, source_target_pairs={{0,64},{64,128},{128,192},{192,0},{1,65},{65,129},{129,193},{193,1... | collective-permute-start | bytes 122888 | tf_op jit(solution)/shard_map/ppermute | solution.py:53
Sparse Core Ops, SparseCore 0:
  9.8 55.5 all-gather.1
  81.2 22.2 reduce-scatter.2
  107.4 44.1 reduce-scatter.4

commit v8 on v7

--- a/solution.py
+++ b/solution.py
@@ -132,9 +132,10 @@
     )
     first_axis, second_axis, *rest = SCATTER_ORDER
     packed = lax.psum_scatter(packed, first_axis, scatter_dimension=0, tiled=True)
+    vectors = lax.psum(vectors, first_axis)
+    packed, vectors = lax.optimization_barrier((packed, vectors))
     packed = lax.psum_scatter(packed.astype(jnp.bfloat16), second_axis, scatter_dimension=0, tiled=True)
     packed = packed.astype(jnp.float32)
-    vectors = lax.psum(vectors, first_axis)
     vectors = lax.psum(vectors, second_axis)
     block = conv_each + mix_each
     held = packed.shape[0] // block

time: 183 us -> 180 us (0.984)
  waiting for transfers between devices: 75.7 us -> 69.6 us
  starting transfers between devices: 8.86 us -> 12.1 us
    reduce_scatter x1, waiting for transfers between devices: 22.1 us -> 9.09 us  [per_device(): lax.psum_scatter(packed, first_axis, scatter_dimension=0, tiled=True)]
    reduce_scatter x1, waiting for transfers between devices: 0.02 us -> 12.3 us  [per_device(): lax.psum_scatter(packed.astype(jnp.bfloat16), second_axis, scatter_dimens...]
    ppermute x6, waiting for transfers between devices: 11.5 us -> 6.03 us  [permute_scatter(): lax.ppermute(chunk, axis, [(j, (j + step) % n) for j in range(n)])]
    ppermute x6, starting transfers between devices: 8.56 us -> 11.8 us  [permute_scatter(): lax.ppermute(chunk, axis, [(j, (j + step) % n) for j in range(n)])]
  transfers between devices with their start and end apart: 9 -> 9, of which waited for: 7 -> 8; matrix products, arithmetic and copies ran while one was open for 13% -> 13% of each run, Pallas kernels for 0% -> 0%
where the time goes in v8:
time: 180 us; the launch traced here: 179 us
  waiting for transfers between devices  69.6 us (39%)
  blocking collectives  33.2 us (18%)
  other arithmetic  20.2 us (11%)
  local copies, waits for them, and re-layouts  15.6 us (9%)
  between operations  14.2 us (8%)
  matrix products  13.9 us (8%)
  starting transfers between devices  12.1 us (7%)
    all_gather x1, waiting for transfers between devices, per_device(): gathered = lax.all_gather(both, 'z', axis=0, tiled=True)  42 us
    psum x1, blocking collectives, per_device(): vectors = lax.psum(vectors, second_axis)  30.7 us
    reduce_scatter x1, waiting for transfers between devices, per_device(): lax.psum_scatter(packed.astype(jnp.bfloat16), second_axis, scatter_dimens...  12.3 us
    ppermute x6, starting transfers between devices, permute_scatter(): lax.ppermute(chunk, axis, [(j, (j + step) % n) for j in range(n)])  11.8 us
    reduce_scatter x1, waiting for transfers between devices, per_device(): lax.psum_scatter(packed, first_axis, scatter_dimension=0, tiled=True)  9.09 us
    ppermute x6, waiting for transfers between devices, permute_scatter(): lax.ppermute(chunk, axis, [(j, (j + step) % n) for j in range(n)])  6.03 us
    dot_general x1, matrix products, per_device(): lax.dot_general(jnp.concatenate([conv_lhs, mix_lhs], axis=0), jnp.concate...  5.59 us
    dot_general x1, matrix products, per_device(): lax.dot_general(cotangent, mix_full, (((1,), (1,)), ((), ())), preferred_...  4.06 us
  transfers between devices with their start and end apart: 9, of which 8 were waited for; matrix products, arithmetic and copies ran while one was open for 13% of the time, Pallas kernels for 0%

profile of v8, /device:TPU:32, one launch (start us, length us, event | category | flops | bytes accessed | tf_op | source)
XLA Modules:
  0.0 178.8 jit_solution(14341642886806805398)
XLA Ops:
  7.2 1.9 %pad_maximum_fusion = bf16[512,512]{1,0:T(8,128)(2,1)} fusion(bf16[64,512]{1,0:T(8,128)(2,1)} %param.14, bf16[448,512]{1,0:T(8,128)(2,1)} %param.13), kind=kLoop, calls=%fused_computation.33 | loop fusion | flops 1048576 | bytes 1048576 | tf_op jit(solution)/shard_map/concatenate | solution.py:64
  10.4 2.8 %fusion.11 = bf16[256,512]{1,0:T(8,128)(2,1)S(1)} fusion(bf16[256,512]{1,0:T(8,128)(2,1)} %param.10, f32[512]{0:T(512)} %param.16), kind=kLoop, calls=%fused_computation.28 | loop fusion | flops 786432 | bytes 526336 | tf_op jit(solution)/shard_map/convert_element_type | solution.py:71
  14.2 1.8 %constant_dynamic-update-slice_fusion = bf16[256,3584]{1,0:T(8,128)(2,1)S(1)} fusion(bf16[256,3584]{1,0:T(8,128)(2,1)S(1)} %select_dynamic-update-slice_fusion.3, f32[512]{0:T(512)S(1)} %copy-done.5, bf16[256,512]{1,0:T(8,128)(2,1)S(1)} %copy-done.1), kind=kLoop, calls=%fused_computation.67 | loop fusion | flops 786432 | bytes 526336
  17.6 2.3 %copy.34 = bf16[256,3584]{0,1:T(8,128)(2,1)} copy(bf16[256,3584]{1,0:T(8,128)(2,1)S(1)} %select_dynamic-update-slice_fusion) | data formatting | bytes 3670016 | tf_op jit(solution)/shard_map/concatenate | solution.py:79
  19.9 2.5 %reshape.131 = bf16[256,256,14]{0,2,1:T(8,128)(2,1)S(1)} reshape(bf16[256,3584]{0,1:T(8,128)(2,1)} %copy.34) | data formatting | bytes 3670016 | tf_op jit(solution)/shard_map/reshape | solution.py:125
  23.3 42.0 %all-gather.2.cloned.1.call-done = bf16[4096,512]{1,0:T(8,128)(2,1)} async-done(((bf16[512,512]{1,0:T(8,128)(2,1)}), bf16[4096,512]{1,0:T(8,128)(2,1)}) %all-gather.2.cloned.1.call-update) | async-done | bytes 4194320 | tf_op jit(solution)/shard_map/all_gather | solution.py:65
  65.4 2.4 %slice.174 = bf16[8,448,512]{2,1,0:T(8,128)(2,1)S(1)} slice(bf16[8,512,512]{2,1,0:T(8,128)(2,1)} %bitcast.49), slice={[0:8], [0:448], [0:512]} | slice | bytes 7340032 | tf_op jit(solution)/shard_map/slice | solution.py:67
  70.4 4.1 %convert_reduce_fusion.1 = (f32[512]{0:T(512)S(1)}, bf16[256,512]{1,0:T(8,128)(2,1)S(1)}, f32[512]{0:T(512)S(1)}, bf16[256,512]{1,0:T(8,128)(2,1)S(1)}) fusion(f32[256,512]{1,0:T(8,128)S(1)} %convolution_add_fusion, f32[512]{0:T(512)S(1)} %get-tuple-element.84, f32[512]{0:T(512)S(1)} %get-tuple-element.85, f32[512]{0:T(512)S(1)} %copy-done.6, ...), kind=kOutput, calls=%fused_computation.38 | convolution fusion | flops 136444928 | bytes 1845248 | tf_op jit(solution)/shard_map/dot_general | solution.py:88
  75.5 5.6 %fusion = f32[4096,512]{1,0:T(8,128)} fusion(bf16[256,4096]{0,1:T(8,128)(2,1)S(1)} %bitcast.52, bf16[256,4096]{0,1:T(8,128)(2,1)S(1)} %bitcast.51, bf16[256,512]{1,0:T(8,128)(2,1)S(1)} %copy-done.4, bf16[256,512]{1,0:T(8,128)(2,1)S(1)} %get-tuple-element.59), kind=kOutput, calls=%fused_computation.1 | convolution fusion | flops 2156920832 | bytes 13107200 | tf_op jit(solution)/shard_map/dot_general | solution.py:127
  81.5 3.2 %convolution_convert_fusion = bf16[256,3584]{1,0:T(8,128)(2,1)S(1)} fusion(bf16[256,512]{1,0:T(8,128)(2,1)S(1)} %get-tuple-element.59, bf16[3584,512]{1,0:T(8,128)(2,1)} %bitcast.46), kind=kOutput, calls=%fused_computation | convolution fusion | flops 940441600 | bytes 5767168 | tf_op jit(solution)/shard_map/dot_general | solution.py:92
  85.4 3.9 %fusion.19 = (f32[512]{0:T(512)S(1)}, f32[256,512]{1,0:T(8,128)S(1)}) fusion(bf16[256,512]{1,0:T(8,128)(2,1)S(1)} %copy-done.1, f32[512]{0:T(512)S(1)} %get-tuple-element.87, f32[512]{0:T(512)S(1)} %get-tuple-element.86, f32[512]{0:T(512)S(1)} %copy-done.5, f32[229,512]{1,0:T(8,128)S(1)} %get-tuple-element.104, f32[238,512]{1,0:T(8,128)S(1)} %get-tuple-element.102, ...), kind=kLoop, calls=%fused_computation.44 | loop fusion | flops 2227712 | bytes 3981312 | tf_op jit(solution)/shard_map/reduce_sum | solution.py:109
  89.3 2.5 %convert_reduce_fusion = (f32[512]{0:T(512)S(1)}, bf16[256,512]{1,0:T(8,128)(2,1)}) fusion(bf16[256,512]{1,0:T(8,128)(2,1)S(1)} %copy-done.4, f32[256,512]{1,0:T(8,128)S(1)} %get-tuple-element.61, bf16[256,512]{1,0:T(8,128)(2,1)S(1)} %copy-done.1, f32[512]{0:T(512)S(1)} %get-tuple-element.86), kind=kLoop, calls=%fused_computation.19 | loop fusion | flops 1048064 | bytes 1314816 | tf_op jit(solution)/shard_map/reduce_sum | solution.py:108
  91.8 2.5 %psum.14 = f32[4,512]{1,0:T(4,128)S(1)} all-reduce(f32[4,512]{1,0:T(4,128)S(1)} %pad_maximum_fusion.1), channel_id=1, replica_groups=mesh['x'=4,'y'=4,'c'=2,'z'=8] {'c'}, use_global_device_ids=true, to_apply=%region_7.8 | all-reduce | flops 2048 | bytes 16384 | tf_op jit(solution)/shard_map/psum | solution.py:135
  94.4 9.1 %reduce-scatter.3.cloned.1.call-done = f32[2048,512]{1,0:T(8,128)} async-done(((f32[4096,512]{1,0:T(8,128)}), f32[2048,512]{1,0:T(8,128)}) %reduce-scatter.3.cloned.1.call-update) | async-done | bytes 4194320 | tf_op jit(solution)/shard_map/reduce_scatter | solution.py:134
  103.4 3.8 %convert_element_type.71 = bf16[2048,512]{1,0:T(8,128)(2,1)} convert(f32[2048,512]{1,0:T(8,128)} %reduce-scatter.3.cloned.1.call-done) | non-fusion elementwise | flops 1048576 | bytes 6291456 | tf_op jit(solution)/shard_map/convert_element_type | solution.py:137
  107.9 30.7 %psum.15 = f32[4,4,2,8,8]{3,2,1,0,4:T(2,128)S(1)} all-reduce(f32[4,4,2,8,8]{3,2,1,0,4:T(2,128)S(1)} %reshape.138), channel_id=1, replica_groups=mesh['x'=4,'y'=4,'c'=2,'z'=8] {'z'}, use_global_device_ids=true, to_apply=%region_9.10 | all-reduce | flops 2048 | bytes 16384 | tf_op jit(solution)/shard_map/psum | solution.py:139
  139.0 12.3 %reduce-scatter.5.cloned.1.call-done = bf16[256,512]{1,0:T(8,128)(2,1)} async-done(((bf16[2048,512]{1,0:T(8,128)(2,1)}), bf16[256,512]{1,0:T(8,128)(2,1)}) %reduce-scatter.5.cloned.1.call-update) | async-done | bytes 262160 | tf_op jit(solution)/shard_map/reduce_scatter | solution.py:137
  152.4 1.6 collective-permute-start
  153.9 2.4 %collective-permute-start.1 = (f32[64,640]{1,0:T(8,128)S(1)}, f32[64,640]{1,0:T(8,128)S(1)}, u32[]{:S(2)}, u32[]{:S(2)}) collective-permute-start(f32[64,640]{1,0:T(8,128)S(1)} %get-tuple-element.70), channel_id=1, source_target_pairs={{0,32},{16,48},{32,0},{48,16},{1,33},{17,49},{33,1},{49,17},{2,34}... | collective-permute-start | bytes 491528 | tf_op jit(solution)/shard_map/ppermute | solution.py:53
  156.3 1.7 collective-permute-start.2
  159.0 2.4 %collective-permute-done.1 = f32[64,640]{1,0:T(8,128)S(1)} collective-permute-done((f32[64,640]{1,0:T(8,128)S(1)}, f32[64,640]{1,0:T(8,128)S(1)}, u32[]{:S(2)}, u32[]{:S(2)}) %collective-permute-start.1) | collective-permute-done | bytes 163872 | tf_op jit(solution)/shard_map/ppermute | solution.py:53
  161.7 1.9 %collective-permute-start.3 = (f32[16,640]{1,0:T(8,128)S(1)}, f32[16,640]{1,0:T(8,128)S(1)}, u32[]{:S(2)}, u32[]{:S(2)}) collective-permute-start(f32[16,640]{1,0:T(8,128)S(1)} %get-tuple-element.81), channel_id=1, source_target_pairs={{0,64},{64,128},{128,192},{192,0},{1,65},{65,129},{129,193},{193,1... | collective-permute-start | bytes 122888 | tf_op jit(solution)/shard_map/ppermute | solution.py:53
  163.6 2.7 %collective-permute-start.4 = (f32[16,640]{1,0:T(8,128)S(1)}, f32[16,640]{1,0:T(8,128)S(1)}, u32[]{:S(2)}, u32[]{:S(2)}) collective-permute-start(f32[16,640]{1,0:T(8,128)S(1)} %get-tuple-element.83), channel_id=1, source_target_pairs={{0,128},{64,192},{128,0},{192,64},{1,129},{65,193},{129,1},{193,65... | collective-permute-start | bytes 122888 | tf_op jit(solution)/shard_map/ppermute | solution.py:53
  166.2 1.5 collective-permute-start.5
  (76 shorter events, 17.0 us)
Async XLA Ops:
  7.2 58.2 %all-gather.2.cloned.1.call-start = ((), (), s32[]{:S(2)}) async-start(), calls=%async_computation.2 | async-start | bytes 4718592 | tf_op jit(solution)/shard_map/all_gather | solution.py:65
  9.2 94.3 %reduce-scatter.3.cloned.1.call-start = ((), (), s32[]{:S(2)}) async-start(), calls=%async_computation.3 | async-start | bytes 12582912 | tf_op jit(solution)/shard_map/reduce_scatter | solution.py:134
  13.2 1.0 copy-start.1
  13.2 0.9 copy-start.5
  16.4 1.3 copy-start.2
  22.6 0.7 copy-start.6
  65.4 3.9 %copy-start.3 = (bf16[256,3584]{1,0:T(8,128)(2,1)S(1)}, bf16[256,3584]{1,0:T(8,128)(2,1)}, u32[]{:S(2)}) copy-start(bf16[256,3584]{1,0:T(8,128)(2,1)} %copy-done.2) | copy-start | bytes 5505028
  65.4 3.9 %copy-start.7 = (f32[512]{0:T(512)S(1)}, f32[512]{0:T(512)}, u32[]{:S(2)}) copy-start(f32[512]{0:T(512)} %param.15) | copy-start | bytes 6148
  67.8 2.6 %copy-start = (bf16[8,448,512]{2,1,0:T(8,128)(2,1)}, bf16[8,448,512]{2,1,0:T(8,128)(2,1)S(1)}, u32[]{:S(2)}) copy-start(bf16[8,448,512]{2,1,0:T(8,128)(2,1)S(1)} %slice.174) | copy-start | bytes 11010052
  69.3 1.1 copy-start.4
  81.1 70.2 %reduce-scatter.5.cloned.1.call-start = ((), (), s32[]{:S(2)}) async-start(), calls=%async_computation.4 | async-start | bytes 2359296 | tf_op jit(solution)/shard_map/reduce_scatter | solution.py:137
  152.4 6.6 %collective-permute-start = (f32[64,640]{1,0:T(8,128)S(1)}, f32[64,640]{1,0:T(8,128)S(1)}, u32[]{:S(2)}, u32[]{:S(2)}) collective-permute-start(f32[64,640]{1,0:T(8,128)S(1)} %get-tuple-element.69), channel_id=1, source_target_pairs={{0,16},{16,32},{32,48},{48,0},{1,17},{17,33},{33,49},{49,1},{2,18}... | collective-permute-start | bytes 491528 | tf_op jit(solution)/shard_map/ppermute | solution.py:53
  153.9 7.4 %collective-permute-start.1 = (f32[64,640]{1,0:T(8,128)S(1)}, f32[64,640]{1,0:T(8,128)S(1)}, u32[]{:S(2)}, u32[]{:S(2)}) collective-permute-start(f32[64,640]{1,0:T(8,128)S(1)} %get-tuple-element.70), channel_id=1, source_target_pairs={{0,32},{16,48},{32,0},{48,16},{1,33},{17,49},{33,1},{49,17},{2,34}... | collective-permute-start | bytes 491528 | tf_op jit(solution)/shard_map/ppermute | solution.py:53
  156.3 5.3 %collective-permute-start.2 = (f32[64,640]{1,0:T(8,128)S(1)}, f32[64,640]{1,0:T(8,128)S(1)}, u32[]{:S(2)}, u32[]{:S(2)}) collective-permute-start(f32[64,640]{1,0:T(8,128)S(1)} %get-tuple-element.71), channel_id=1, source_target_pairs={{0,48},{16,0},{32,16},{48,32},{1,49},{17,1},{33,17},{49,33},{2,50}... | collective-permute-start | bytes 491528 | tf_op jit(solution)/shard_map/ppermute | solution.py:53
  161.7 6.1 %collective-permute-start.3 = (f32[16,640]{1,0:T(8,128)S(1)}, f32[16,640]{1,0:T(8,128)S(1)}, u32[]{:S(2)}, u32[]{:S(2)}) collective-permute-start(f32[16,640]{1,0:T(8,128)S(1)} %get-tuple-element.81), channel_id=1, source_target_pairs={{0,64},{64,128},{128,192},{192,0},{1,65},{65,129},{129,193},{193,1... | collective-permute-start | bytes 122888 | tf_op jit(solution)/shard_map/ppermute | solution.py:53
  163.6 5.5 %collective-permute-start.4 = (f32[16,640]{1,0:T(8,128)S(1)}, f32[16,640]{1,0:T(8,128)S(1)}, u32[]{:S(2)}, u32[]{:S(2)}) collective-permute-start(f32[16,640]{1,0:T(8,128)S(1)} %get-tuple-element.83), channel_id=1, source_target_pairs={{0,128},{64,192},{128,0},{192,64},{1,129},{65,193},{129,1},{193,65... | collective-permute-start | bytes 122888 | tf_op jit(solution)/shard_map/ppermute | solution.py:53
  166.2 4.0 %collective-permute-start.5 = (f32[16,640]{1,0:T(8,128)S(1)}, f32[16,640]{1,0:T(8,128)S(1)}, u32[]{:S(2)}, u32[]{:S(2)}) collective-permute-start(f32[16,640]{1,0:T(8,128)S(1)} %get-tuple-element.82), channel_id=1, source_target_pairs={{0,192},{64,0},{128,64},{192,128},{1,193},{65,1},{129,65},{193,129... | collective-permute-start | bytes 122888 | tf_op jit(solution)/shard_map/ppermute | solution.py:53
Sparse Core Ops, SparseCore 0:
  9.8 55.5 all-gather.1
  81.2 22.2 reduce-scatter.2
  107.4 43.8 reduce-scatter.4

commit v9 on v8

--- a/solution.py
+++ b/solution.py
@@ -62,7 +62,13 @@
     conv_rows = conv_weight.shape[0]
     mix_rows = mix_weight.shape[0]
     both = jnp.concatenate([conv_weight, mix_weight], axis=0)
-    gathered = lax.all_gather(both, "z", axis=0, tiled=True)
+    core = lax.axis_index("c")
+    half = C // 2
+    own = lax.all_gather(lax.dynamic_slice_in_dim(both, core * half, half, axis=1), "z", axis=0, tiled=True)
+    other = lax.ppermute(own, "c", [(0, 1), (1, 0)])
+    first_half = jnp.where(core == 0, own, other)
+    second_half = jnp.where(core == 0, other, own)
+    gathered = jnp.concatenate([first_half, second_half], axis=1)
     gathered = gathered.reshape(-1, conv_rows + mix_rows, C)
     conv_full = gathered[:, :conv_rows].reshape(-1, C)
     mix_full = gathered[:, conv_rows:].reshape(-1, C)

time: 180 us -> 178 us (0.989)
  waiting for transfers between devices: 69.6 us -> 66.2 us
  other arithmetic: 20.2 us -> 22.4 us
    unnamed x17 -> x19, local copies, waits for them, and re-layouts: 2.68 us -> 5.06 us
    slice x1, local copies, waits for them, and re-layouts: 2.41 us -> 0.24 us  [per_device(): conv_full = gathered[:, :conv_rows].reshape(-1, C)]
    select_n x0 -> x1, other arithmetic: none -> 2.13 us  [per_device(): first_half = jnp.where(core == 0, own, other)]
  transfers between devices with their start and end apart: 9 -> 10, of which waited for: 8 -> 8; matrix products, arithmetic and copies ran while one was open for 13% -> 13% of each run, Pallas kernels for 0% -> 0%
where the time goes in v9:
time: 178 us; the launch traced here: 176 us
  waiting for transfers between devices  66.2 us (37%)
  blocking collectives  33.5 us (19%)
  other arithmetic  22.4 us (13%)
  local copies, waits for them, and re-layouts  14.4 us (8%)
  between operations  14.2 us (8%)
  matrix products  13.9 us (8%)
  starting transfers between devices  11.6 us (7%)
    all_gather x1, waiting for transfers between devices, per_device(): lax.all_gather(lax.dynamic_slice_in_dim(both, core * half, half, axis=1),...  40.4 us
    psum x1, blocking collectives, per_device(): vectors = lax.psum(vectors, second_axis)  30.8 us
    reduce_scatter x1, waiting for transfers between devices, per_device(): lax.psum_scatter(packed.astype(jnp.bfloat16), second_axis, scatter_dimens...  11.6 us
    ppermute x6, starting transfers between devices, permute_scatter(): lax.ppermute(chunk, axis, [(j, (j + step) % n) for j in range(n)])  11.3 us
    reduce_scatter x1, waiting for transfers between devices, per_device(): lax.psum_scatter(packed, first_axis, scatter_dimension=0, tiled=True)  7.49 us
    ppermute x6, waiting for transfers between devices, permute_scatter(): lax.ppermute(chunk, axis, [(j, (j + step) % n) for j in range(n)])  6.63 us
    dot_general x1, matrix products, per_device(): lax.dot_general(jnp.concatenate([conv_lhs, mix_lhs], axis=0), jnp.concate...  5.57 us
    unnamed x19, local copies, waits for them, and re-layouts  5.06 us
  transfers between devices with their start and end apart: 10, of which 8 were waited for; matrix products, arithmetic and copies ran while one was open for 13% of the time, Pallas kernels for 0%

profile of v9, /device:TPU:32, one launch (start us, length us, event | category | flops | bytes accessed | tf_op | source)
XLA Modules:
  0.0 176.2 jit_solution(12769090973652856688)
XLA Ops:
  7.2 1.7 fusion.20
  10.2 2.8 %fusion.11 = bf16[256,512]{1,0:T(8,128)(2,1)S(1)} fusion(bf16[256,512]{1,0:T(8,128)(2,1)} %param.10, f32[512]{0:T(512)} %param.16), kind=kLoop, calls=%fused_computation.31 | loop fusion | flops 786432 | bytes 526336 | tf_op jit(solution)/shard_map/convert_element_type | solution.py:77
  13.2 40.4 %all-gather.2.cloned.1.call-done = bf16[4096,256]{1,0:T(8,128)(2,1)} async-done(((bf16[512,256]{1,0:T(8,128)(2,1)}), bf16[4096,256]{1,0:T(8,128)(2,1)}) %all-gather.2.cloned.1.call-update) | async-done | bytes 2097168 | tf_op jit(solution)/shard_map/all_gather | solution.py:67
  54.0 1.8 %constant_dynamic-update-slice_fusion = bf16[256,3584]{1,0:T(8,128)(2,1)S(1)} fusion(bf16[256,3584]{1,0:T(8,128)(2,1)S(1)} %select_dynamic-update-slice_fusion.3, f32[512]{0:T(512)S(1)} %copy-done.6, bf16[256,512]{1,0:T(8,128)(2,1)S(1)} %copy-done.1), kind=kLoop, calls=%fused_computation.72 | loop fusion | flops 786432 | bytes 526336
  57.4 2.2 %copy.34 = bf16[256,3584]{0,1:T(8,128)(2,1)} copy(bf16[256,3584]{1,0:T(8,128)(2,1)S(1)} %select_dynamic-update-slice_fusion) | data formatting | bytes 3670016 | tf_op jit(solution)/shard_map/concatenate | solution.py:85
  59.7 2.5 %reshape.131 = bf16[256,256,14]{0,2,1:T(8,128)(2,1)S(1)} reshape(bf16[256,3584]{0,1:T(8,128)(2,1)} %copy.34) | data formatting | bytes 3670016 | tf_op jit(solution)/shard_map/reshape | solution.py:131
  64.1 2.1 %broadcast_select_fusion.1 = (bf16[4096,256]{1,0:T(8,128)(2,1)S(1)}, bf16[4096,256]{1,0:T(8,128)(2,1)S(1)}) fusion(bf16[4096,256]{1,0:T(8,128)(2,1)S(1)} %copy-done.4, bf16[4096,256]{1,0:T(8,128)(2,1)} %collective-permute-done, pred[]{:T(512)S(6)} %eq.30), kind=kLoop, calls=%fused_computation.7 | loop fusion | flops 2097152 | bytes 8388609 | tf_op jit(solution)/shard_map/jit(_where)/select_n | solution.py:69
  66.9 1.8 %copy-done.3 = bf16[256,3584]{1,0:T(8,128)(2,1)S(1)} copy-done((bf16[256,3584]{1,0:T(8,128)(2,1)S(1)}, bf16[256,3584]{1,0:T(8,128)(2,1)}, u32[]{:S(2)}) %copy-start.3) | copy-done | bytes 1835032
  69.8 4.1 %convert_reduce_fusion.1 = (f32[512]{0:T(512)S(1)}, bf16[256,512]{1,0:T(8,128)(2,1)S(1)}, f32[512]{0:T(512)S(1)}, bf16[256,512]{1,0:T(8,128)(2,1)S(1)}) fusion(f32[256,512]{1,0:T(8,128)S(1)} %convolution_add_fusion, f32[512]{0:T(512)S(1)} %get-tuple-element.86, f32[512]{0:T(512)S(1)} %get-tuple-element.87, f32[512]{0:T(512)S(1)} %copy-done.7, ...), kind=kOutput, calls=%fused_computation.42 | convolution fusion | flops 136444928 | bytes 1845248 | tf_op jit(solution)/shard_map/dot_general | solution.py:94
  74.9 5.6 %fusion = f32[4096,512]{1,0:T(8,128)} fusion(bf16[256,4096]{0,1:T(8,128)(2,1)S(1)} %bitcast.52, bf16[256,4096]{0,1:T(8,128)(2,1)S(1)} %bitcast.51, bf16[256,512]{1,0:T(8,128)(2,1)S(1)} %copy-done.5, bf16[256,512]{1,0:T(8,128)(2,1)S(1)} %get-tuple-element.59), kind=kOutput, calls=%fused_computation.2 | convolution fusion | flops 2156920832 | bytes 13107200 | tf_op jit(solution)/shard_map/dot_general | solution.py:133
  80.9 3.2 %convolution_convert_fusion = bf16[256,3584]{1,0:T(8,128)(2,1)S(1)} fusion(bf16[256,512]{1,0:T(8,128)(2,1)S(1)} %get-tuple-element.59, bf16[3584,512]{1,0:T(8,128)(2,1)} %bitcast.48), kind=kOutput, calls=%fused_computation | convolution fusion | flops 940441600 | bytes 5767168 | tf_op jit(solution)/shard_map/dot_general | solution.py:98
  84.8 3.9 %fusion.19 = (f32[512]{0:T(512)S(1)}, f32[256,512]{1,0:T(8,128)S(1)}) fusion(bf16[256,512]{1,0:T(8,128)(2,1)S(1)} %copy-done.1, f32[512]{0:T(512)S(1)} %get-tuple-element.89, f32[512]{0:T(512)S(1)} %get-tuple-element.88, f32[512]{0:T(512)S(1)} %copy-done.6, f32[229,512]{1,0:T(8,128)S(1)} %get-tuple-element.106, f32[238,512]{1,0:T(8,128)S(1)} %get-tuple-element.104, ...), kind=kLoop, calls=%fused_computation.48 | loop fusion | flops 2227712 | bytes 3981312 | tf_op jit(solution)/shard_map/reduce_sum | solution.py:115
  88.7 2.5 %convert_reduce_fusion = (f32[512]{0:T(512)S(1)}, bf16[256,512]{1,0:T(8,128)(2,1)}) fusion(bf16[256,512]{1,0:T(8,128)(2,1)S(1)} %copy-done.5, f32[256,512]{1,0:T(8,128)S(1)} %get-tuple-element.61, bf16[256,512]{1,0:T(8,128)(2,1)S(1)} %copy-done.1, f32[512]{0:T(512)S(1)} %get-tuple-element.88), kind=kLoop, calls=%fused_computation.22 | loop fusion | flops 1048064 | bytes 1314816 | tf_op jit(solution)/shard_map/reduce_sum | solution.py:114
  91.2 2.7 %psum.14 = f32[4,512]{1,0:T(4,128)S(1)} all-reduce(f32[4,512]{1,0:T(4,128)S(1)} %pad_maximum_fusion.1), channel_id=1, replica_groups=mesh['x'=4,'y'=4,'c'=2,'z'=8] {'c'}, use_global_device_ids=true, to_apply=%region_7.8 | all-reduce | flops 2048 | bytes 16384 | tf_op jit(solution)/shard_map/psum | solution.py:141
  93.9 7.5 %reduce-scatter.3.cloned.1.call-done = f32[2048,512]{1,0:T(8,128)} async-done(((f32[4096,512]{1,0:T(8,128)}), f32[2048,512]{1,0:T(8,128)}) %reduce-scatter.3.cloned.1.call-update) | async-done | bytes 4194320 | tf_op jit(solution)/shard_map/reduce_scatter | solution.py:140
  101.4 3.8 %convert_element_type.71 = bf16[2048,512]{1,0:T(8,128)(2,1)} convert(f32[2048,512]{1,0:T(8,128)} %reduce-scatter.3.cloned.1.call-done) | non-fusion elementwise | flops 1048576 | bytes 6291456 | tf_op jit(solution)/shard_map/convert_element_type | solution.py:143
  105.8 30.8 %psum.15 = f32[4,4,2,8,8]{3,2,1,0,4:T(2,128)S(1)} all-reduce(f32[4,4,2,8,8]{3,2,1,0,4:T(2,128)S(1)} %reshape.138), channel_id=1, replica_groups=mesh['x'=4,'y'=4,'c'=2,'z'=8] {'z'}, use_global_device_ids=true, to_apply=%region_9.10 | all-reduce | flops 2048 | bytes 16384 | tf_op jit(solution)/shard_map/psum | solution.py:145
  137.0 11.6 %reduce-scatter.5.cloned.1.call-done = bf16[256,512]{1,0:T(8,128)(2,1)} async-done(((bf16[2048,512]{1,0:T(8,128)(2,1)}), bf16[256,512]{1,0:T(8,128)(2,1)}) %reduce-scatter.5.cloned.1.call-update) | async-done | bytes 262160 | tf_op jit(solution)/shard_map/reduce_scatter | solution.py:143
  149.7 1.6 collective-permute-start.1
  151.3 3.0 %collective-permute-start.2 = (f32[64,640]{1,0:T(8,128)S(1)}, f32[64,640]{1,0:T(8,128)S(1)}, u32[]{:S(2)}, u32[]{:S(2)}) collective-permute-start(f32[64,640]{1,0:T(8,128)S(1)} %get-tuple-element.72), channel_id=1, source_target_pairs={{0,32},{16,48},{32,0},{48,16},{1,33},{17,49},{33,1},{49,17},{2,34}... | collective-permute-start | bytes 491528 | tf_op jit(solution)/shard_map/ppermute | solution.py:53
  156.4 3.0 %collective-permute-done.2 = f32[64,640]{1,0:T(8,128)S(1)} collective-permute-done((f32[64,640]{1,0:T(8,128)S(1)}, f32[64,640]{1,0:T(8,128)S(1)}, u32[]{:S(2)}, u32[]{:S(2)}) %collective-permute-start.2) | collective-permute-done | bytes 163872 | tf_op jit(solution)/shard_map/ppermute | solution.py:53
  161.0 2.7 %collective-permute-start.5 = (f32[16,640]{1,0:T(8,128)S(1)}, f32[16,640]{1,0:T(8,128)S(1)}, u32[]{:S(2)}, u32[]{:S(2)}) collective-permute-start(f32[16,640]{1,0:T(8,128)S(1)} %get-tuple-element.85), channel_id=1, source_target_pairs={{0,128},{64,192},{128,0},{192,64},{1,129},{65,193},{129,1},{193,65... | collective-permute-start | bytes 122888 | tf_op jit(solution)/shard_map/ppermute | solution.py:53
  163.7 1.5 collective-permute-start.6
  165.2 1.3 collective-permute-done.5
  (82 shorter events, 17.9 us)
Async XLA Ops:
  7.2 46.4 %all-gather.2.cloned.1.call-start = ((), (), s32[]{:S(2)}) async-start(), calls=%async_computation.2 | async-start | bytes 2359296 | tf_op jit(solution)/shard_map/all_gather | solution.py:67
  8.9 92.5 %reduce-scatter.3.cloned.1.call-start = ((), (), s32[]{:S(2)}) async-start(), calls=%async_computation.3 | async-start | bytes 12582912 | tf_op jit(solution)/shard_map/reduce_scatter | solution.py:140
  12.9 41.0 %copy-start.1 = (bf16[256,512]{1,0:T(8,128)(2,1)S(1)}, bf16[256,512]{1,0:T(8,128)(2,1)}, u32[]{:S(2)}) copy-start(bf16[256,512]{1,0:T(8,128)(2,1)} %param.10) | copy-start | bytes 786436
  13.0 41.0 %copy-start.6 = (f32[512]{0:T(512)S(1)}, f32[512]{0:T(512)}, u32[]{:S(2)}) copy-start(f32[512]{0:T(512)} %param.16) | copy-start | bytes 6148
  53.6 9.6 %collective-permute-start = (bf16[4096,256]{1,0:T(8,128)(2,1)}, bf16[4096,256]{1,0:T(8,128)(2,1)}, u32[]{:S(2)}, u32[]{:S(2)}) collective-permute-start(bf16[4096,256]{1,0:T(8,128)(2,1)} %all-gather.2.cloned.1.call-done), channel_id=1, source_target_pairs={{0,8},{8,0},{1,9},{9,1},{2,10},{10,2},{3,11},{11,3},{4,12},{12,4},... | collective-permute-start | bytes 6291464 | tf_op jit(solution)/shard_map/ppermute | solution.py:68
  56.2 1.3 copy-start.2
  62.5 0.7 copy-start.7
  62.5 1.6 copy-start.4
  66.5 2.2 %copy-start.3 = (bf16[256,3584]{1,0:T(8,128)(2,1)S(1)}, bf16[256,3584]{1,0:T(8,128)(2,1)}, u32[]{:S(2)}) copy-start(bf16[256,3584]{1,0:T(8,128)(2,1)} %copy-done.2) | copy-start | bytes 5505028
  66.5 2.2 %copy-start.8 = (f32[512]{0:T(512)S(1)}, f32[512]{0:T(512)}, u32[]{:S(2)}) copy-start(f32[512]{0:T(512)} %param.15) | copy-start | bytes 6148
  66.8 3.0 %copy-start = (bf16[8,448,512]{2,1,0:T(8,128)(2,1)}, bf16[8,448,512]{2,1,0:T(8,128)(2,1)S(1)}, u32[]{:S(2)}) copy-start(bf16[8,448,512]{2,1,0:T(8,128)(2,1)S(1)} %slice.174) | copy-start | bytes 11010052
  68.7 1.1 copy-start.5
  80.5 68.2 %reduce-scatter.5.cloned.1.call-start = ((), (), s32[]{:S(2)}) async-start(), calls=%async_computation.4 | async-start | bytes 2359296 | tf_op jit(solution)/shard_map/reduce_scatter | solution.py:143
  149.7 6.6 %collective-permute-start.1 = (f32[64,640]{1,0:T(8,128)S(1)}, f32[64,640]{1,0:T(8,128)S(1)}, u32[]{:S(2)}, u32[]{:S(2)}) collective-permute-start(f32[64,640]{1,0:T(8,128)S(1)} %get-tuple-element.71), channel_id=1, source_target_pairs={{0,16},{16,32},{32,48},{48,0},{1,17},{17,33},{33,49},{49,1},{2,18}... | collective-permute-start | bytes 491528 | tf_op jit(solution)/shard_map/ppermute | solution.py:53
  151.3 8.0 %collective-permute-start.2 = (f32[64,640]{1,0:T(8,128)S(1)}, f32[64,640]{1,0:T(8,128)S(1)}, u32[]{:S(2)}, u32[]{:S(2)}) collective-permute-start(f32[64,640]{1,0:T(8,128)S(1)} %get-tuple-element.72), channel_id=1, source_target_pairs={{0,32},{16,48},{32,0},{48,16},{1,33},{17,49},{33,1},{49,17},{2,34}... | collective-permute-start | bytes 491528 | tf_op jit(solution)/shard_map/ppermute | solution.py:53
  154.3 5.3 %collective-permute-start.3 = (f32[64,640]{1,0:T(8,128)S(1)}, f32[64,640]{1,0:T(8,128)S(1)}, u32[]{:S(2)}, u32[]{:S(2)}) collective-permute-start(f32[64,640]{1,0:T(8,128)S(1)} %get-tuple-element.73), channel_id=1, source_target_pairs={{0,48},{16,0},{32,16},{48,32},{1,49},{17,1},{33,17},{49,33},{2,50}... | collective-permute-start | bytes 491528 | tf_op jit(solution)/shard_map/ppermute | solution.py:53
  159.7 5.5 %collective-permute-start.4 = (f32[16,640]{1,0:T(8,128)S(1)}, f32[16,640]{1,0:T(8,128)S(1)}, u32[]{:S(2)}, u32[]{:S(2)}) collective-permute-start(f32[16,640]{1,0:T(8,128)S(1)} %get-tuple-element.83), channel_id=1, source_target_pairs={{0,64},{64,128},{128,192},{192,0},{1,65},{65,129},{129,193},{193,1... | collective-permute-start | bytes 122888 | tf_op jit(solution)/shard_map/ppermute | solution.py:53
  161.0 5.5 %collective-permute-start.5 = (f32[16,640]{1,0:T(8,128)S(1)}, f32[16,640]{1,0:T(8,128)S(1)}, u32[]{:S(2)}, u32[]{:S(2)}) collective-permute-start(f32[16,640]{1,0:T(8,128)S(1)} %get-tuple-element.85), channel_id=1, source_target_pairs={{0,128},{64,192},{128,0},{192,64},{1,129},{65,193},{129,1},{193,65... | collective-permute-start | bytes 122888 | tf_op jit(solution)/shard_map/ppermute | solution.py:53
  163.7 4.0 %collective-permute-start.6 = (f32[16,640]{1,0:T(8,128)S(1)}, f32[16,640]{1,0:T(8,128)S(1)}, u32[]{:S(2)}, u32[]{:S(2)}) collective-permute-start(f32[16,640]{1,0:T(8,128)S(1)} %get-tuple-element.84), channel_id=1, source_target_pairs={{0,192},{64,0},{128,64},{192,128},{1,193},{65,1},{129,65},{193,129... | collective-permute-start | bytes 122888 | tf_op jit(solution)/shard_map/ppermute | solution.py:53
Sparse Core Ops, SparseCore 0:
  10.3 43.2 all-gather.1
  80.6 20.7 reduce-scatter.2
  105.3 43.2 reduce-scatter.4

commit v10 on v9

--- a/solution.py
+++ b/solution.py
@@ -65,13 +65,6 @@
     core = lax.axis_index("c")
     half = C // 2
     own = lax.all_gather(lax.dynamic_slice_in_dim(both, core * half, half, axis=1), "z", axis=0, tiled=True)
-    other = lax.ppermute(own, "c", [(0, 1), (1, 0)])
-    first_half = jnp.where(core == 0, own, other)
-    second_half = jnp.where(core == 0, other, own)
-    gathered = jnp.concatenate([first_half, second_half], axis=1)
-    gathered = gathered.reshape(-1, conv_rows + mix_rows, C)
-    conv_full = gathered[:, :conv_rows].reshape(-1, C)
-    mix_full = gathered[:, conv_rows:].reshape(-1, C)
     audio_f = audio.astype(jnp.float32)
     act_in, slope_in, dalpha_in = snake_parts(audio_f, alpha_in)
     first = act_in.astype(jnp.bfloat16)
@@ -83,6 +76,27 @@
             jnp.where(same_clip_flags[kernel_tap_index][:, None], moved, jnp.zeros_like(moved))
         )
     unfolded = jnp.concatenate(columns, axis=1)
+    sizes = [lax.axis_size(a) for a in FRAME_AXES]
+    devices = 1
+    for s in sizes:
+        devices *= s
+    conv_each = unfolded.shape[1] // devices
+    mix_each = C // devices
+    order = [FRAME_AXES.index(a) for a in SCATTER_ORDER]
+
+    def lay_out(left):
+        left = jnp.concatenate(left, axis=2).reshape(rows, *sizes, conv_each + mix_each)
+        return left.transpose(0, *[o + 1 for o in order], 5).reshape(rows, -1)
+
+    conv_lhs = lay_out([unfolded.reshape(rows, devices, conv_each), jnp.zeros((rows, devices, mix_each), unfolded.dtype)])
+    own, conv_lhs = lax.optimization_barrier((own, conv_lhs))
+    other = lax.ppermute(own, "c", [(0, 1), (1, 0)])
+    first_half = jnp.where(core == 0, own, other)
+    second_half = jnp.where(core == 0, other, own)
+    gathered = jnp.concatenate([first_half, second_half], axis=1)
+    gathered = gathered.reshape(-1, conv_rows + mix_rows, C)
+    conv_full = gathered[:, :conv_rows].reshape(-1, C)
+    mix_full = gathered[:, conv_rows:].reshape(-1, C)
     product = jnp.dot(
         unfolded,
         conv_full,
@@ -116,19 +130,6 @@
             jnp.sum(second_gradient * dalpha_mid, axis=0),
         ]
     )
-    sizes = [lax.axis_size(a) for a in FRAME_AXES]
-    devices = 1
-    for s in sizes:
-        devices *= s
-    conv_each = unfolded.shape[1] // devices
-    mix_each = second.shape[1] // devices
-    order = [FRAME_AXES.index(a) for a in SCATTER_ORDER]
-
-    def lay_out(left):
-        left = jnp.concatenate(left, axis=2).reshape(rows, *sizes, conv_each + mix_each)
-        return left.transpose(0, *[o + 1 for o in order], 5).reshape(rows, -1)
-
-    conv_lhs = lay_out([unfolded.reshape(rows, devices, conv_each), jnp.zeros((rows, devices, mix_each), unfolded.dtype)])
     mix_lhs = lay_out([jnp.zeros((rows, devices, conv_each), second.dtype), second.reshape(rows, devices, mix_each)])
     packed = lax.dot_general(
         jnp.concatenate([conv_lhs, mix_lhs], axis=0),

time: 178 us -> 173 us (0.972)
  waiting for transfers between devices: 66.2 us -> 61.2 us
    all_gather x1, waiting for transfers between devices: 40.4 us -> 30.9 us  [per_device(): lax.all_gather(lax.dynamic_slice_in_dim(both, core * half, half, axis=1),...]
    ppermute x1, waiting for transfers between devices: 0.01 us -> 4.49 us  [per_device(): other = lax.ppermute(own, 'c', [(0, 1), (1, 0)])]
    unnamed x19 -> x17, local copies, waits for them, and re-layouts: 5.06 us -> 4.16 us
  transfers between devices with their start and end apart: 10 -> 10, of which waited for: 8 -> 9; matrix products, arithmetic and copies ran while one was open for 13% -> 14% of each run, Pallas kernels for 0% -> 0%
where the time goes in v10:
time: 173 us; the launch traced here: 171 us
  waiting for transfers between devices  61.2 us (35%)
  blocking collectives  33.4 us (19%)
  other arithmetic  22.8 us (13%)
  between operations  14.2 us (8%)
  matrix products  13.9 us (8%)
  local copies, waits for them, and re-layouts  13.5 us (8%)
  starting transfers between devices  11.9 us (7%)
    all_gather x1, waiting for transfers between devices, per_device(): lax.all_gather(lax.dynamic_slice_in_dim(both, core * half, half, axis=1),...  30.9 us
    psum x1, blocking collectives, per_device(): vectors = lax.psum(vectors, second_axis)  30.8 us
    reduce_scatter x1, waiting for transfers between devices, per_device(): lax.psum_scatter(packed.astype(jnp.bfloat16), second_axis, scatter_dimens...  12.2 us
    ppermute x6, starting transfers between devices, permute_scatter(): lax.ppermute(chunk, axis, [(j, (j + step) % n) for j in range(n)])  11.6 us
    reduce_scatter x1, waiting for transfers between devices, per_device(): lax.psum_scatter(packed, first_axis, scatter_dimension=0, tiled=True)  7.52 us
    ppermute x6, waiting for transfers between devices, permute_scatter(): lax.ppermute(chunk, axis, [(j, (j + step) % n) for j in range(n)])  6.04 us
    dot_general x1, matrix products, per_device(): lax.dot_general(jnp.concatenate([conv_lhs, mix_lhs], axis=0), jnp.concate...  5.57 us
    ppermute x1, waiting for transfers between devices, per_device(): other = lax.ppermute(own, 'c', [(0, 1), (1, 0)])  4.49 us
  transfers between devices with their start and end apart: 10, of which 9 were waited for; matrix products, arithmetic and copies ran while one was open for 14% of the time, Pallas kernels for 0%

profile of v10, /device:TPU:32, one launch (start us, length us, event | category | flops | bytes accessed | tf_op | source)
XLA Modules:
  0.0 170.8 jit_solution(9046032100366842321)
XLA Ops:
  7.2 1.7 fusion.20
  10.2 2.8 %fusion.11 = bf16[256,512]{1,0:T(8,128)(2,1)S(1)} fusion(bf16[256,512]{1,0:T(8,128)(2,1)} %param.10, f32[512]{0:T(512)} %param.16), kind=kLoop, calls=%fused_computation.31 | loop fusion | flops 786432 | bytes 526336 | tf_op jit(solution)/shard_map/convert_element_type | solution.py:70
  13.9 1.8 %constant_dynamic-update-slice_fusion = bf16[256,3584]{1,0:T(8,128)(2,1)S(1)} fusion(bf16[256,3584]{1,0:T(8,128)(2,1)S(1)} %select_dynamic-update-slice_fusion.3, f32[512]{0:T(512)S(1)} %copy-done.5, bf16[256,512]{1,0:T(8,128)(2,1)S(1)} %copy-done.1), kind=kLoop, calls=%fused_computation.72 | loop fusion | flops 786432 | bytes 526336
  17.3 2.3 %copy.34 = bf16[256,3584]{0,1:T(8,128)(2,1)} copy(bf16[256,3584]{1,0:T(8,128)(2,1)S(1)} %select_dynamic-update-slice_fusion) | data formatting | bytes 3670016 | tf_op jit(solution)/shard_map/concatenate | solution.py:78
  19.6 2.5 %reshape.128 = bf16[256,256,14]{0,2,1:T(8,128)(2,1)S(1)} reshape(bf16[256,3584]{0,1:T(8,128)(2,1)} %copy.34) | data formatting | bytes 3670016 | tf_op jit(solution)/shard_map/reshape | solution.py:91
  22.7 30.9 %all-gather.2.cloned.1.call-done = bf16[4096,256]{1,0:T(8,128)(2,1)} async-done(((bf16[512,256]{1,0:T(8,128)(2,1)}), bf16[4096,256]{1,0:T(8,128)(2,1)}) %all-gather.2.cloned.1.call-update) | async-done | bytes 2097168 | tf_op jit(solution)/shard_map/all_gather | solution.py:67
  53.6 4.5 %collective-permute-done = bf16[4096,256]{1,0:T(8,128)(2,1)} collective-permute-done((bf16[4096,256]{1,0:T(8,128)(2,1)}, bf16[4096,256]{1,0:T(8,128)(2,1)}, u32[]{:S(2)}, u32[]{:S(2)}) %collective-permute-start) | collective-permute-done | bytes 2097184 | tf_op jit(solution)/shard_map/ppermute | solution.py:93
  58.1 2.5 %broadcast_select_fusion.1 = (bf16[4096,256]{1,0:T(8,128)(2,1)S(1)}, bf16[4096,256]{1,0:T(8,128)(2,1)S(1)}) fusion(bf16[4096,256]{1,0:T(8,128)(2,1)} %all-gather.2.cloned.1.call-done, bf16[4096,256]{1,0:T(8,128)(2,1)} %collective-permute-done, pred[]{:T(512)S(6)} %eq.30), kind=kLoop, calls=%fused_computation.7 | loop fusion | flops 2097152 | bytes 8388609 | tf_op jit(solution)/shard_map/jit(_where)/select_n | solution.py:94
  61.2 1.8 %copy-done.3 = bf16[256,3584]{1,0:T(8,128)(2,1)S(1)} copy-done((bf16[256,3584]{1,0:T(8,128)(2,1)S(1)}, bf16[256,3584]{1,0:T(8,128)(2,1)}, u32[]{:S(2)}) %copy-start.3) | copy-done | bytes 1835032
  64.2 4.1 %convert_reduce_fusion.1 = (f32[512]{0:T(512)S(1)}, bf16[256,512]{1,0:T(8,128)(2,1)S(1)}, f32[512]{0:T(512)S(1)}, bf16[256,512]{1,0:T(8,128)(2,1)S(1)}) fusion(f32[256,512]{1,0:T(8,128)S(1)} %convolution_add_fusion, f32[512]{0:T(512)S(1)} %get-tuple-element.90, f32[512]{0:T(512)S(1)} %get-tuple-element.91, f32[512]{0:T(512)S(1)} %copy-done.6, ...), kind=kOutput, calls=%fused_computation.42 | convolution fusion | flops 136444928 | bytes 1845248 | tf_op jit(solution)/shard_map/dot_general | solution.py:108
  69.3 5.6 %fusion = f32[4096,512]{1,0:T(8,128)} fusion(bf16[256,4096]{0,1:T(8,128)(2,1)S(1)} %bitcast.52, bf16[256,4096]{0,1:T(8,128)(2,1)S(1)} %bitcast.51, bf16[256,512]{1,0:T(8,128)(2,1)S(1)} %copy-done.4, bf16[256,512]{1,0:T(8,128)(2,1)S(1)} %get-tuple-element.63), kind=kOutput, calls=%fused_computation.2 | convolution fusion | flops 2156920832 | bytes 13107200 | tf_op jit(solution)/shard_map/dot_general | solution.py:134
  75.3 3.2 %convolution_convert_fusion = bf16[256,3584]{1,0:T(8,128)(2,1)S(1)} fusion(bf16[256,512]{1,0:T(8,128)(2,1)S(1)} %get-tuple-element.63, bf16[3584,512]{1,0:T(8,128)(2,1)} %bitcast.48), kind=kOutput, calls=%fused_computation | convolution fusion | flops 940441600 | bytes 5767168 | tf_op jit(solution)/shard_map/dot_general | solution.py:112
  79.2 3.9 %fusion.19 = (f32[512]{0:T(512)S(1)}, f32[256,512]{1,0:T(8,128)S(1)}) fusion(bf16[256,512]{1,0:T(8,128)(2,1)S(1)} %copy-done.1, f32[512]{0:T(512)S(1)} %get-tuple-element.93, f32[512]{0:T(512)S(1)} %get-tuple-element.92, f32[512]{0:T(512)S(1)} %copy-done.5, f32[229,512]{1,0:T(8,128)S(1)} %get-tuple-element.110, f32[238,512]{1,0:T(8,128)S(1)} %get-tuple-element.108, ...), kind=kLoop, calls=%fused_computation.48 | loop fusion | flops 2227712 | bytes 3981312 | tf_op jit(solution)/shard_map/reduce_sum | solution.py:129
  83.1 2.5 %convert_reduce_fusion = (f32[512]{0:T(512)S(1)}, bf16[256,512]{1,0:T(8,128)(2,1)}) fusion(bf16[256,512]{1,0:T(8,128)(2,1)S(1)} %copy-done.4, f32[256,512]{1,0:T(8,128)S(1)} %get-tuple-element.65, bf16[256,512]{1,0:T(8,128)(2,1)S(1)} %copy-done.1, f32[512]{0:T(512)S(1)} %get-tuple-element.92), kind=kLoop, calls=%fused_computation.22 | loop fusion | flops 1048064 | bytes 1314816 | tf_op jit(solution)/shard_map/reduce_sum | solution.py:128
  85.6 2.5 %psum.14 = f32[4,512]{1,0:T(4,128)S(1)} all-reduce(f32[4,512]{1,0:T(4,128)S(1)} %pad_maximum_fusion.1), channel_id=1, replica_groups=mesh['x'=4,'y'=4,'c'=2,'z'=8] {'c'}, use_global_device_ids=true, to_apply=%region_7.8 | all-reduce | flops 2048 | bytes 16384 | tf_op jit(solution)/shard_map/psum | solution.py:142
  88.1 7.5 %reduce-scatter.3.cloned.1.call-done = f32[2048,512]{1,0:T(8,128)} async-done(((f32[4096,512]{1,0:T(8,128)}), f32[2048,512]{1,0:T(8,128)}) %reduce-scatter.3.cloned.1.call-update) | async-done | bytes 4194320 | tf_op jit(solution)/shard_map/reduce_scatter | solution.py:141
  95.7 3.8 %convert_element_type.71 = bf16[2048,512]{1,0:T(8,128)(2,1)} convert(f32[2048,512]{1,0:T(8,128)} %reduce-scatter.3.cloned.1.call-done) | non-fusion elementwise | flops 1048576 | bytes 6291456 | tf_op jit(solution)/shard_map/convert_element_type | solution.py:144
  100.1 30.8 %psum.15 = f32[4,4,2,8,8]{3,2,1,0,4:T(2,128)S(1)} all-reduce(f32[4,4,2,8,8]{3,2,1,0,4:T(2,128)S(1)} %reshape.138), channel_id=1, replica_groups=mesh['x'=4,'y'=4,'c'=2,'z'=8] {'z'}, use_global_device_ids=true, to_apply=%region_9.10 | all-reduce | flops 2048 | bytes 16384 | tf_op jit(solution)/shard_map/psum | solution.py:146
  131.3 12.2 %reduce-scatter.5.cloned.1.call-done = bf16[256,512]{1,0:T(8,128)(2,1)} async-done(((bf16[2048,512]{1,0:T(8,128)(2,1)}), bf16[256,512]{1,0:T(8,128)(2,1)}) %reduce-scatter.5.cloned.1.call-update) | async-done | bytes 262160 | tf_op jit(solution)/shard_map/reduce_scatter | solution.py:144
  145.5 3.3 %collective-permute-start.2 = (f32[64,640]{1,0:T(8,128)S(1)}, f32[64,640]{1,0:T(8,128)S(1)}, u32[]{:S(2)}, u32[]{:S(2)}) collective-permute-start(f32[64,640]{1,0:T(8,128)S(1)} %get-tuple-element.76), channel_id=1, source_target_pairs={{0,32},{16,48},{32,0},{48,16},{1,33},{17,49},{33,1},{49,17},{2,34}... | collective-permute-start | bytes 491528 | tf_op jit(solution)/shard_map/ppermute | solution.py:53
  148.8 1.5 collective-permute-start.3
  151.2 2.7 %collective-permute-done.2 = f32[64,640]{1,0:T(8,128)S(1)} collective-permute-done((f32[64,640]{1,0:T(8,128)S(1)}, f32[64,640]{1,0:T(8,128)S(1)}, u32[]{:S(2)}, u32[]{:S(2)}) %collective-permute-start.2) | collective-permute-done | bytes 163872 | tf_op jit(solution)/shard_map/ppermute | solution.py:53
  155.5 2.8 %collective-permute-start.5 = (f32[16,640]{1,0:T(8,128)S(1)}, f32[16,640]{1,0:T(8,128)S(1)}, u32[]{:S(2)}, u32[]{:S(2)}) collective-permute-start(f32[16,640]{1,0:T(8,128)S(1)} %get-tuple-element.89), channel_id=1, source_target_pairs={{0,128},{64,192},{128,0},{192,64},{1,129},{65,193},{129,1},{193,65... | collective-permute-start | bytes 122888 | tf_op jit(solution)/shard_map/ppermute | solution.py:53
  158.3 1.7 %collective-permute-start.6 = (f32[16,640]{1,0:T(8,128)S(1)}, f32[16,640]{1,0:T(8,128)S(1)}, u32[]{:S(2)}, u32[]{:S(2)}) collective-permute-start(f32[16,640]{1,0:T(8,128)S(1)} %get-tuple-element.88), channel_id=1, source_target_pairs={{0,192},{64,0},{128,64},{192,128},{1,193},{65,1},{129,65},{193,129... | collective-permute-start | bytes 122888 | tf_op jit(solution)/shard_map/ppermute | solution.py:53
  (80 shorter events, 17.7 us)
Async XLA Ops:
  7.2 46.4 %all-gather.2.cloned.1.call-start = ((), (), s32[]{:S(2)}) async-start(), calls=%async_computation.2 | async-start | bytes 2359296 | tf_op jit(solution)/shard_map/all_gather | solution.py:67
  8.9 86.8 %reduce-scatter.3.cloned.1.call-start = ((), (), s32[]{:S(2)}) async-start(), calls=%async_computation.3 | async-start | bytes 12582912 | tf_op jit(solution)/shard_map/reduce_scatter | solution.py:141
  12.9 1.0 copy-start.1
  12.9 0.9 copy-start.5
  16.1 1.3 copy-start.2
  22.4 31.2 %copy-start.6 = (f32[512]{0:T(512)S(1)}, f32[512]{0:T(512)}, u32[]{:S(2)}) copy-start(f32[512]{0:T(512)} %param.17) | copy-start | bytes 6148
  53.6 4.5 %collective-permute-start = (bf16[4096,256]{1,0:T(8,128)(2,1)}, bf16[4096,256]{1,0:T(8,128)(2,1)}, u32[]{:S(2)}, u32[]{:S(2)}) collective-permute-start(bf16[4096,256]{1,0:T(8,128)(2,1)} %all-gather.2.cloned.1.call-done), channel_id=1, source_target_pairs={{0,8},{8,0},{1,9},{9,1},{2,10},{10,2},{3,11},{11,3},{4,12},{12,4},... | collective-permute-start | bytes 6291464 | tf_op jit(solution)/shard_map/ppermute | solution.py:93
  60.9 2.2 %copy-start.3 = (bf16[256,3584]{1,0:T(8,128)(2,1)S(1)}, bf16[256,3584]{1,0:T(8,128)(2,1)}, u32[]{:S(2)}) copy-start(bf16[256,3584]{1,0:T(8,128)(2,1)} %copy-done.2) | copy-start | bytes 5505028
  60.9 2.2 %copy-start.7 = (f32[512]{0:T(512)S(1)}, f32[512]{0:T(512)}, u32[]{:S(2)}) copy-start(f32[512]{0:T(512)} %param.15) | copy-start | bytes 6148
  61.2 3.0 %copy-start = (bf16[8,448,512]{2,1,0:T(8,128)(2,1)}, bf16[8,448,512]{2,1,0:T(8,128)(2,1)S(1)}, u32[]{:S(2)}) copy-start(bf16[8,448,512]{2,1,0:T(8,128)(2,1)S(1)} %slice.174) | copy-start | bytes 11010052
  63.1 1.1 copy-start.4
  74.9 68.7 %reduce-scatter.5.cloned.1.call-start = ((), (), s32[]{:S(2)}) async-start(), calls=%async_computation.4 | async-start | bytes 2359296 | tf_op jit(solution)/shard_map/reduce_scatter | solution.py:144
  144.6 6.6 %collective-permute-start.1 = (f32[64,640]{1,0:T(8,128)S(1)}, f32[64,640]{1,0:T(8,128)S(1)}, u32[]{:S(2)}, u32[]{:S(2)}) collective-permute-start(f32[64,640]{1,0:T(8,128)S(1)} %get-tuple-element.75), channel_id=1, source_target_pairs={{0,16},{16,32},{32,48},{48,0},{1,17},{17,33},{33,49},{49,1},{2,18}... | collective-permute-start | bytes 491528 | tf_op jit(solution)/shard_map/ppermute | solution.py:53
  145.5 8.4 %collective-permute-start.2 = (f32[64,640]{1,0:T(8,128)S(1)}, f32[64,640]{1,0:T(8,128)S(1)}, u32[]{:S(2)}, u32[]{:S(2)}) collective-permute-start(f32[64,640]{1,0:T(8,128)S(1)} %get-tuple-element.76), channel_id=1, source_target_pairs={{0,32},{16,48},{32,0},{48,16},{1,33},{17,49},{33,1},{49,17},{2,34}... | collective-permute-start | bytes 491528 | tf_op jit(solution)/shard_map/ppermute | solution.py:53
  148.8 5.3 %collective-permute-start.3 = (f32[64,640]{1,0:T(8,128)S(1)}, f32[64,640]{1,0:T(8,128)S(1)}, u32[]{:S(2)}, u32[]{:S(2)}) collective-permute-start(f32[64,640]{1,0:T(8,128)S(1)} %get-tuple-element.77), channel_id=1, source_target_pairs={{0,48},{16,0},{32,16},{48,32},{1,49},{17,1},{33,17},{49,33},{2,50}... | collective-permute-start | bytes 491528 | tf_op jit(solution)/shard_map/ppermute | solution.py:53
  154.2 5.8 %collective-permute-start.4 = (f32[16,640]{1,0:T(8,128)S(1)}, f32[16,640]{1,0:T(8,128)S(1)}, u32[]{:S(2)}, u32[]{:S(2)}) collective-permute-start(f32[16,640]{1,0:T(8,128)S(1)} %get-tuple-element.87), channel_id=1, source_target_pairs={{0,64},{64,128},{128,192},{192,0},{1,65},{65,129},{129,193},{193,1... | collective-permute-start | bytes 122888 | tf_op jit(solution)/shard_map/ppermute | solution.py:53
  155.5 5.5 %collective-permute-start.5 = (f32[16,640]{1,0:T(8,128)S(1)}, f32[16,640]{1,0:T(8,128)S(1)}, u32[]{:S(2)}, u32[]{:S(2)}) collective-permute-start(f32[16,640]{1,0:T(8,128)S(1)} %get-tuple-element.89), channel_id=1, source_target_pairs={{0,128},{64,192},{128,0},{192,64},{1,129},{65,193},{129,1},{193,65... | collective-permute-start | bytes 122888 | tf_op jit(solution)/shard_map/ppermute | solution.py:53
  158.3 4.0 %collective-permute-start.6 = (f32[16,640]{1,0:T(8,128)S(1)}, f32[16,640]{1,0:T(8,128)S(1)}, u32[]{:S(2)}, u32[]{:S(2)}) collective-permute-start(f32[16,640]{1,0:T(8,128)S(1)} %get-tuple-element.88), channel_id=1, source_target_pairs={{0,192},{64,0},{128,64},{192,128},{1,193},{65,1},{129,65},{193,129... | collective-permute-start | bytes 122888 | tf_op jit(solution)/shard_map/ppermute | solution.py:53
Sparse Core Ops, SparseCore 0:
  10.3 43.2 all-gather.1
  75.0 20.6 reduce-scatter.2
  99.6 43.8 reduce-scatter.4

commit v11 on v10

--- a/solution.py
+++ b/solution.py
@@ -138,10 +138,10 @@
         preferred_element_type=jnp.float32,
     )
     first_axis, second_axis, *rest = SCATTER_ORDER
-    packed = lax.psum_scatter(packed, first_axis, scatter_dimension=0, tiled=True)
+    packed = lax.psum_scatter(packed.astype(jnp.bfloat16), first_axis, scatter_dimension=0, tiled=True)
     vectors = lax.psum(vectors, first_axis)
     packed, vectors = lax.optimization_barrier((packed, vectors))
-    packed = lax.psum_scatter(packed.astype(jnp.bfloat16), second_axis, scatter_dimension=0, tiled=True)
+    packed = lax.psum_scatter(packed, second_axis, scatter_dimension=0, tiled=True)
     packed = packed.astype(jnp.float32)
     vectors = lax.psum(vectors, second_axis)
     block = conv_each + mix_each

time: 173 us -> 165 us (0.954)
  other arithmetic: 22.8 us -> 19 us
  waiting for transfers between devices: 61.2 us -> 59.1 us
    convert_element_type x1 -> x0, other arithmetic: 3.79 us -> none  [per_device(): packed.astype(jnp.bfloat16)]
    reduce_scatter x2, waiting for transfers between devices: 19.7 us -> 17.8 us  [the longest x1 14.7 us: per_device(): lax.psum_scatter(packed, second_axis, scatter_dimension=0, tiled=True)]
where the time goes in v11:
time: 165 us; the launch traced here: 164 us
  waiting for transfers between devices  59.1 us (36%)
  blocking collectives  33.2 us (20%)
  other arithmetic  19 us (12%)
  between operations  14.2 us (9%)
  local copies, waits for them, and re-layouts  13.6 us (8%)
  matrix products  12.7 us (8%)
  starting transfers between devices  12 us (7%)
    all_gather x1, waiting for transfers between devices, per_device(): lax.all_gather(lax.dynamic_slice_in_dim(both, core * half, half, axis=1),...  30.8 us
    psum x1, blocking collectives, per_device(): vectors = lax.psum(vectors, second_axis)  30.7 us
    reduce_scatter x1, waiting for transfers between devices, per_device(): lax.psum_scatter(packed, second_axis, scatter_dimension=0, tiled=True)  14.7 us
    ppermute x6, starting transfers between devices, permute_scatter(): lax.ppermute(chunk, axis, [(j, (j + step) % n) for j in range(n)])  11.7 us
    ppermute x6, waiting for transfers between devices, permute_scatter(): lax.ppermute(chunk, axis, [(j, (j + step) % n) for j in range(n)])  5.9 us
    ppermute x1, waiting for transfers between devices, per_device(): other = lax.ppermute(own, 'c', [(0, 1), (1, 0)])  4.49 us
    dot_general x1, matrix products, per_device(): lax.dot_general(jnp.concatenate([conv_lhs, mix_lhs], axis=0), jnp.concate...  4.39 us
    unnamed x17, local copies, waits for them, and re-layouts  4.23 us
  transfers between devices with their start and end apart: 10, of which 9 were waited for; matrix products, arithmetic and copies ran while one was open for 14% of the time, Pallas kernels for 0%

profile of v11, /device:TPU:32, one launch (start us, length us, event | category | flops | bytes accessed | tf_op | source)
XLA Modules:
  0.0 163.8 jit_solution(2630460605486601233)
XLA Ops:
  7.2 1.7 %fusion.19 = bf16[512,256]{1,0:T(8,128)(2,1)} fusion(s32[]{:T(128)S(6)} %select_n.127, bf16[448,512]{1,0:T(8,128)(2,1)} %param.13, bf16[64,512]{1,0:T(8,128)(2,1)} %param.14), kind=kLoop, calls=%fused_computation.55 | loop fusion | flops 524288 | bytes 786436 | tf_op jit(solution)/shard_map/concatenate | solution.py:64
  10.2 2.8 %fusion.10 = bf16[256,512]{1,0:T(8,128)(2,1)S(1)} fusion(bf16[256,512]{1,0:T(8,128)(2,1)} %param.10, f32[512]{0:T(512)} %param.16), kind=kLoop, calls=%fused_computation.31 | loop fusion | flops 786432 | bytes 526336 | tf_op jit(solution)/shard_map/convert_element_type | solution.py:70
  13.9 1.8 %constant_dynamic-update-slice_fusion = bf16[256,3584]{1,0:T(8,128)(2,1)S(1)} fusion(bf16[256,3584]{1,0:T(8,128)(2,1)S(1)} %select_dynamic-update-slice_fusion.3, f32[512]{0:T(512)S(1)} %copy-done.5, bf16[256,512]{1,0:T(8,128)(2,1)S(1)} %copy-done.1), kind=kLoop, calls=%fused_computation.72 | loop fusion | flops 786432 | bytes 526336
  17.4 2.3 %copy.34 = bf16[256,3584]{0,1:T(8,128)(2,1)} copy(bf16[256,3584]{1,0:T(8,128)(2,1)S(1)} %select_dynamic-update-slice_fusion) | data formatting | bytes 3670016 | tf_op jit(solution)/shard_map/concatenate | solution.py:78
  19.7 2.5 %reshape.128 = bf16[256,256,14]{0,2,1:T(8,128)(2,1)S(1)} reshape(bf16[256,3584]{0,1:T(8,128)(2,1)} %copy.34) | data formatting | bytes 3670016 | tf_op jit(solution)/shard_map/reshape | solution.py:91
  22.8 30.8 %all-gather.2.cloned.1.call-done = bf16[4096,256]{1,0:T(8,128)(2,1)} async-done(((bf16[512,256]{1,0:T(8,128)(2,1)}), bf16[4096,256]{1,0:T(8,128)(2,1)}) %all-gather.2.cloned.1.call-update) | async-done | bytes 2097168 | tf_op jit(solution)/shard_map/all_gather | solution.py:67
  53.6 4.5 %collective-permute-done = bf16[4096,256]{1,0:T(8,128)(2,1)} collective-permute-done((bf16[4096,256]{1,0:T(8,128)(2,1)}, bf16[4096,256]{1,0:T(8,128)(2,1)}, u32[]{:S(2)}, u32[]{:S(2)}) %collective-permute-start) | collective-permute-done | bytes 2097184 | tf_op jit(solution)/shard_map/ppermute | solution.py:93
  58.1 2.5 %broadcast_select_fusion.1 = (bf16[4096,256]{1,0:T(8,128)(2,1)S(1)}, bf16[4096,256]{1,0:T(8,128)(2,1)S(1)}) fusion(bf16[4096,256]{1,0:T(8,128)(2,1)} %all-gather.2.cloned.1.call-done, bf16[4096,256]{1,0:T(8,128)(2,1)} %collective-permute-done, pred[]{:T(512)S(6)} %eq.30), kind=kLoop, calls=%fused_computation.7 | loop fusion | flops 2097152 | bytes 8388609 | tf_op jit(solution)/shard_map/jit(_where)/select_n | solution.py:94
  61.2 1.8 %copy-done.3 = bf16[256,3584]{1,0:T(8,128)(2,1)S(1)} copy-done((bf16[256,3584]{1,0:T(8,128)(2,1)S(1)}, bf16[256,3584]{1,0:T(8,128)(2,1)}, u32[]{:S(2)}) %copy-start.3) | copy-done | bytes 1835032
  64.2 4.1 %convert_reduce_fusion.1 = (f32[512]{0:T(512)S(1)}, bf16[256,512]{1,0:T(8,128)(2,1)S(1)}, f32[512]{0:T(512)S(1)}, bf16[256,512]{1,0:T(8,128)(2,1)S(1)}) fusion(f32[256,512]{1,0:T(8,128)S(1)} %convolution_add_fusion, f32[512]{0:T(512)S(1)} %get-tuple-element.90, f32[512]{0:T(512)S(1)} %get-tuple-element.91, f32[512]{0:T(512)S(1)} %copy-done.6, ...), kind=kOutput, calls=%fused_computation.42 | convolution fusion | flops 136444928 | bytes 1845248 | tf_op jit(solution)/shard_map/dot_general | solution.py:108
  69.3 4.4 %convolution_convert_fusion = bf16[4096,512]{1,0:T(8,128)(2,1)} fusion(bf16[256,4096]{0,1:T(8,128)(2,1)S(1)} %bitcast.52, bf16[256,4096]{0,1:T(8,128)(2,1)S(1)} %bitcast.51, bf16[256,512]{1,0:T(8,128)(2,1)S(1)} %copy-done.4, bf16[256,512]{1,0:T(8,128)(2,1)S(1)} %get-tuple-element.63), kind=kOutput, calls=%fused_computation | convolution fusion | flops 2159017984 | bytes 8912896 | tf_op jit(solution)/shard_map/dot_general | solution.py:134
  74.2 3.2 %convolution_convert_fusion.1 = bf16[256,3584]{1,0:T(8,128)(2,1)S(1)} fusion(bf16[256,512]{1,0:T(8,128)(2,1)S(1)} %get-tuple-element.63, bf16[3584,512]{1,0:T(8,128)(2,1)} %bitcast.48), kind=kOutput, calls=%fused_computation.1 | convolution fusion | flops 940441600 | bytes 5767168 | tf_op jit(solution)/shard_map/dot_general | solution.py:112
  78.1 3.9 %fusion.18 = (f32[512]{0:T(512)S(1)}, f32[256,512]{1,0:T(8,128)S(1)}) fusion(bf16[256,512]{1,0:T(8,128)(2,1)S(1)} %copy-done.1, f32[512]{0:T(512)S(1)} %get-tuple-element.93, f32[512]{0:T(512)S(1)} %get-tuple-element.92, f32[512]{0:T(512)S(1)} %copy-done.5, f32[229,512]{1,0:T(8,128)S(1)} %get-tuple-element.110, f32[238,512]{1,0:T(8,128)S(1)} %get-tuple-element.108, ...), kind=kLoop, calls=%fused_computation.48 | loop fusion | flops 2227712 | bytes 3981312 | tf_op jit(solution)/shard_map/reduce_sum | solution.py:129
  81.9 2.5 %convert_reduce_fusion = (f32[512]{0:T(512)S(1)}, bf16[256,512]{1,0:T(8,128)(2,1)}) fusion(bf16[256,512]{1,0:T(8,128)(2,1)S(1)} %copy-done.4, f32[256,512]{1,0:T(8,128)S(1)} %get-tuple-element.65, bf16[256,512]{1,0:T(8,128)(2,1)S(1)} %copy-done.1, f32[512]{0:T(512)S(1)} %get-tuple-element.92), kind=kLoop, calls=%fused_computation.22 | loop fusion | flops 1048064 | bytes 1314816 | tf_op jit(solution)/shard_map/reduce_sum | solution.py:128
  84.5 2.5 %psum.14 = f32[4,512]{1,0:T(4,128)S(1)} all-reduce(f32[4,512]{1,0:T(4,128)S(1)} %pad_maximum_fusion.1), channel_id=1, replica_groups=mesh['x'=4,'y'=4,'c'=2,'z'=8] {'c'}, use_global_device_ids=true, to_apply=%region_7.8 | all-reduce | flops 2048 | bytes 16384 | tf_op jit(solution)/shard_map/psum | solution.py:142
  87.0 3.2 %reduce-scatter.3.cloned.1.call-done = bf16[2048,512]{1,0:T(8,128)(2,1)} async-done(((bf16[4096,512]{1,0:T(8,128)(2,1)}), bf16[2048,512]{1,0:T(8,128)(2,1)}) %reduce-scatter.3.cloned.1.call-update) | async-done | bytes 2097168 | tf_op jit(solution)/shard_map/reduce_scatter | solution.py:141
  90.8 30.7 %psum.15 = f32[4,4,2,8,8]{3,2,1,0,4:T(2,128)S(1)} all-reduce(f32[4,4,2,8,8]{3,2,1,0,4:T(2,128)S(1)} %reshape.138), channel_id=1, replica_groups=mesh['x'=4,'y'=4,'c'=2,'z'=8] {'z'}, use_global_device_ids=true, to_apply=%region_9.10 | all-reduce | flops 2048 | bytes 16384 | tf_op jit(solution)/shard_map/psum | solution.py:146
  121.8 14.7 %reduce-scatter.5.cloned.1.call-done = bf16[256,512]{1,0:T(8,128)(2,1)} async-done(((bf16[2048,512]{1,0:T(8,128)(2,1)}), bf16[256,512]{1,0:T(8,128)(2,1)}) %reduce-scatter.5.cloned.1.call-update) | async-done | bytes 262160 | tf_op jit(solution)/shard_map/reduce_scatter | solution.py:144
  137.6 1.7 %collective-permute-start.1 = (f32[64,640]{1,0:T(8,128)S(1)}, f32[64,640]{1,0:T(8,128)S(1)}, u32[]{:S(2)}, u32[]{:S(2)}) collective-permute-start(f32[64,640]{1,0:T(8,128)S(1)} %get-tuple-element.75), channel_id=1, source_target_pairs={{0,16},{16,32},{32,48},{48,0},{1,17},{17,33},{33,49},{49,1},{2,18}... | collective-permute-start | bytes 491528 | tf_op jit(solution)/shard_map/ppermute | solution.py:53
  139.3 2.3 %collective-permute-start.2 = (f32[64,640]{1,0:T(8,128)S(1)}, f32[64,640]{1,0:T(8,128)S(1)}, u32[]{:S(2)}, u32[]{:S(2)}) collective-permute-start(f32[64,640]{1,0:T(8,128)S(1)} %get-tuple-element.76), channel_id=1, source_target_pairs={{0,32},{16,48},{32,0},{48,16},{1,33},{17,49},{33,1},{49,17},{2,34}... | collective-permute-start | bytes 491528 | tf_op jit(solution)/shard_map/ppermute | solution.py:53
  141.6 1.9 %collective-permute-start.3 = (f32[64,640]{1,0:T(8,128)S(1)}, f32[64,640]{1,0:T(8,128)S(1)}, u32[]{:S(2)}, u32[]{:S(2)}) collective-permute-start(f32[64,640]{1,0:T(8,128)S(1)} %get-tuple-element.77), channel_id=1, source_target_pairs={{0,48},{16,0},{32,16},{48,32},{1,49},{17,1},{33,17},{49,33},{2,50}... | collective-permute-start | bytes 491528 | tf_op jit(solution)/shard_map/ppermute | solution.py:53
  144.2 2.5 %collective-permute-done.2 = f32[64,640]{1,0:T(8,128)S(1)} collective-permute-done((f32[64,640]{1,0:T(8,128)S(1)}, f32[64,640]{1,0:T(8,128)S(1)}, u32[]{:S(2)}, u32[]{:S(2)}) %collective-permute-start.2) | collective-permute-done | bytes 163872 | tf_op jit(solution)/shard_map/ppermute | solution.py:53
  147.0 1.9 %collective-permute-start.4 = (f32[16,640]{1,0:T(8,128)S(1)}, f32[16,640]{1,0:T(8,128)S(1)}, u32[]{:S(2)}, u32[]{:S(2)}) collective-permute-start(f32[16,640]{1,0:T(8,128)S(1)} %get-tuple-element.87), channel_id=1, source_target_pairs={{0,64},{64,128},{128,192},{192,0},{1,65},{65,129},{129,193},{193,1... | collective-permute-start | bytes 122888 | tf_op jit(solution)/shard_map/ppermute | solution.py:53
  148.9 2.4 %collective-permute-start.5 = (f32[16,640]{1,0:T(8,128)S(1)}, f32[16,640]{1,0:T(8,128)S(1)}, u32[]{:S(2)}, u32[]{:S(2)}) collective-permute-start(f32[16,640]{1,0:T(8,128)S(1)} %get-tuple-element.89), channel_id=1, source_target_pairs={{0,128},{64,192},{128,0},{192,64},{1,129},{65,193},{129,1},{193,65... | collective-permute-start | bytes 122888 | tf_op jit(solution)/shard_map/ppermute | solution.py:53
  (79 shorter events, 17.2 us)
Async XLA Ops:
  7.2 46.4 %all-gather.2.cloned.1.call-start = ((), (), s32[]{:S(2)}) async-start(), calls=%async_computation.2 | async-start | bytes 2359296 | tf_op jit(solution)/shard_map/all_gather | solution.py:67
  8.9 81.2 %reduce-scatter.3.cloned.1.call-start = ((), (), s32[]{:S(2)}) async-start(), calls=%async_computation.3 | async-start | bytes 6291456 | tf_op jit(solution)/shard_map/reduce_scatter | solution.py:141
  12.9 1.0 copy-start.1
  12.9 0.9 copy-start.5
  16.1 1.3 copy-start.2
  22.5 31.1 %copy-start.6 = (f32[512]{0:T(512)S(1)}, f32[512]{0:T(512)}, u32[]{:S(2)}) copy-start(f32[512]{0:T(512)} %param.17) | copy-start | bytes 6148
  53.6 4.5 %collective-permute-start = (bf16[4096,256]{1,0:T(8,128)(2,1)}, bf16[4096,256]{1,0:T(8,128)(2,1)}, u32[]{:S(2)}, u32[]{:S(2)}) collective-permute-start(bf16[4096,256]{1,0:T(8,128)(2,1)} %all-gather.2.cloned.1.call-done), channel_id=1, source_target_pairs={{0,8},{8,0},{1,9},{9,1},{2,10},{10,2},{3,11},{11,3},{4,12},{12,4},... | collective-permute-start | bytes 6291464 | tf_op jit(solution)/shard_map/ppermute | solution.py:93
  60.9 2.2 %copy-start.3 = (bf16[256,3584]{1,0:T(8,128)(2,1)S(1)}, bf16[256,3584]{1,0:T(8,128)(2,1)}, u32[]{:S(2)}) copy-start(bf16[256,3584]{1,0:T(8,128)(2,1)} %copy-done.2) | copy-start | bytes 5505028
  60.9 2.2 %copy-start.7 = (f32[512]{0:T(512)S(1)}, f32[512]{0:T(512)}, u32[]{:S(2)}) copy-start(f32[512]{0:T(512)} %param.15) | copy-start | bytes 6148
  61.2 3.0 %copy-start = (bf16[8,448,512]{2,1,0:T(8,128)(2,1)}, bf16[8,448,512]{2,1,0:T(8,128)(2,1)S(1)}, u32[]{:S(2)}) copy-start(bf16[8,448,512]{2,1,0:T(8,128)(2,1)S(1)} %slice.174) | copy-start | bytes 11010052
  63.1 1.1 copy-start.4
  73.7 62.8 %reduce-scatter.5.cloned.1.call-start = ((), (), s32[]{:S(2)}) async-start(), calls=%async_computation.4 | async-start | bytes 2359296 | tf_op jit(solution)/shard_map/reduce_scatter | solution.py:144
  137.6 6.6 %collective-permute-start.1 = (f32[64,640]{1,0:T(8,128)S(1)}, f32[64,640]{1,0:T(8,128)S(1)}, u32[]{:S(2)}, u32[]{:S(2)}) collective-permute-start(f32[64,640]{1,0:T(8,128)S(1)} %get-tuple-element.75), channel_id=1, source_target_pairs={{0,16},{16,32},{32,48},{48,0},{1,17},{17,33},{33,49},{49,1},{2,18}... | collective-permute-start | bytes 491528 | tf_op jit(solution)/shard_map/ppermute | solution.py:53
  139.3 7.4 %collective-permute-start.2 = (f32[64,640]{1,0:T(8,128)S(1)}, f32[64,640]{1,0:T(8,128)S(1)}, u32[]{:S(2)}, u32[]{:S(2)}) collective-permute-start(f32[64,640]{1,0:T(8,128)S(1)} %get-tuple-element.76), channel_id=1, source_target_pairs={{0,32},{16,48},{32,0},{48,16},{1,33},{17,49},{33,1},{49,17},{2,34}... | collective-permute-start | bytes 491528 | tf_op jit(solution)/shard_map/ppermute | solution.py:53
  141.6 5.3 %collective-permute-start.3 = (f32[64,640]{1,0:T(8,128)S(1)}, f32[64,640]{1,0:T(8,128)S(1)}, u32[]{:S(2)}, u32[]{:S(2)}) collective-permute-start(f32[64,640]{1,0:T(8,128)S(1)} %get-tuple-element.77), channel_id=1, source_target_pairs={{0,48},{16,0},{32,16},{48,32},{1,49},{17,1},{33,17},{49,33},{2,50}... | collective-permute-start | bytes 491528 | tf_op jit(solution)/shard_map/ppermute | solution.py:53
  147.0 5.8 %collective-permute-start.4 = (f32[16,640]{1,0:T(8,128)S(1)}, f32[16,640]{1,0:T(8,128)S(1)}, u32[]{:S(2)}, u32[]{:S(2)}) collective-permute-start(f32[16,640]{1,0:T(8,128)S(1)} %get-tuple-element.87), channel_id=1, source_target_pairs={{0,64},{64,128},{128,192},{192,0},{1,65},{65,129},{129,193},{193,1... | collective-permute-start | bytes 122888 | tf_op jit(solution)/shard_map/ppermute | solution.py:53
  148.9 5.5 %collective-permute-start.5 = (f32[16,640]{1,0:T(8,128)S(1)}, f32[16,640]{1,0:T(8,128)S(1)}, u32[]{:S(2)}, u32[]{:S(2)}) collective-permute-start(f32[16,640]{1,0:T(8,128)S(1)} %get-tuple-element.89), channel_id=1, source_target_pairs={{0,128},{64,192},{128,0},{192,64},{1,129},{65,193},{129,1},{193,65... | collective-permute-start | bytes 122888 | tf_op jit(solution)/shard_map/ppermute | solution.py:53
  151.2 4.0 %collective-permute-start.6 = (f32[16,640]{1,0:T(8,128)S(1)}, f32[16,640]{1,0:T(8,128)S(1)}, u32[]{:S(2)}, u32[]{:S(2)}) collective-permute-start(f32[16,640]{1,0:T(8,128)S(1)} %get-tuple-element.88), channel_id=1, source_target_pairs={{0,192},{64,0},{128,64},{192,128},{1,193},{65,1},{129,65},{193,129... | collective-permute-start | bytes 122888 | tf_op jit(solution)/shard_map/ppermute | solution.py:53
Sparse Core Ops, SparseCore 0:
  10.3 43.2 all-gather.1
  73.8 16.2 reduce-scatter.2
  92.7 43.7 reduce-scatter.4
